TPU v7x, 128 devices: a whole 4x4x4 slice. The times are simulated.
128 devices in a mesh: occ: 16 (over z, x_lo, core), aux: 8 (over y, x_hi).
Axes of the slice: x: 4 (x_hi: 2, x_lo: 2; x = x_hi * 2 + x_lo), y: 4, z: 4, core: 2. Of those that a mesh axis runs over, the one named last changes fastest.
Arguments:
- integrals: bfloat16 [11264, 16, 2176], P(('occ', 'aux')), may hold values from -0.5 to 0.5
- owner_order: int32 [16], replicated, may hold values from 0 to 15, each once
- occ_energy: float32 [16], replicated, may hold values from -1.5 to -0.3
- vir_energy: float32 [2176], replicated, may hold values from 0.03 to 30
Outputs:
- pair_rows: float32 [16, 1, 2176], P('occ', None, 'aux')
- pair_energy: float32 [16, 1], P('occ')
Inputs may be any that keep to these rules, and one draw needn't show every extreme that they name: owner_order holds each of 0 to 15 once; only its first 1 entries are used.
All inputs are finite; a program needn't handle non-finite values.
Results may differ from a plain program's by a relative error of at most 0.0003.
Values may be sent and summed in bfloat16 or wider, within the bound.
No kernel may reach another device: no remote copies, remote signals or barrier semaphores. Data moves between devices by JAX's collectives and lax.ppermute only.
A program may use at most 128 MiB of HBM per device.

v0:
```python
import jax
import jax.numpy as jnp
from jax import lax
from jax.sharding import PartitionSpec as P


def split_up(array, dim, peers):
    lengths = array.shape
    tiles = array.reshape(*lengths[:dim], peers, lengths[dim] // peers, *lengths[dim + 1 :])
    return jnp.moveaxis(tiles, dim, 0)


def cut_rows(length, count):
    unit = 8 if length >= 8 * count else 1
    return [length // unit * k // count * unit for k in range(1, count)]


def joined_along(tiles, dim):
    lengths = list(tiles.shape[1:])
    lengths[dim] *= tiles.shape[0]
    return jnp.moveaxis(tiles, 0, dim).reshape(lengths)


def cut_exchange(array, axis, pieces, split_dim, concat_dim):
    tiles = split_up(array, split_dim, lax.axis_size(axis))
    widest = max(range(1, max(2, tiles.ndim - 1)), key=lambda d: tiles.shape[d])
    outs = []
    for slab in jnp.split(tiles, cut_rows(tiles.shape[widest], pieces), axis=widest):
        if slab.size:
            outs.append(lax.all_to_all(slab, axis, split_axis=0, concat_axis=0, tiled=True))
    return joined_along(jnp.concatenate(outs, axis=widest), concat_dim)


def sent_to_all(array, axis):
    copies = jnp.broadcast_to(array, (lax.axis_size(axis), *array.shape))
    return lax.all_to_all(copies, axis, split_axis=0, concat_axis=0, tiled=True)


def over_copies(array, axis):
    return sent_to_all(array, axis).sum(axis=0)


def per_device(integrals, owner_order, occ_energy, vir_energy):
    own_block = cut_exchange(integrals, "occ", 2, 1, 0)[:, 0, :]
    nvirtual = vir_energy.shape[0]
    vir_rows = nvirtual // lax.axis_size("aux")
    row_offset = lax.axis_index("aux") * vir_rows
    near_energy = lax.dynamic_slice_in_dim(vir_energy, row_offset, vir_rows)
    own_energy = lax.dynamic_index_in_dim(occ_energy, lax.axis_index("occ"), 0, keepdims=False)
    owner = owner_order[0]
    owner_energy = lax.dynamic_index_in_dim(occ_energy, owner, 0, keepdims=False)
    owner_column = lax.dynamic_index_in_dim(integrals, owner, 1, keepdims=False)
    owner_panel = lax.all_gather(owner_column, "occ", axis=0, tiled=True)
    partial_sum = lax.dot_general(
        own_block, owner_panel, (((0,), (0,)), ((), ())), preferred_element_type=jnp.float32
    )
    summed = lax.psum_scatter(partial_sum, "aux", scatter_dimension=0, tiled=True)
    denominator = own_energy + owner_energy - near_energy[:, None] - vir_energy[None, :]
    outputs = [jnp.sum(summed * summed / denominator, axis=1)]
    pair_rows = jnp.stack(outputs, axis=0)[None]
    totals = over_copies(jnp.sum(pair_rows, axis=2), "aux")
    return (pair_rows, totals)


def solution(mesh):
    in_specs = (P(("occ", "aux"), None, None), P(), P(), P())
    out_specs = (P("occ", None, "aux"), P("occ", None))
    return jax.shard_map(
        per_device, mesh=mesh, in_specs=in_specs, out_specs=out_specs, check_vma=False
    )
```

profile of v0, /device:TPU:12, one launch (start us, length us, event | category | flops | bytes accessed | tf_op | source)
XLA Modules:
  0.0 409.7 jit_solution(13848321706207867697)
XLA Ops:
  7.2 0.0 all-gather.3.cloned.1.call-start
  8.5 0.0 copy-start.2
  8.5 6.5 %copy.24 = bf16[88,16,2176]{2,0,1:T(8,128)(2,1)} copy(bf16[88,16,2176]{2,1,0:T(8,128)(2,1)} %param.4) | data formatting | bytes 12255232 | tf_op args[0]
  15.0 0.0 copy-done.2
  15.1 1.8 constant_dynamic-slice_fusion
  16.8 0.0 all-gather.3.cloned.1.call-update
  16.8 3.6 split.8
  20.4 6.1 %all-to-all-start = ((bf16[16,40,1,2176]{3,1,2,0:T(8,128)(2,1)}), bf16[16,40,1,2176]{3,1,2,0:T(8,128)(2,1)}, u32[]{:S(2)}, u32[]{:S(2)}) async-start(bf16[16,40,1,2176]{3,1,2,0:T(8,128)(2,1)} %split.8), calls=%async_computation | async-start | bytes 5570560 | tf_op jit(solution)/shard_map/all_to_all | solution.py:30
  26.5 0.0 reduce-scatter.2.cloned.1.call-start
  26.6 2.2 split.9
  28.8 56.2 %all-to-all-done = bf16[16,40,1,2176]{3,1,2,0:T(8,128)(2,1)} async-done(((bf16[16,40,1,2176]{3,1,2,0:T(8,128)(2,1)}), bf16[16,40,1,2176]{3,1,2,0:T(8,128)(2,1)}, u32[]{:S(2)}, u32[]{:S(2)}) %all-to-all-start) | async-done | bytes 2785312 | tf_op jit(solution)/shard_map/all_to_all | solution.py:30
  85.0 43.6 %all_to_all.15 = bf16[16,48,1,2176]{3,1,2,0:T(8,128)(2,1)S(1)} all-to-all(bf16[16,48,1,2176]{3,1,2,0:T(8,128)(2,1)S(1)} %split.9), channel_id=1, replica_groups=mesh['occ'=16,'aux'=8] {'occ'}, dimensions={0} | all-to-all | bytes 6684672 | tf_op jit(solution)/shard_map/all_to_all | solution.py:30
  128.6 4.9 %pad_maximum_fusion = bf16[16,88,1,2176]{3,1,0,2:T(8,128)(2,1)} fusion(bf16[16,48,1,2176]{3,1,0,2:T(8,128)(2,1)S(1)} %bitcast.17, bf16[16,40,1,2176]{3,1,0,2:T(8,128)(2,1)} %bitcast.2), kind=kLoop, calls=%fused_computation | loop fusion | flops 12255232 | bytes 12255232 | tf_op jit(solution)/shard_map/concatenate | solution.py:31
  133.5 0.0 all-gather.3.cloned.1.call-done
  133.5 22.3 %fusion = f32[2176,2176]{1,0:T(8,128)} fusion(bf16[1408,2176]{1,0:T(8,128)(2,1)} %bitcast.18, bf16[1408,1,2176]{2,0,1:T(8,128)(2,1)} %all-gather.3.cloned.1.call-done), kind=kOutput, calls=%fused_computation.1 | convolution fusion | flops 13333692416 | bytes 31195136 | tf_op jit(solution)/shard_map/dot_general | solution.py:54
  155.7 0.0 copy-start.1
  155.7 0.0 copy-start
  155.7 0.0 reduce-scatter.2.cloned.1.call-update
  155.8 0.6 copy-done.1
  156.4 0.6 fusion.5
  158.3 0.0 copy-done
  158.3 0.1 dynamic-slice_subtract_fusion
  158.4 227.7 %reduce-scatter.2.cloned.1.call-done = f32[272,2176]{1,0:T(8,128)} async-done(((f32[2176,2176]{1,0:T(8,128)}), f32[272,2176]{1,0:T(8,128)}) %reduce-scatter.2.cloned.1.call-update) | async-done | bytes 2367504 | tf_op jit(solution)/shard_map/reduce_scatter | solution.py:57
  386.0 3.3 fusion.2
  389.4 0.6 broadcast_in_dim_stack.3
  389.9 0.6 broadcast_in_dim.2
  390.6 11.6 %all_to_all.16 = f32[8,1,1]{2,1,0:T(1,128)S(1)} all-to-all(f32[8,1,1]{2,1,0:T(1,128)S(1)} %broadcast_in_dim.2), channel_id=1, replica_groups=mesh['occ'=16,'aux'=8] {'aux'}, dimensions={0} | all-to-all | bytes 64 | tf_op jit(solution)/shard_map/all_to_all | solution.py:36
  402.2 0.6 reduce_sum.31
Async XLA Ops:
  7.2 126.3 %all-gather.3.cloned.1.call-start = ((), (), s32[]{:S(2)}) async-start(), calls=%async_computation.5 | async-start | bytes 6510592 | tf_op jit(solution)/shard_map/all_gather | solution.py:53
  8.5 6.5 %copy-start.2 = (s32[16]{0:T(128)S(1)}, s32[16]{0:T(128)}, u32[]{:S(2)}) copy-start(s32[16]{0:T(128)} %param.5) | copy-start | bytes 196
  20.4 64.6 %all-to-all-start = ((bf16[16,40,1,2176]{3,1,2,0:T(8,128)(2,1)}), bf16[16,40,1,2176]{3,1,2,0:T(8,128)(2,1)}, u32[]{:S(2)}, u32[]{:S(2)}) async-start(bf16[16,40,1,2176]{3,1,2,0:T(8,128)(2,1)} %split.8), calls=%async_computation | async-start | bytes 5570560 | tf_op jit(solution)/shard_map/all_to_all | solution.py:30
  26.5 359.5 %reduce-scatter.2.cloned.1.call-start = ((), (), s32[]{:S(2)}) async-start(), calls=%async_computation.4 | async-start | bytes 21307392 | tf_op jit(solution)/shard_map/reduce_scatter | solution.py:57
  155.7 0.7 copy-start.1
  155.7 2.5 copy-start
Sparse Core Ops, SparseCore 0:
  17.0 73.6 all-gather.2
  155.9 230.0 reduce-scatter.1
where the time goes:
time: 414 us; the launch traced here: 410 us
  waiting for transfers between devices  284 us (69%)
  blocking collectives  55.2 us (13%)
  matrix products  22.3 us (5%)
  between operations  16.7 us (4%)
  local copies, waits for them, and re-layouts  16.4 us (4%)
  other arithmetic  8.92 us (2%)
  starting transfers between devices  6.18 us (1%)
    reduce_scatter x1, waiting for transfers between devices, per_device(): lax.psum_scatter(partial_sum, 'aux', scatter_dimension=0, tiled=True)  228 us
    all_to_all x1, waiting for transfers between devices, cut_exchange(): lax.all_to_all(slab, axis, split_axis=0, concat_axis=0, tiled=True)  56.2 us
    all_to_all x1, blocking collectives, cut_exchange(): lax.all_to_all(slab, axis, split_axis=0, concat_axis=0, tiled=True)  43.6 us
    dot_general x1, matrix products, per_device(): lax.dot_general(own_block, owner_panel, (((0,), (0,)), ((), ())), preferr...  22.3 us
    all_to_all x1, blocking collectives, sent_to_all(): return lax.all_to_all(copies, axis, split_axis=0, concat_axis=0, tiled=True)  11.6 us
  transfers between devices with their start and end apart: 3, of which 2 were waited for; matrix products, arithmetic and copies ran while one was open for 3% of the time, Pallas kernels for 0%

commit v1 on v0

v1 whole, which is shorter than its diff:
```python
import jax
import jax.numpy as jnp
from jax import lax
from jax.sharding import Mesh, PartitionSpec as P

GROUP = ("oz", "core", "xh")


def per_device(integrals, owner_order, occ_energy, vir_energy):
    nq, nocc, nvir = integrals.shape
    ny, nh, nc = lax.axis_size("y"), lax.axis_size("xh"), lax.axis_size("core")
    noz = lax.axis_size("oz")
    blk = nvir // (ny * nh)
    y, h, c = lax.axis_index("y"), lax.axis_index("xh"), lax.axis_index("core")
    orbital = lax.axis_index("oz") * nc + c

    tiles = integrals.reshape(nq, nocc, ny, nh, blk)
    tiles = jnp.transpose(tiles, (1, 3, 0, 2, 4)).reshape(nocc * nh, nq, ny * blk)
    left = lax.all_to_all(tiles, GROUP, 0, 0, tiled=True)
    left = left.reshape(noz, nc, nh, nq, ny * blk)

    owner = owner_order[0]
    column = lax.dynamic_index_in_dim(integrals, owner, 1, keepdims=False)
    chip_rows = lax.all_gather(column, "core", axis=0, tiled=False)
    half = nvir // nc
    mine = lax.dynamic_slice_in_dim(chip_rows, c * half, half, axis=2)
    panel = lax.all_gather(mine, ("oz", "xh"), axis=0, tiled=False)
    panel = panel.reshape(noz, nh, nc, nq, half)
    panel = lax.all_gather(panel, "core", axis=0, tiled=False)

    partial_sum = lax.dot_general(
        left, panel, (((0, 1, 2, 3), (1, 3, 2, 4)), ((), ())), preferred_element_type=jnp.float32
    ).reshape(ny * blk, nvir)
    summed = lax.psum_scatter(partial_sum, "y", scatter_dimension=0, tiled=True)

    near_energy = lax.dynamic_slice_in_dim(vir_energy, (y * nh + h) * blk, blk)
    own_energy = lax.dynamic_index_in_dim(occ_energy, orbital, 0, keepdims=False)
    owner_energy = lax.dynamic_index_in_dim(occ_energy, owner, 0, keepdims=False)
    denominator = own_energy + owner_energy - near_energy[:, None] - vir_energy[None, :]
    rows = jnp.sum(summed * summed / denominator, axis=1)
    pair_rows = rows.reshape(1, 1, blk)
    totals = lax.psum(jnp.sum(rows), ("y", "xh")).reshape(1, 1)
    return pair_rows, totals


def solution(mesh):
    nocc, naux = mesh.shape["occ"], mesh.shape["aux"]
    cores, ys = 2, naux // 2
    fine = Mesh(mesh.devices.reshape(nocc // cores, cores, ys, naux // ys), ("oz", "core", "y", "xh"))
    in_specs = (P(("oz", "core", "y", "xh"), None, None), P(), P(), P())
    out_specs = (P(("oz", "core"), None, ("y", "xh")), P(("oz", "core"), None))
    return jax.shard_map(
        per_device, mesh=fine, in_specs=in_specs, out_specs=out_specs, check_vma=False
    )
```

time: 414 us -> 452 us (1.092)
  local copies, waits for them, and re-layouts: 16.4 us -> 68.5 us
  waiting for transfers between devices: 284 us -> 233 us
  blocking collectives: 55.2 us -> 102 us
  other arithmetic: 8.92 us -> 1.9 us
  starting transfers between devices: 6.18 us -> 0.12 us
    reduce_scatter x1 -> x0, waiting for transfers between devices: 228 us -> none  [per_device(): lax.psum_scatter(partial_sum, 'aux', scatter_dimension=0, tiled=True)]
    all_gather x1 -> x2, waiting for transfers between devices: 0.01 us -> 148 us  [the longest x1 148 us: per_device(): panel = lax.all_gather(mine, ('oz', 'xh'), axis=0, tiled=False)]
    unnamed x2 -> x4, waiting for transfers between devices: 0.03 us -> 85.4 us
    all_to_all x1 -> x0, waiting for transfers between devices: 56.2 us -> none  [cut_exchange(): lax.all_to_all(slab, axis, split_axis=0, concat_axis=0, tiled=True)]
    reshape x0 -> x3, local copies, waits for them, and re-layouts: none -> 40.2 us  [the longest x1 25.6 us: per_device(): tiles = integrals.reshape(nq, nocc, ny, nh, blk)]
    all_to_all x2 -> x1, blocking collectives: 55.2 us -> 80.6 us  [per_device(): left = lax.all_to_all(tiles, GROUP, 0, 0, tiled=True)]
    psum x0 -> x1, blocking collectives: none -> 19.2 us  [per_device(): totals = lax.psum(jnp.sum(rows), ('y', 'xh')).reshape(1, 1)]
    unnamed x7, local copies, waits for them, and re-layouts: 7.13 us -> 15.6 us
  transfers between devices with their start and end apart: 3 -> 3, of which waited for: 2 -> 2; matrix products, arithmetic and copies ran while one was open for 3% -> 11% of each run, Pallas kernels for 0% -> 0%
where the time goes in v1:
time: 452 us; the launch traced here: 446 us
  waiting for transfers between devices  233 us (52%)
  blocking collectives  102 us (23%)
  local copies, waits for them, and re-layouts  68.5 us (15%)
  matrix products  23.3 us (5%)
  between operations  17 us (4%)
    all_gather x1, waiting for transfers between devices, per_device(): panel = lax.all_gather(mine, ('oz', 'xh'), axis=0, tiled=False)  148 us
    unnamed x4, waiting for transfers between devices  85.4 us
    all_to_all x1, blocking collectives, per_device(): left = lax.all_to_all(tiles, GROUP, 0, 0, tiled=True)  80.6 us
    reshape x1, local copies, waits for them, and re-layouts, per_device(): tiles = integrals.reshape(nq, nocc, ny, nh, blk)  25.6 us
    dot_general x1, matrix products, per_device(): lax.dot_general(left, panel, (((0, 1, 2, 3), (1, 3, 2, 4)), ((), ())), pr...  23.3 us
    psum x1, blocking collectives, per_device(): totals = lax.psum(jnp.sum(rows), ('y', 'xh')).reshape(1, 1)  19.2 us
    unnamed x7, local copies, waits for them, and re-layouts  15.6 us
    reshape x1, local copies, waits for them, and re-layouts, per_device(): jnp.transpose(tiles, (1, 3, 0, 2, 4)).reshape(nocc * nh, nq, ny * blk)  14.1 us
  transfers between devices with their start and end apart: 3, of which 2 were waited for; matrix products, arithmetic and copies ran while one was open for 11% of the time, Pallas kernels for 0%

profile of v1, /device:TPU:12, one launch (start us, length us, event | category | flops | bytes accessed | tf_op | source)
XLA Modules:
  0.0 445.9 jit_solution(8238950380326691210)
XLA Ops:
  7.2 0.0 all-gather.7.cloned.1.call-start
  9.2 2.7 constant_dynamic-slice_fusion.1
  11.9 2.4 all-gather
  14.2 0.9 constant_dynamic-slice_fusion
  15.2 0.0 all-gather.7.cloned.1.call-update
  15.2 0.0 all-gather.5.cloned.1.call-start
  15.2 147.5 %all-gather.7.cloned.1.call-done = bf16[32,88,1088]{2,1,0:T(8,128)(2,1)} async-done(((bf16[2,88,1088]{2,1,0:T(8,128)(2,1)}), bf16[32,88,1088]{2,1,0:T(8,128)(2,1)}) %all-gather.7.cloned.1.call-update) | async-done | bytes 6127632 | tf_op jit(solution)/shard_map/all_gather | solution.py:27
  162.8 0.0 all-gather.5.cloned.1.call-update
  162.8 0.0 reduce-scatter.4.cloned.1.call-start
  162.8 25.6 %reshape.27 = bf16[88,16,4,2,272]{4,3,2,1,0:T(2,128)(2,1)} reshape(bf16[88,16,2176]{2,1,0:T(8,128)(2,1)} %param.4) | data formatting | bytes 12255232 | tf_op jit(solution)/shard_map/reshape | solution.py:17
  188.4 8.5 %copy.11 = bf16[16,2,88,4,272]{4,3,2,1,0:T(4,128)(2,1)} copy(bf16[16,2,88,4,272]{4,1,3,0,2:T(2,128)(2,1)} %bitcast.24) | data formatting | bytes 12255232 | tf_op jit(solution)/shard_map/transpose | solution.py:18
  196.9 14.1 %reshape.28 = bf16[32,88,1088]{2,1,0:T(8,128)(2,1)} reshape(bf16[16,2,88,4,272]{4,3,2,1,0:T(4,128)(2,1)} %copy.11) | data formatting | bytes 12255232 | tf_op jit(solution)/shard_map/reshape | solution.py:18
  210.9 80.6 %all_to_all.5 = bf16[32,88,1088]{2,1,0:T(8,128)(2,1)} all-to-all(bf16[32,88,1088]{2,1,0:T(8,128)(2,1)} %reshape.28), channel_id=1, replica_groups=mesh['oz'=8,'core'=2,'y'=4,'xh'=2] {'oz','core','xh'}, dimensions={0} | all-to-all | bytes 12255232 | tf_op jit(solution)/shard_map/all_to_all | solution.py:19
  291.5 0.0 all-gather.5.cloned.1.call-done
  291.5 23.3 %fusion = f32[2,1088,1088,1,1,1]{2,1,4,5,3,0:T(8,128)} fusion(bf16[2,8,2,2,88,1088]{5,4,3,2,1,0:T(8,128)(2,1)} %all-gather.5.cloned.1.call-done, bf16[8,2,2,88,1088,1]{4,3,2,1,0,5:T(8,128)(2,1)} %bitcast.27), kind=kOutput, calls=%fused_computation | convolution fusion | flops 13333692416 | bytes 27852800 | tf_op jit(solution)/shard_map/dot_general | solution.py:31
  314.8 12.2 %copy.17 = f32[1088,2176]{1,0:T(8,128)} copy(f32[1088,2176]{0,1:T(8,128)} %bitcast.25) | data formatting | bytes 18939904
  327.0 0.0 copy-start.1
  327.0 0.0 copy-start
  327.0 0.0 reduce-scatter.4.cloned.1.call-update
  327.0 0.6 copy-done.1
  327.7 0.6 fusion.5
  329.5 0.0 copy-done
  329.6 0.1 dynamic-slice_subtract_fusion
  329.6 85.4 %reduce-scatter.4.cloned.1.call-done = f32[272,2176]{1,0:T(8,128)} async-done(((f32[1088,2176]{1,0:T(8,128)}), f32[272,2176]{1,0:T(8,128)}) %reduce-scatter.4.cloned.1.call-update) | async-done | bytes 2367504
  415.0 2.8 copy.18
  417.8 1.8 fusion.3
  419.6 19.2 %psum.7 = f32[1,1]{1,0:T(1,128)} all-reduce(f32[1,1]{1,0:T(1,128)} %bitcast.11), channel_id=1, replica_groups=mesh['oz'=8,'core'=2,'y'=4,'xh'=2] {'y','xh'}, use_global_device_ids=true, to_apply=%region_3.4 | all-reduce | flops 1 | bytes 8 | tf_op jit(solution)/shard_map/psum | solution.py:42
  438.9 0.6 reshape.31
  (1 shorter events, 0.0 us)
Async XLA Ops:
  7.2 155.6 %all-gather.7.cloned.1.call-start = ((), (), s32[]{:S(2)}) async-start(), calls=%async_computation.3 | async-start | bytes 6893568 | tf_op jit(solution)/shard_map/all_gather | solution.py:27
  15.2 276.3 %all-gather.5.cloned.1.call-start = ((), (), s32[]{:S(2)}) async-start(), calls=%async_computation.2 | async-start | bytes 19464192 | tf_op jit(solution)/shard_map/all_gather | solution.py:29
  162.8 252.2 %reduce-scatter.4.cloned.1.call-start = ((), (), s32[]{:S(2)}) async-start(), calls=%async_computation.4 | async-start | bytes 11837440
  327.0 0.7 copy-start.1
  327.0 2.5 copy-start
Sparse Core Ops, SparseCore 0:
  15.3 147.3 all-gather.6
  164.4 28.3 all-gather.4
  327.2 87.8 reduce-scatter.3

commit v2 on v1

v2 whole, which is shorter than its diff:
```python
import jax
import jax.numpy as jnp
from jax import lax
from jax.sharding import Mesh, PartitionSpec as P

GROUP = ("oz", "xh")


def per_device(integrals, owner_order, occ_energy, vir_energy):
    nq, nocc, nvir = integrals.shape
    ny, nh, nc = lax.axis_size("y"), lax.axis_size("xh"), lax.axis_size("core")
    blk = nvir // (ny * nh)
    oz, y, h, c = lax.axis_index("oz"), lax.axis_index("y"), lax.axis_index("xh"), lax.axis_index("core")
    orbital = oz * nh + h

    left = lax.all_to_all(integrals, GROUP, 1, 0, tiled=True)[:, 0, :]
    owner = owner_order[0]
    column = lax.dynamic_index_in_dim(integrals, owner, 1, keepdims=False)
    panel = lax.all_gather(column, GROUP, axis=0, tiled=True)

    left = jnp.transpose(left.reshape(-1, ny, nc, blk), (0, 2, 1, 3))
    partial_sum = lax.dot_general(
        left, panel, (((0,), (0,)), ((), ())), preferred_element_type=jnp.float32
    ).reshape(nc * ny * blk, nvir)
    summed = lax.psum_scatter(partial_sum, "core", scatter_dimension=0, tiled=True)
    summed = lax.psum_scatter(summed, "y", scatter_dimension=0, tiled=True)

    near_energy = lax.dynamic_slice_in_dim(vir_energy, (y * nc + c) * blk, blk)
    own_energy = lax.dynamic_index_in_dim(occ_energy, orbital, 0, keepdims=False)
    owner_energy = lax.dynamic_index_in_dim(occ_energy, owner, 0, keepdims=False)
    denominator = own_energy + owner_energy - near_energy[:, None] - vir_energy[None, :]
    rows = jnp.sum(summed * summed / denominator, axis=1)

    swap = [(cc * nh + hh, hh * nc + cc) for cc in range(nc) for hh in range(nh)]
    rows = lax.ppermute(rows, ("core", "xh"), swap)
    totals = lax.psum(jnp.sum(rows), ("y", "xh")).reshape(1, 1)
    return rows.reshape(1, 1, blk), totals


def solution(mesh):
    nocc, naux = mesh.shape["occ"], mesh.shape["aux"]
    cores, ys = 2, naux // 2
    fine = Mesh(mesh.devices.reshape(nocc // cores, cores, ys, naux // ys), ("oz", "core", "y", "xh"))
    in_specs = (P(("oz", "core", "y", "xh"), None, None), P(), P(), P())
    out_specs = (P(("oz", "core"), None, ("y", "xh")), P(("oz", "core"), None))
    return jax.shard_map(
        per_device, mesh=fine, in_specs=in_specs, out_specs=out_specs, check_vma=False
    )
```

time: 452 us -> 403 us (0.89)
  waiting for transfers between devices: 233 us -> 138 us
  blocking collectives: 102 us -> 158 us
  local copies, waits for them, and re-layouts: 68.5 us -> 56.6 us
    all_gather x2 -> x1, waiting for transfers between devices: 148 us -> 13.3 us  [per_device(): panel = lax.all_gather(column, GROUP, axis=0, tiled=True)]
    reduce_scatter x0 -> x2, waiting for transfers between devices: none -> 120 us  [the longest x1 90 us: per_device(): summed = lax.psum_scatter(summed, 'y', scatter_dimension=0, tiled=True)]
    unnamed x4 -> x3, waiting for transfers between devices: 85.4 us -> 0.05 us
    all_to_all x1, blocking collectives: 80.6 us -> 141 us  [per_device(): left = lax.all_to_all(integrals, GROUP, 1, 0, tiled=True)[:, 0, :]]
    another operation x0 -> x2, local copies, waits for them, and re-layouts: none -> 47.1 us  [per_device(): left = jnp.transpose(left.reshape(-1, ny, nc, blk), (0, 2, 1, 3))]
    reshape x3 -> x1, local copies, waits for them, and re-layouts: 40.2 us -> 0.56 us  [per_device(): return (rows.reshape(1, 1, blk), totals)]
    unnamed x7, local copies, waits for them, and re-layouts: 15.6 us -> 6.52 us
    transpose x1 -> x0, local copies, waits for them, and re-layouts: 8.48 us -> none  [per_device(): jnp.transpose(tiles, (1, 3, 0, 2, 4)).reshape(nocc * nh, nq, ny * blk)]
  transfers between devices with their start and end apart: 3 -> 4, of which waited for: 2 -> 4; matrix products, arithmetic and copies ran while one was open for 11% -> 12% of each run, Pallas kernels for 0% -> 0%
where the time goes in v2:
time: 403 us; the launch traced here: 395 us
  blocking collectives  158 us (39%)
  waiting for transfers between devices  138 us (34%)
  local copies, waits for them, and re-layouts  56.6 us (14%)
  matrix products  21.6 us (5%)
  between operations  15.2 us (4%)
    all_to_all x1, blocking collectives, per_device(): left = lax.all_to_all(integrals, GROUP, 1, 0, tiled=True)[:, 0, :]  141 us
    reduce_scatter x1, waiting for transfers between devices, per_device(): summed = lax.psum_scatter(summed, 'y', scatter_dimension=0, tiled=True)  90 us
    another operation x2, local copies, waits for them, and re-layouts, per_device(): left = jnp.transpose(left.reshape(-1, ny, nc, blk), (0, 2, 1, 3))  47.1 us
    reduce_scatter x1, waiting for transfers between devices, per_device(): lax.psum_scatter(partial_sum, 'core', scatter_dimension=0, tiled=True)  30.2 us
    dot_general x1, matrix products, per_device(): lax.dot_general(left, panel, (((0,), (0,)), ((), ())), preferred_element_...  21.6 us
    psum x1, blocking collectives, per_device(): totals = lax.psum(jnp.sum(rows), ('y', 'xh')).reshape(1, 1)  17.5 us
    all_gather x1, waiting for transfers between devices, per_device(): panel = lax.all_gather(column, GROUP, axis=0, tiled=True)  13.3 us
  transfers between devices with their start and end apart: 4, of which 4 were waited for; matrix products, arithmetic and copies ran while one was open for 12% of the time, Pallas kernels for 0%

profile of v2, /device:TPU:12, one launch (start us, length us, event | category | flops | bytes accessed | tf_op | source)
XLA Modules:
  0.0 394.8 jit_solution(7151527639368418609)
XLA Ops:
  7.2 0.0 copy-start.2
  7.2 0.0 all-gather.3.cloned.1.call-start
  7.2 6.5 %copy.10 = bf16[88,16,2176]{2,0,1:T(8,128)(2,1)} copy(bf16[88,16,2176]{2,1,0:T(8,128)(2,1)} %param.4) | data formatting | bytes 12255232 | tf_op args[0]
  13.7 0.0 copy-done.2
  13.8 1.8 constant_dynamic-slice_fusion
  15.6 0.0 all-gather.3.cloned.1.call-update
  15.6 0.0 reduce-scatter.3.cloned.1.call-start
  15.7 140.9 %all_to_all.15 = bf16[88,16,2176]{2,0,1:T(8,128)(2,1)} all-to-all(bf16[88,16,2176]{2,0,1:T(8,128)(2,1)} %copy.10), channel_id=1, replica_groups=mesh['oz'=8,'core'=2,'y'=4,'xh'=2] {'oz','xh'}, dimensions={1} | all-to-all | bytes 12255232 | tf_op jit(solution)/shard_map/all_to_all | solution.py:16
  156.6 25.6 %reshape.23 = bf16[1408,4,2,272]{3,2,1,0:T(2,128)(2,1)} reshape(bf16[16,88,1,2176]{3,1,0,2:T(8,128)(2,1)} %bitcast.24) | data formatting | bytes 12255232 | tf_op jit(solution)/shard_map/reshape;squeeze | solution.py:21
  182.2 21.5 %copy.13 = bf16[1408,4,2,272]{0,3,1,2:T(8,128)(2,1)} copy(bf16[1408,4,2,272]{3,2,1,0:T(2,128)(2,1)} %reshape.23) | data formatting | bytes 12255232 | tf_op jit(solution)/shard_map/reshape;squeeze | solution.py:21
  203.7 13.3 %all-gather.3.cloned.1.call-done = bf16[1408,1,2176]{2,0,1:T(8,128)(2,1)} async-done(((bf16[88,1,2176]{2,0,1:T(8,128)(2,1)}), bf16[1408,1,2176]{2,0,1:T(8,128)(2,1)}) %all-gather.3.cloned.1.call-update) | async-done | bytes 6127632 | tf_op jit(solution)/shard_map/all_gather | solution.py:19
  217.1 21.6 %fusion = f32[2176,2,4,272]{0,3,2,1:T(8,128)} fusion(bf16[1408,1,2176]{2,0,1:T(8,128)(2,1)} %all-gather.3.cloned.1.call-done, bf16[1408,4,2,272]{0,3,1,2:T(8,128)(2,1)} %copy.13), kind=kOutput, calls=%fused_computation | convolution fusion | flops 13333692416 | bytes 31195136 | tf_op jit(solution)/shard_map/dot_general | solution.py:22
  238.6 0.0 reduce-scatter.3.cloned.1.call-update
  238.7 0.0 copy-start.1
  238.7 0.0 copy-start
  238.7 0.0 reduce-scatter.5.cloned.1.call-start
  238.7 30.2 %reduce-scatter.3.cloned.1.call-done = f32[1088,2176]{1,0:T(8,128)} async-done(((f32[2176,2176]{1,0:T(8,128)}), f32[1088,2176]{1,0:T(8,128)}) %reduce-scatter.3.cloned.1.call-update) | async-done | bytes 9469968 | tf_op jit(solution)/shard_map/reduce_scatter | solution.py:25
  269.0 0.0 reduce-scatter.5.cloned.1.call-update
  269.0 0.0 copy-done.1
  269.0 0.6 fusion.4
  270.9 0.0 copy-done
  270.9 0.1 dynamic-slice_subtract_fusion
  271.0 90.0 %reduce-scatter.5.cloned.1.call-done = f32[272,2176]{1,0:T(8,128)} async-done(((f32[1088,2176]{1,0:T(8,128)}), f32[272,2176]{1,0:T(8,128)}) %reduce-scatter.5.cloned.1.call-update) | async-done | bytes 2367504 | tf_op jit(solution)/shard_map/reduce_scatter | solution.py:26
  361.0 2.2 fusion.3
  363.2 1.9 collective-permute-start
  365.1 4.5 %collective-permute-done = f32[272]{0:T(512)S(1)} collective-permute-done((f32[272]{0:T(512)S(1)}, f32[272]{0:T(512)S(1)}, u32[]{:S(2)}, u32[]{:S(2)}) %collective-permute-start) | collective-permute-done | bytes 1120 | tf_op jit(solution)/shard_map/ppermute | solution.py:35
  369.6 0.6 reduce_sum.19
  370.2 17.5 %psum.7 = f32[1,1]{1,0:T(1,128)} all-reduce(f32[1,1]{1,0:T(1,128)} %bitcast.10), channel_id=1, replica_groups=mesh['oz'=8,'core'=2,'y'=4,'xh'=2] {'y','xh'}, use_global_device_ids=true, to_apply=%region_4.5 | all-reduce | flops 1 | bytes 8 | tf_op jit(solution)/shard_map/psum | solution.py:36
  387.7 0.6 reshape.19
Async XLA Ops:
  7.2 6.6 %copy-start.2 = (s32[16]{0:T(128)S(1)}, s32[16]{0:T(128)}, u32[]{:S(2)}) copy-start(s32[16]{0:T(128)} %param.5) | copy-start | bytes 196
  7.2 209.9 %all-gather.3.cloned.1.call-start = ((), (), s32[]{:S(2)}) async-start(), calls=%async_computation.5 | async-start | bytes 6510592 | tf_op jit(solution)/shard_map/all_gather | solution.py:19
  15.6 253.3 %reduce-scatter.3.cloned.1.call-start = ((), (), s32[]{:S(2)}) async-start(), calls=%async_computation.3 | async-start | bytes 28409856 | tf_op jit(solution)/shard_map/reduce_scatter | solution.py:25
  238.7 30.3 %copy-start.1 = (f32[16]{0:T(128)S(1)}, f32[16]{0:T(128)}, u32[]{:S(2)}) copy-start(f32[16]{0:T(128)} %param.6) | copy-start | bytes 196
  238.7 32.2 %copy-start = (f32[2176]{0:T(1024)S(1)}, f32[2176]{0:T(1024)}, u32[]{:S(2)}) copy-start(f32[2176]{0:T(1024)} %param.7) | copy-start | bytes 26116
  238.7 122.3 %reduce-scatter.5.cloned.1.call-start = ((), (), s32[]{:S(2)}) async-start(), calls=%async_computation.4 | async-start | bytes 11837440 | tf_op jit(solution)/shard_map/reduce_scatter | solution.py:26
  363.2 6.4 %collective-permute-start = (f32[272]{0:T(512)S(1)}, f32[272]{0:T(512)S(1)}, u32[]{:S(2)}, u32[]{:S(2)}) collective-permute-start(f32[272]{0:T(512)S(1)} %fusion.3), channel_id=1, source_target_pairs={{0,0},{1,8},{8,1},{9,9},{2,2},{3,10},{10,3},{11,11},{4,4},{5,12},{... | collective-permute-start | bytes 3272 | tf_op jit(solution)/shard_map/ppermute | solution.py:35
Sparse Core Ops, SparseCore 0:
  15.8 201.2 all-gather.2
  238.8 30.1 reduce-scatter.2
  271.4 89.4 reduce-scatter.4

commit v3 on v2

v3 whole, which is shorter than its diff:
```python
import jax
import jax.numpy as jnp
from jax import lax
from jax.sharding import Mesh, PartitionSpec as P

GROUP = ("z", "xh", "xl")


def per_device(integrals, owner_order, occ_energy, vir_energy):
    nq, nocc, nvir = integrals.shape
    ny, nh, nc, nl = lax.axis_size("y"), lax.axis_size("xh"), lax.axis_size("core"), lax.axis_size("xl")
    blk = nvir // (ny * nh)
    z, l, y, h, c = (lax.axis_index(a) for a in ("z", "xl", "y", "xh", "core"))
    orbital = (z * nh + h) * nl + l
    block = c * ny + y

    left = lax.all_to_all(integrals, GROUP, 1, 0, tiled=True)[:, 0, :]
    owner = owner_order[0]
    column = lax.dynamic_index_in_dim(integrals, owner, 1, keepdims=False)
    panel = lax.all_gather(column, GROUP, axis=0, tiled=True)

    partial_sum = lax.dot_general(
        left, panel, (((0,), (0,)), ((), ())), preferred_element_type=jnp.float32
    )
    summed = lax.psum_scatter(partial_sum, "core", scatter_dimension=0, tiled=True)
    summed = lax.psum_scatter(summed, "y", scatter_dimension=0, tiled=True)

    near_energy = lax.dynamic_slice_in_dim(vir_energy, block * blk, blk)
    own_energy = lax.dynamic_index_in_dim(occ_energy, orbital, 0, keepdims=False)
    owner_energy = lax.dynamic_index_in_dim(occ_energy, owner, 0, keepdims=False)
    denominator = own_energy + owner_energy - near_energy[:, None] - vir_energy[None, :]
    rows = jnp.sum(summed * summed / denominator, axis=1)

    total = jnp.sum(rows)
    total = total + lax.ppermute(total, "core", [(k, (k + 1) % nc) for k in range(nc)])
    total = total + lax.ppermute(total, "y", [(k, (k + 1) % ny) for k in range(ny)])
    total = total + lax.ppermute(total, "y", [(k, (k + 2) % ny) for k in range(ny)])

    def index(ll, cc, yy, hh):
        return ((ll * nc + cc) * ny + yy) * nh + hh

    moves = []
    for ll in range(nl):
        for cc in range(nc):
            for yy in range(ny):
                for hh in range(nh):
                    b = cc * ny + yy
                    moves.append((index(ll, cc, yy, hh), index(hh, ll, b // nh, b % nh)))
    packed = jnp.concatenate([rows, total[None]])
    packed = lax.ppermute(packed, ("xl", "core", "y", "xh"), moves)
    return packed[:blk].reshape(1, 1, blk), packed[blk:].reshape(1, 1)


def solution(mesh):
    nocc, naux = mesh.shape["occ"], mesh.shape["aux"]
    cores, xls, ys = 2, 2, naux // 2
    shape = (nocc // (cores * xls), xls, cores, ys, naux // ys)
    fine = Mesh(mesh.devices.reshape(shape), ("z", "xl", "core", "y", "xh"))
    in_specs = (P(("z", "xl", "core", "y", "xh"), None, None), P(), P(), P())
    out_specs = (P(("z", "xl", "core"), None, ("y", "xh")), P(("z", "xl", "core"), None))
    return jax.shard_map(
        per_device, mesh=fine, in_specs=in_specs, out_specs=out_specs, check_vma=False
    )
```

time: 403 us -> 326 us (0.81); the launches traced: 395 us -> 324 us
  blocking collectives: 158 us -> 83.5 us
  local copies, waits for them, and re-layouts: 56.6 us -> 33.4 us
  waiting for transfers between devices: 138 us -> 153 us
  starting transfers between devices: 2.04 us -> 11.2 us
    reduce_scatter x2 -> x0, waiting for transfers between devices: 120 us -> none  [the longest x1 90 us: per_device(): summed = lax.psum_scatter(summed, 'y', scatter_dimension=0, tiled=True)]
    unnamed x3 -> x5, waiting for transfers between devices: 0.05 us -> 119 us
    all_to_all x1, blocking collectives: 141 us -> 83.5 us  [per_device(): left = lax.all_to_all(integrals, GROUP, 1, 0, tiled=True)[:, 0, :]]
    another operation x2 -> x0, local copies, waits for them, and re-layouts: 47.1 us -> none  [per_device(): left = jnp.transpose(left.reshape(-1, ny, nc, blk), (0, 2, 1, 3))]
    unnamed x7 -> x9, local copies, waits for them, and re-layouts: 6.52 us -> 29.9 us
    psum x1 -> x0, blocking collectives: 17.5 us -> none  [per_device(): totals = lax.psum(jnp.sum(rows), ('y', 'xh')).reshape(1, 1)]
    all_gather x1, waiting for transfers between devices: 13.3 us -> 25 us  [per_device(): panel = lax.all_gather(column, GROUP, axis=0, tiled=True)]
    ppermute x1 -> x4, starting transfers between devices: 1.92 us -> 11.1 us  [the longest x1 5.51 us: per_device(): packed = lax.ppermute(packed, ('xl', 'core', 'y', 'xh'), moves)]
  transfers between devices with their start and end apart: 4 -> 7, of which waited for: 4 -> 7; matrix products, arithmetic and copies ran while one was open for 12% -> 0% of each run, Pallas kernels for 0% -> 0%
where the time goes in v3:
time: 326 us; the launch traced here: 324 us
  waiting for transfers between devices  153 us (47%)
  blocking collectives  83.5 us (26%)
  local copies, waits for them, and re-layouts  33.4 us (10%)
  matrix products  22.3 us (7%)
  between operations  19.2 us (6%)
  starting transfers between devices  11.2 us (3%)
    unnamed x5, waiting for transfers between devices  119 us
    all_to_all x1, blocking collectives, per_device(): left = lax.all_to_all(integrals, GROUP, 1, 0, tiled=True)[:, 0, :]  83.5 us
    unnamed x9, local copies, waits for them, and re-layouts  29.9 us
    all_gather x1, waiting for transfers between devices, per_device(): panel = lax.all_gather(column, GROUP, axis=0, tiled=True)  25 us
    dot_general x1, matrix products, per_device(): lax.dot_general(left, panel, (((0,), (0,)), ((), ())), preferred_element_...  22.3 us
  transfers between devices with their start and end apart: 7, of which 7 were waited for; matrix products, arithmetic and copies ran while one was open for 0% of the time, Pallas kernels for 0%

profile of v3, /device:TPU:12, one launch (start us, length us, event | category | flops | bytes accessed | tf_op | source)
XLA Modules:
  0.0 324.1 jit_solution(2128678945617478445)
XLA Ops:
  7.2 0.0 all-gather.3.cloned.1.call-start
  8.5 0.0 copy-start.2
  8.5 6.5 %copy.8 = bf16[88,16,2176]{2,0,1:T(8,128)(2,1)} copy(bf16[88,16,2176]{2,1,0:T(8,128)(2,1)} %param.4) | data formatting | bytes 12255232 | tf_op args[0]
  15.0 0.0 copy-done.2
  15.1 1.8 constant_dynamic-slice_fusion
  16.9 0.0 all-gather.3.cloned.1.call-update
  16.9 0.0 reduce-scatter.7.cloned.1.call-start
  16.9 83.5 %all_to_all.15 = bf16[88,16,2176]{2,0,1:T(8,128)(2,1)} all-to-all(bf16[88,16,2176]{2,0,1:T(8,128)(2,1)} %copy.8), channel_id=1, replica_groups=mesh['z'=4,'xl'=2,'core'=2,'y'=4,'xh'=2] {'z','xh','xl'}, dimensions={1} | all-to-all | bytes 12255232 | tf_op jit(solution)/shard_map/all_to_all | solution.py:17
  100.4 25.0 %all-gather.3.cloned.1.call-done = bf16[1408,1,2176]{2,0,1:T(8,128)(2,1)} async-done(((bf16[88,1,2176]{2,0,1:T(8,128)(2,1)}), bf16[1408,1,2176]{2,0,1:T(8,128)(2,1)}) %all-gather.3.cloned.1.call-update) | async-done | bytes 6127632 | tf_op jit(solution)/shard_map/all_gather | solution.py:20
  125.4 22.3 %convolution_bitcast_fusion = f32[2176,2176]{0,1:T(8,128)} fusion(bf16[1408,2176]{1,0:T(8,128)(2,1)} %bitcast.19, bf16[1408,1,2176]{2,0,1:T(8,128)(2,1)} %all-gather.3.cloned.1.call-done), kind=kOutput, calls=%fused_computation | convolution fusion | flops 13333692416 | bytes 31195136 | tf_op jit(solution)/shard_map/dot_general | solution.py:22
  147.8 20.6 %copy.10 = f32[2176,2176]{1,0:T(8,128)} copy(f32[2176,2176]{0,1:T(8,128)} %convolution_bitcast_fusion) | data formatting | bytes 37879808
  168.3 0.0 reduce-scatter.7.cloned.1.call-update
  168.4 0.0 copy-start.1
  168.4 0.0 copy-start
  168.4 0.0 reduce-scatter.9.cloned.1.call-start
  168.4 29.3 %reduce-scatter.7.cloned.1.call-done = f32[1088,2176]{1,0:T(8,128)} async-done(((f32[2176,2176]{1,0:T(8,128)}), f32[1088,2176]{1,0:T(8,128)}) %reduce-scatter.7.cloned.1.call-update) | async-done | bytes 9469968
  197.7 0.0 reduce-scatter.9.cloned.1.call-update
  197.7 0.0 copy-done.1
  197.7 0.6 fusion.3
  199.6 0.0 copy-done
  199.6 0.1 dynamic-slice_subtract_fusion
  199.7 90.0 %reduce-scatter.9.cloned.1.call-done = f32[272,2176]{1,0:T(8,128)} async-done(((f32[1088,2176]{1,0:T(8,128)}), f32[272,2176]{1,0:T(8,128)}) %reduce-scatter.9.cloned.1.call-update) | async-done | bytes 2367504
  289.7 2.8 copy.13
  292.5 1.8 fusion.2
  294.3 0.0 collective-permute-start
  294.3 1.3 collective-permute-done
  296.9 2.5 collective-permute-start.1
  299.4 1.0 collective-permute-done.1
  301.2 3.0 collective-permute-start.2
  304.2 2.1 collective-permute-done.2
  307.0 0.1 pad_maximum_fusion
  307.1 5.5 %collective-permute-start.3 = (f32[273]{0:T(512)S(1)}, f32[273]{0:T(512)S(1)}, u32[]{:S(2)}, u32[]{:S(2)}) collective-permute-start(f32[273]{0:T(512)S(1)} %pad_maximum_fusion), channel_id=1, source_target_pairs={{0,0},{1,16},{2,1},{3,17},{4,2},{5,18},{6,3},{7,19},{8,4},{9,20},{... | collective-permute-start | bytes 3284 | tf_op jit(solution)/shard_map/ppermute | solution.py:50
  312.6 3.9 %collective-permute-done.3 = f32[273]{0:T(512)S(1)} collective-permute-done((f32[273]{0:T(512)S(1)}, f32[273]{0:T(512)S(1)}, u32[]{:S(2)}, u32[]{:S(2)}) %collective-permute-start.3) | collective-permute-done | bytes 1124 | tf_op jit(solution)/shard_map/ppermute | solution.py:50
  316.4 0.6 reshape.15
  317.0 0.6 slice.11
Async XLA Ops:
  7.2 118.3 %all-gather.3.cloned.1.call-start = ((), (), s32[]{:S(2)}) async-start(), calls=%async_computation.3 | async-start | bytes 6510592 | tf_op jit(solution)/shard_map/all_gather | solution.py:20
  8.5 6.5 %copy-start.2 = (s32[16]{0:T(128)S(1)}, s32[16]{0:T(128)}, u32[]{:S(2)}) copy-start(s32[16]{0:T(128)} %param.5) | copy-start | bytes 196
  16.9 180.8 %reduce-scatter.7.cloned.1.call-start = ((), (), s32[]{:S(2)}) async-start(), calls=%async_computation.4 | async-start | bytes 28409856
  168.4 29.4 %copy-start.1 = (f32[16]{0:T(128)S(1)}, f32[16]{0:T(128)}, u32[]{:S(2)}) copy-start(f32[16]{0:T(128)} %param.6) | copy-start | bytes 196
  168.4 31.3 %copy-start = (f32[2176]{0:T(1024)S(1)}, f32[2176]{0:T(1024)}, u32[]{:S(2)}) copy-start(f32[2176]{0:T(1024)} %param.7) | copy-start | bytes 26116
  168.4 121.3 %reduce-scatter.9.cloned.1.call-start = ((), (), s32[]{:S(2)}) async-start(), calls=%async_computation.5 | async-start | bytes 11837440
  294.3 1.3 collective-permute-start
  296.9 3.6 %collective-permute-start.1 = (f32[]{:T(128)}, f32[]{:T(128)}, u32[]{:S(2)}, u32[]{:S(2)}) collective-permute-start(f32[]{:T(128)} %add.48), channel_id=1, source_target_pairs={{0,2},{2,4},{4,6},{6,0},{1,3},{3,5},{5,7},{7,1},{8,10},{10,12},{12... | collective-permute-start | bytes 20 | tf_op jit(solution)/shard_map/ppermute | solution.py:36
  301.2 5.1 %collective-permute-start.2 = (f32[]{:T(128)}, f32[]{:T(128)}, u32[]{:S(2)}, u32[]{:S(2)}) collective-permute-start(f32[]{:T(128)} %add.49), channel_id=1, source_target_pairs={{0,4},{2,6},{4,0},{6,2},{1,5},{3,7},{5,1},{7,3},{8,12},{10,14},{12... | collective-permute-start | bytes 20 | tf_op jit(solution)/shard_map/ppermute | solution.py:37
  307.1 9.4 %collective-permute-start.3 = (f32[273]{0:T(512)S(1)}, f32[273]{0:T(512)S(1)}, u32[]{:S(2)}, u32[]{:S(2)}) collective-permute-start(f32[273]{0:T(512)S(1)} %pad_maximum_fusion), channel_id=1, source_target_pairs={{0,0},{1,16},{2,1},{3,17},{4,2},{5,18},{6,3},{7,19},{8,4},{9,20},{... | collective-permute-start | bytes 3284 | tf_op jit(solution)/shard_map/ppermute | solution.py:50
Sparse Core Ops, SparseCore 0:
  17.0 108.3 all-gather.2
  168.5 29.1 reduce-scatter.6
  200.2 89.4 reduce-scatter.8

commit v4 on v3

--- a/solution.py
+++ b/solution.py
@@ -22,19 +22,25 @@
     partial_sum = lax.dot_general(
         left, panel, (((0,), (0,)), ((), ())), preferred_element_type=jnp.float32
     )
-    summed = lax.psum_scatter(partial_sum, "core", scatter_dimension=0, tiled=True)
-    summed = lax.psum_scatter(summed, "y", scatter_dimension=0, tiled=True)
+    summed = lax.psum_scatter(partial_sum, "core", scatter_dimension=1, tiled=True)
+    summed = lax.psum_scatter(summed, "y", scatter_dimension=1, tiled=True)
 
     near_energy = lax.dynamic_slice_in_dim(vir_energy, block * blk, blk)
     own_energy = lax.dynamic_index_in_dim(occ_energy, orbital, 0, keepdims=False)
     owner_energy = lax.dynamic_index_in_dim(occ_energy, owner, 0, keepdims=False)
-    denominator = own_energy + owner_energy - near_energy[:, None] - vir_energy[None, :]
-    rows = jnp.sum(summed * summed / denominator, axis=1)
+    denominator = own_energy + owner_energy - vir_energy[:, None] - near_energy[None, :]
+    part_rows = jnp.sum(summed * summed / denominator, axis=1)
 
-    total = jnp.sum(rows)
-    total = total + lax.ppermute(total, "core", [(k, (k + 1) % nc) for k in range(nc)])
-    total = total + lax.ppermute(total, "y", [(k, (k + 1) % ny) for k in range(ny)])
-    total = total + lax.ppermute(total, "y", [(k, (k + 2) % ny) for k in range(ny)])
+    total = jnp.sum(part_rows)
+    pieces = part_rows.reshape(nc, ny // 2, 2, blk)
+    for axis, bit, step, size in (("core", c, 1, nc), ("y", y // 2, 2, ny), ("y", y % 2, 1, ny)):
+        keep = lax.dynamic_index_in_dim(pieces, bit, 0, keepdims=False)
+        give = lax.dynamic_index_in_dim(pieces, 1 - bit, 0, keepdims=False)
+        flip = [(k, k ^ step) for k in range(size)]
+        got = lax.ppermute(jnp.concatenate([give.reshape(-1), total[None]]), axis, flip)
+        pieces = keep + got[:-1].reshape(keep.shape)
+        total = total + got[-1]
+    rows = pieces.reshape(blk)
 
     def index(ll, cc, yy, hh):
         return ((ll * nc + cc) * ny + yy) * nh + hh

time: 326 us -> 305 us (0.936)
  local copies, waits for them, and re-layouts: 33.4 us -> 12.3 us
  starting transfers between devices: 11.2 us -> 7.73 us
    unnamed x5 -> x3, waiting for transfers between devices: 119 us -> 0.05 us
    reduce_scatter x0 -> x2, waiting for transfers between devices: none -> 119 us  [the longest x1 90 us: per_device(): summed = lax.psum_scatter(summed, 'y', scatter_dimension=1, tiled=True)]
    unnamed x9 -> x7, local copies, waits for them, and re-layouts: 29.9 us -> 6.52 us
where the time goes in v4:
time: 305 us
  waiting for transfers between devices  156 us (51%)
  blocking collectives  83.5 us (27%)
  matrix products  22.2 us (7%)
  between operations  19.1 us (6%)
  local copies, waits for them, and re-layouts  12.3 us (4%)
  starting transfers between devices  7.73 us (3%)
  other arithmetic  4.28 us (1%)
    reduce_scatter x1, waiting for transfers between devices, per_device(): summed = lax.psum_scatter(summed, 'y', scatter_dimension=1, tiled=True)  90 us
    all_to_all x1, blocking collectives, per_device(): left = lax.all_to_all(integrals, GROUP, 1, 0, tiled=True)[:, 0, :]  83.5 us
    reduce_scatter x1, waiting for transfers between devices, per_device(): lax.psum_scatter(partial_sum, 'core', scatter_dimension=1, tiled=True)  29.3 us
    all_gather x1, waiting for transfers between devices, per_device(): panel = lax.all_gather(column, GROUP, axis=0, tiled=True)  25 us
    dot_general x1, matrix products, per_device(): lax.dot_general(left, panel, (((0,), (0,)), ((), ())), preferred_element_...  22.2 us
    ppermute x3, waiting for transfers between devices, per_device(): lax.ppermute(jnp.concatenate([give.reshape(-1), total[None]]), axis, flip)  6.59 us
    unnamed x7, local copies, waits for them, and re-layouts  6.52 us
  transfers between devices with their start and end apart: 7, of which 7 were waited for; matrix products, arithmetic and copies ran while one was open for 0% of the time, Pallas kernels for 0%

profile of v4, /device:TPU:12, one launch (start us, length us, event | category | flops | bytes accessed | tf_op | source)
XLA Modules:
  0.0 305.1 jit_solution(8882906203427185969)
XLA Ops:
  7.2 0.0 all-gather.3.cloned.1.call-start
  8.5 0.0 copy-start.2
  8.5 6.5 %copy.6 = bf16[88,16,2176]{2,0,1:T(8,128)(2,1)} copy(bf16[88,16,2176]{2,1,0:T(8,128)(2,1)} %param.4) | data formatting | bytes 12255232 | tf_op args[0]
  15.0 0.0 copy-done.2
  15.1 1.8 constant_dynamic-slice_fusion.4
  16.8 0.0 all-gather.3.cloned.1.call-update
  16.9 0.0 reduce-scatter.3.cloned.1.call-start
  16.9 83.5 %all_to_all.15 = bf16[88,16,2176]{2,0,1:T(8,128)(2,1)} all-to-all(bf16[88,16,2176]{2,0,1:T(8,128)(2,1)} %copy.6), channel_id=1, replica_groups=mesh['z'=4,'xl'=2,'core'=2,'y'=4,'xh'=2] {'z','xh','xl'}, dimensions={1} | all-to-all | bytes 12255232 | tf_op jit(solution)/shard_map/all_to_all | solution.py:17
  100.4 25.0 %all-gather.3.cloned.1.call-done = bf16[1408,1,2176]{2,0,1:T(8,128)(2,1)} async-done(((bf16[88,1,2176]{2,0,1:T(8,128)(2,1)}), bf16[1408,1,2176]{2,0,1:T(8,128)(2,1)}) %all-gather.3.cloned.1.call-update) | async-done | bytes 6127632 | tf_op jit(solution)/shard_map/all_gather | solution.py:20
  125.4 22.2 %convolution_bitcast_fusion = f32[2176,2176]{0,1:T(8,128)} fusion(bf16[1408,2176]{1,0:T(8,128)(2,1)} %bitcast.29, bf16[1408,1,2176]{2,0,1:T(8,128)(2,1)} %all-gather.3.cloned.1.call-done), kind=kOutput, calls=%fused_computation | convolution fusion | flops 13333692416 | bytes 31195136 | tf_op jit(solution)/shard_map/dot_general | solution.py:22
  147.7 0.0 reduce-scatter.3.cloned.1.call-update
  147.7 0.0 copy-start.1
  147.7 0.0 copy-start
  147.7 0.0 reduce-scatter.5.cloned.1.call-start
  147.8 29.3 %reduce-scatter.3.cloned.1.call-done = f32[2176,1088]{0,1:T(8,128)} async-done(((f32[2176,2176]{0,1:T(8,128)}), f32[2176,1088]{0,1:T(8,128)}) %reduce-scatter.3.cloned.1.call-update) | async-done | bytes 9469968 | tf_op jit(solution)/shard_map/reduce_scatter | solution.py:25
  177.0 0.0 reduce-scatter.5.cloned.1.call-update
  177.1 0.0 copy-done.1
  177.1 0.6 fusion.5
  179.0 0.0 copy-done
  179.0 0.1 dynamic_slice.38
  179.0 90.0 %reduce-scatter.5.cloned.1.call-done = f32[2176,272]{0,1:T(8,128)} async-done(((f32[2176,1088]{0,1:T(8,128)}), f32[2176,272]{0,1:T(8,128)}) %reduce-scatter.5.cloned.1.call-update) | async-done | bytes 2367504 | tf_op jit(solution)/shard_map/reduce_scatter | solution.py:26
  269.0 3.3 %fusion.2 = (f32[2176]{0:T(1024)S(1)}, f32[]{:T(128)}) fusion(f32[272]{0:T(512)S(1)} %dynamic_slice.38, f32[2176]{0:T(1024)S(1)} %broadcast_subtract_fusion, f32[2176,272]{0,1:T(8,128)} %reduce-scatter.5.cloned.1.call-done), kind=kLoop, calls=%fused_computation.4 | loop fusion | flops 2957183 | bytes 2385988 | tf_op jit(solution)/shard_map/reduce_sum | solution.py:32
  272.3 0.1 reshape.32
  272.4 0.1 reshape.33
  272.5 0.7 pad_maximum_fusion
  273.2 0.0 collective-permute-start
  273.3 1.1 collective-permute-done
  274.4 0.1 reshape.34
  274.5 0.1 reshape.35
  274.6 0.6 slice.37
  276.5 0.1 pad_maximum_fusion.1
  276.6 1.5 collective-permute-start.1
  278.0 3.7 %collective-permute-done.1 = f32[545]{0:T(1024)S(1)} collective-permute-done((f32[545]{0:T(1024)S(1)}, f32[545]{0:T(1024)S(1)}, u32[]{:S(2)}, u32[]{:S(2)}) %collective-permute-start.1) | collective-permute-done | bytes 2212 | tf_op jit(solution)/shard_map/ppermute | solution.py:40
  281.7 0.1 reshape.36
  281.8 0.6 slice.31
  283.1 0.1 pad_maximum_fusion.2
  283.1 1.8 collective-permute-start.2
  285.0 1.8 collective-permute-done.2
  286.7 0.6 slice.33
  288.0 0.1 pad_maximum_fusion.3
  288.1 4.3 %collective-permute-start.3 = (f32[273]{0:T(512)S(1)}, f32[273]{0:T(512)S(1)}, u32[]{:S(2)}, u32[]{:S(2)}) collective-permute-start(f32[273]{0:T(512)S(1)} %pad_maximum_fusion.3), channel_id=1, source_target_pairs={{0,0},{1,16},{2,1},{3,17},{4,2},{5,18},{6,3},{7,19},{8,4},{9,20},{... | collective-permute-start | bytes 3284 | tf_op jit(solution)/shard_map/ppermute | solution.py:56
  292.4 5.1 %collective-permute-done.3 = f32[273]{0:T(512)S(1)} collective-permute-done((f32[273]{0:T(512)S(1)}, f32[273]{0:T(512)S(1)}, u32[]{:S(2)}, u32[]{:S(2)}) %collective-permute-start.3) | collective-permute-done | bytes 1124 | tf_op jit(solution)/shard_map/ppermute | solution.py:56
  297.4 0.6 reshape.37
  298.0 0.6 slice.35
  (7 shorter events, 0.1 us)
Async XLA Ops:
  7.2 118.2 %all-gather.3.cloned.1.call-start = ((), (), s32[]{:S(2)}) async-start(), calls=%async_computation.5 | async-start | bytes 6510592 | tf_op jit(solution)/shard_map/all_gather | solution.py:20
  8.5 6.5 %copy-start.2 = (s32[16]{0:T(128)S(1)}, s32[16]{0:T(128)}, u32[]{:S(2)}) copy-start(s32[16]{0:T(128)} %param.5) | copy-start | bytes 196
  16.9 160.2 %reduce-scatter.3.cloned.1.call-start = ((), (), s32[]{:S(2)}) async-start(), calls=%async_computation.3 | async-start | bytes 28409856 | tf_op jit(solution)/shard_map/reduce_scatter | solution.py:25
  147.7 29.4 %copy-start.1 = (f32[16]{0:T(128)S(1)}, f32[16]{0:T(128)}, u32[]{:S(2)}) copy-start(f32[16]{0:T(128)} %param.6) | copy-start | bytes 196
  147.7 31.3 %copy-start = (f32[2176]{0:T(1024)S(1)}, f32[2176]{0:T(1024)}, u32[]{:S(2)}) copy-start(f32[2176]{0:T(1024)} %param.7) | copy-start | bytes 26116
  147.7 121.3 %reduce-scatter.5.cloned.1.call-start = ((), (), s32[]{:S(2)}) async-start(), calls=%async_computation.4 | async-start | bytes 11837440 | tf_op jit(solution)/shard_map/reduce_scatter | solution.py:26
  273.2 1.2 collective-permute-start
  276.6 5.1 %collective-permute-start.1 = (f32[545]{0:T(1024)S(1)}, f32[545]{0:T(1024)S(1)}, u32[]{:S(2)}, u32[]{:S(2)}) collective-permute-start(f32[545]{0:T(1024)S(1)} %pad_maximum_fusion.1), channel_id=1, source_target_pairs={{0,4},{2,6},{4,0},{6,2},{1,5},{3,7},{5,1},{7,3},{8,12},{10,14},{12... | collective-permute-start | bytes 6548 | tf_op jit(solution)/shard_map/ppermute | solution.py:40
  283.1 3.6 %collective-permute-start.2 = (f32[273]{0:T(512)S(1)}, f32[273]{0:T(512)S(1)}, u32[]{:S(2)}, u32[]{:S(2)}) collective-permute-start(f32[273]{0:T(512)S(1)} %pad_maximum_fusion.2), channel_id=1, source_target_pairs={{0,2},{2,0},{4,6},{6,4},{1,3},{3,1},{5,7},{7,5},{8,10},{10,8},{12,... | collective-permute-start | bytes 3284 | tf_op jit(solution)/shard_map/ppermute | solution.py:40
  288.1 9.4 %collective-permute-start.3 = (f32[273]{0:T(512)S(1)}, f32[273]{0:T(512)S(1)}, u32[]{:S(2)}, u32[]{:S(2)}) collective-permute-start(f32[273]{0:T(512)S(1)} %pad_maximum_fusion.3), channel_id=1, source_target_pairs={{0,0},{1,16},{2,1},{3,17},{4,2},{5,18},{6,3},{7,19},{8,4},{9,20},{... | collective-permute-start | bytes 3284 | tf_op jit(solution)/shard_map/ppermute | solution.py:56
Sparse Core Ops, SparseCore 0:
  17.0 108.3 all-gather.2
  147.8 29.1 reduce-scatter.2
  179.5 89.4 reduce-scatter.4

commit v5 on v4

--- a/solution.py
+++ b/solution.py
@@ -31,29 +31,25 @@
     denominator = own_energy + owner_energy - vir_energy[:, None] - near_energy[None, :]
     part_rows = jnp.sum(summed * summed / denominator, axis=1)
 
-    total = jnp.sum(part_rows)
-    pieces = part_rows.reshape(nc, ny // 2, 2, blk)
-    for axis, bit, step, size in (("core", c, 1, nc), ("y", y // 2, 2, ny), ("y", y % 2, 1, ny)):
-        keep = lax.dynamic_index_in_dim(pieces, bit, 0, keepdims=False)
-        give = lax.dynamic_index_in_dim(pieces, 1 - bit, 0, keepdims=False)
-        flip = [(k, k ^ step) for k in range(size)]
-        got = lax.ppermute(jnp.concatenate([give.reshape(-1), total[None]]), axis, flip)
-        pieces = keep + got[:-1].reshape(keep.shape)
-        total = total + got[-1]
-    rows = pieces.reshape(blk)
+    nb = nc * ny
+    part_total = jnp.sum(part_rows)
 
     def index(ll, cc, yy, hh):
         return ((ll * nc + cc) * ny + yy) * nh + hh
 
-    moves = []
-    for ll in range(nl):
-        for cc in range(nc):
-            for yy in range(ny):
-                for hh in range(nh):
-                    b = cc * ny + yy
-                    moves.append((index(ll, cc, yy, hh), index(hh, ll, b // nh, b % nh)))
-    packed = jnp.concatenate([rows, total[None]])
-    packed = lax.ppermute(packed, ("xl", "core", "y", "xh"), moves)
+    got = []
+    for k in range(nb):
+        moves = []
+        for ll in range(nl):
+            for cc in range(nc):
+                for yy in range(ny):
+                    for hh in range(nh):
+                        x = (cc * ny + yy + k) % nb
+                        moves.append((index(ll, cc, yy, hh), index(hh, ll, x // nh, x % nh)))
+        piece = lax.dynamic_slice_in_dim(part_rows, ((block + k) % nb) * blk, blk)
+        packed = jnp.concatenate([piece, part_total[None]])
+        got.append(lax.ppermute(packed, ("xl", "core", "y", "xh"), moves))
+    packed = sum(got[1:], got[0])
     return packed[:blk].reshape(1, 1, blk), packed[blk:].reshape(1, 1)
 
 

time: 305 us -> 320 us (1.049)
  starting transfers between devices: 7.73 us -> 27.3 us
  waiting for transfers between devices: 156 us -> 148 us
  other arithmetic: 4.28 us -> 9.08 us
    ppermute x4 -> x8, starting transfers between devices: 7.61 us -> 27.2 us  [per_device(): got.append(lax.ppermute(packed, ('xl', 'core', 'y', 'xh'), moves))]
    ppermute x4 -> x8, waiting for transfers between devices: 11.7 us -> 4.27 us  [per_device(): got.append(lax.ppermute(packed, ('xl', 'core', 'y', 'xh'), moves))]
    concatenate x4 -> x8, other arithmetic: 0.96 us -> 5.76 us  [per_device(): packed = jnp.concatenate([piece, part_total[None]])]
  transfers between devices with their start and end apart: 7 -> 11, of which waited for: 7 -> 5; matrix products, arithmetic and copies ran while one was open for 0% -> 2% of each run, Pallas kernels for 0% -> 0%
where the time goes in v5:
time: 320 us; the launch traced here: 318 us
  waiting for transfers between devices  148 us (46%)
  blocking collectives  83.5 us (26%)
  starting transfers between devices  27.3 us (9%)
  matrix products  22.3 us (7%)
  between operations  16.7 us (5%)
  local copies, waits for them, and re-layouts  10.2 us (3%)
  other arithmetic  9.08 us (3%)
    reduce_scatter x1, waiting for transfers between devices, per_device(): summed = lax.psum_scatter(summed, 'y', scatter_dimension=1, tiled=True)  89.8 us
    all_to_all x1, blocking collectives, per_device(): left = lax.all_to_all(integrals, GROUP, 1, 0, tiled=True)[:, 0, :]  83.5 us
    reduce_scatter x1, waiting for transfers between devices, per_device(): lax.psum_scatter(partial_sum, 'core', scatter_dimension=1, tiled=True)  29.3 us
    ppermute x8, starting transfers between devices, per_device(): got.append(lax.ppermute(packed, ('xl', 'core', 'y', 'xh'), moves))  27.2 us
    all_gather x1, waiting for transfers between devices, per_device(): panel = lax.all_gather(column, GROUP, axis=0, tiled=True)  25 us
    dot_general x1, matrix products, per_device(): lax.dot_general(left, panel, (((0,), (0,)), ((), ())), preferred_element_...  22.3 us
    unnamed x7, local copies, waits for them, and re-layouts  6.52 us
  transfers between devices with their start and end apart: 11, of which 5 were waited for; matrix products, arithmetic and copies ran while one was open for 2% of the time, Pallas kernels for 0%

profile of v5, /device:TPU:12, one launch (start us, length us, event | category | flops | bytes accessed | tf_op | source)
XLA Modules:
  0.0 317.6 jit_solution(4484921156300594656)
XLA Ops:
  7.2 0.0 all-gather.3.cloned.1.call-start
  8.5 0.0 copy-start.2
  8.5 6.5 %copy.6 = bf16[88,16,2176]{2,0,1:T(8,128)(2,1)} copy(bf16[88,16,2176]{2,1,0:T(8,128)(2,1)} %param.4) | data formatting | bytes 12255232 | tf_op args[0]
  15.0 0.0 copy-done.2
  15.1 1.8 constant_dynamic-slice_fusion
  16.8 0.0 all-gather.3.cloned.1.call-update
  16.9 0.0 reduce-scatter.3.cloned.1.call-start
  16.9 83.5 %all_to_all.15 = bf16[88,16,2176]{2,0,1:T(8,128)(2,1)} all-to-all(bf16[88,16,2176]{2,0,1:T(8,128)(2,1)} %copy.6), channel_id=1, replica_groups=mesh['z'=4,'xl'=2,'core'=2,'y'=4,'xh'=2] {'z','xh','xl'}, dimensions={1} | all-to-all | bytes 12255232 | tf_op jit(solution)/shard_map/all_to_all | solution.py:17
  100.4 25.0 %all-gather.3.cloned.1.call-done = bf16[1408,1,2176]{2,0,1:T(8,128)(2,1)} async-done(((bf16[88,1,2176]{2,0,1:T(8,128)(2,1)}), bf16[1408,1,2176]{2,0,1:T(8,128)(2,1)}) %all-gather.3.cloned.1.call-update) | async-done | bytes 6127632 | tf_op jit(solution)/shard_map/all_gather | solution.py:20
  125.4 22.3 %convolution_bitcast_fusion = f32[2176,2176]{0,1:T(8,128)} fusion(bf16[1408,2176]{1,0:T(8,128)(2,1)} %bitcast.17, bf16[1408,1,2176]{2,0,1:T(8,128)(2,1)} %all-gather.3.cloned.1.call-done), kind=kOutput, calls=%fused_computation | convolution fusion | flops 13333692416 | bytes 31195136 | tf_op jit(solution)/shard_map/dot_general | solution.py:22
  147.8 0.0 reduce-scatter.3.cloned.1.call-update
  147.8 0.0 copy-start
  147.8 0.0 copy-start.1
  147.8 0.0 reduce-scatter.5.cloned.1.call-start
  147.9 29.3 %reduce-scatter.3.cloned.1.call-done = f32[2176,1088]{0,1:T(8,128)} async-done(((f32[2176,2176]{0,1:T(8,128)}), f32[2176,1088]{0,1:T(8,128)}) %reduce-scatter.3.cloned.1.call-update) | async-done | bytes 9469968 | tf_op jit(solution)/shard_map/reduce_scatter | solution.py:25
  177.1 0.0 reduce-scatter.5.cloned.1.call-update
  177.3 0.1 dynamic_slice.41
  177.3 0.0 copy-done.1
  177.3 0.6 fusion.4
  179.3 89.8 %reduce-scatter.5.cloned.1.call-done = f32[2176,272]{0,1:T(8,128)} async-done(((f32[2176,1088]{0,1:T(8,128)}), f32[2176,272]{0,1:T(8,128)}) %reduce-scatter.5.cloned.1.call-update) | async-done | bytes 2367504 | tf_op jit(solution)/shard_map/reduce_scatter | solution.py:26
  269.1 3.3 %fusion.2 = (f32[2176]{0:T(1024)S(1)}, f32[]{:T(128)}) fusion(f32[272]{0:T(512)S(1)} %dynamic_slice.41, f32[2176]{0:T(1024)S(1)} %broadcast_subtract_fusion, f32[2176,272]{0,1:T(8,128)} %reduce-scatter.5.cloned.1.call-done), kind=kLoop, calls=%fused_computation.4 | loop fusion | flops 2957183 | bytes 2385988 | tf_op jit(solution)/shard_map/reduce_sum | solution.py:32
  272.4 0.1 fusion.3
  272.5 0.7 pad_maximum_fusion
  273.2 3.7 %collective-permute-start.7 = (f32[273]{0:T(512)S(1)}, f32[273]{0:T(512)S(1)}, u32[]{:S(2)}, u32[]{:S(2)}) collective-permute-start(f32[273]{0:T(512)S(1)} %pad_maximum_fusion), channel_id=1, source_target_pairs={{0,7},{1,23},{2,0},{3,16},{4,1},{5,17},{6,2},{7,18},{8,3},{9,19},{... | collective-permute-start | bytes 3284 | tf_op jit(solution)/shard_map/ppermute | solution.py:51
  276.9 0.7 pad_maximum_fusion.1
  277.7 4.5 %collective-permute-start.6 = (f32[273]{0:T(512)S(1)}, f32[273]{0:T(512)S(1)}, u32[]{:S(2)}, u32[]{:S(2)}) collective-permute-start(f32[273]{0:T(512)S(1)} %pad_maximum_fusion.1), channel_id=1, source_target_pairs={{0,6},{1,22},{2,7},{3,23},{4,0},{5,16},{6,1},{7,17},{8,2},{9,18},{... | collective-permute-start | bytes 3284 | tf_op jit(solution)/shard_map/ppermute | solution.py:51
  282.2 0.7 pad_maximum_fusion.2
  282.9 2.8 collective-permute-start.5
  285.7 0.7 pad_maximum_fusion.3
  286.4 0.0 collective-permute-start.4
  286.5 0.7 pad_maximum_fusion.4
  287.2 4.8 %collective-permute-start.3 = (f32[273]{0:T(512)S(1)}, f32[273]{0:T(512)S(1)}, u32[]{:S(2)}, u32[]{:S(2)}) collective-permute-start(f32[273]{0:T(512)S(1)} %pad_maximum_fusion.4), channel_id=1, source_target_pairs={{0,3},{1,19},{2,4},{3,20},{4,5},{5,21},{6,6},{7,22},{8,7},{9,23},{... | collective-permute-start | bytes 3284 | tf_op jit(solution)/shard_map/ppermute | solution.py:51
  292.0 0.7 pad_maximum_fusion.5
  292.7 0.7 pad_maximum_fusion.7
  293.4 0.7 pad_maximum_fusion.6
  294.2 0.0 collective-permute-done.7
  294.2 3.5 %collective-permute-start.2 = (f32[273]{0:T(512)S(1)}, f32[273]{0:T(512)S(1)}, u32[]{:S(2)}, u32[]{:S(2)}) collective-permute-start(f32[273]{0:T(512)S(1)} %pad_maximum_fusion.5), channel_id=1, source_target_pairs={{0,2},{1,18},{2,3},{3,19},{4,4},{5,20},{6,5},{7,21},{8,6},{9,22},{... | collective-permute-start | bytes 3284 | tf_op jit(solution)/shard_map/ppermute | solution.py:51
  297.7 0.0 collective-permute-done.6
  297.7 4.3 %collective-permute-start = (f32[273]{0:T(512)S(1)}, f32[273]{0:T(512)S(1)}, u32[]{:S(2)}, u32[]{:S(2)}) collective-permute-start(f32[273]{0:T(512)S(1)} %pad_maximum_fusion.7), channel_id=1, source_target_pairs={{0,0},{1,16},{2,1},{3,17},{4,2},{5,18},{6,3},{7,19},{8,4},{9,20},{... | collective-permute-start | bytes 3284 | tf_op jit(solution)/shard_map/ppermute | solution.py:51
  302.0 0.0 collective-permute-done.5
  302.0 3.6 %collective-permute-start.1 = (f32[273]{0:T(512)S(1)}, f32[273]{0:T(512)S(1)}, u32[]{:S(2)}, u32[]{:S(2)}) collective-permute-start(f32[273]{0:T(512)S(1)} %pad_maximum_fusion.6), channel_id=1, source_target_pairs={{0,1},{1,17},{2,2},{3,18},{4,3},{5,19},{6,4},{7,20},{8,5},{9,21},{... | collective-permute-start | bytes 3284 | tf_op jit(solution)/shard_map/ppermute | solution.py:51
  305.6 0.0 collective-permute-done.4
  305.6 0.0 collective-permute-done.3
  305.6 0.0 collective-permute-done.2
  305.6 1.5 collective-permute-done
  307.1 2.8 collective-permute-done.1
  309.9 0.6 slice.11
  310.5 0.6 reshape.15
  (3 shorter events, 0.0 us)
Async XLA Ops:
  7.2 118.3 %all-gather.3.cloned.1.call-start = ((), (), s32[]{:S(2)}) async-start(), calls=%async_computation.5 | async-start | bytes 6510592 | tf_op jit(solution)/shard_map/all_gather | solution.py:20
  8.5 6.5 %copy-start.2 = (s32[16]{0:T(128)S(1)}, s32[16]{0:T(128)}, u32[]{:S(2)}) copy-start(s32[16]{0:T(128)} %param.5) | copy-start | bytes 196
  16.9 160.2 %reduce-scatter.3.cloned.1.call-start = ((), (), s32[]{:S(2)}) async-start(), calls=%async_computation.3 | async-start | bytes 28409856 | tf_op jit(solution)/shard_map/reduce_scatter | solution.py:25
  147.8 29.5 %copy-start = (f32[2176]{0:T(1024)S(1)}, f32[2176]{0:T(1024)}, u32[]{:S(2)}) copy-start(f32[2176]{0:T(1024)} %param.7) | copy-start | bytes 26116
  147.8 29.5 %copy-start.1 = (f32[16]{0:T(128)S(1)}, f32[16]{0:T(128)}, u32[]{:S(2)}) copy-start(f32[16]{0:T(128)} %param.6) | copy-start | bytes 196
  147.8 121.3 %reduce-scatter.5.cloned.1.call-start = ((), (), s32[]{:S(2)}) async-start(), calls=%async_computation.4 | async-start | bytes 11837440 | tf_op jit(solution)/shard_map/reduce_scatter | solution.py:26
  273.2 20.9 %collective-permute-start.7 = (f32[273]{0:T(512)S(1)}, f32[273]{0:T(512)S(1)}, u32[]{:S(2)}, u32[]{:S(2)}) collective-permute-start(f32[273]{0:T(512)S(1)} %pad_maximum_fusion), channel_id=1, source_target_pairs={{0,7},{1,23},{2,0},{3,16},{4,1},{5,17},{6,2},{7,18},{8,3},{9,19},{... | collective-permute-start | bytes 3284 | tf_op jit(solution)/shard_map/ppermute | solution.py:51
  277.7 20.0 %collective-permute-start.6 = (f32[273]{0:T(512)S(1)}, f32[273]{0:T(512)S(1)}, u32[]{:S(2)}, u32[]{:S(2)}) collective-permute-start(f32[273]{0:T(512)S(1)} %pad_maximum_fusion.1), channel_id=1, source_target_pairs={{0,6},{1,22},{2,7},{3,23},{4,0},{5,16},{6,1},{7,17},{8,2},{9,18},{... | collective-permute-start | bytes 3284 | tf_op jit(solution)/shard_map/ppermute | solution.py:51
  282.9 19.1 %collective-permute-start.5 = (f32[273]{0:T(512)S(1)}, f32[273]{0:T(512)S(1)}, u32[]{:S(2)}, u32[]{:S(2)}) collective-permute-start(f32[273]{0:T(512)S(1)} %pad_maximum_fusion.2), channel_id=1, source_target_pairs={{0,5},{1,21},{2,6},{3,22},{4,7},{5,23},{6,0},{7,16},{8,1},{9,17},{... | collective-permute-start | bytes 3284 | tf_op jit(solution)/shard_map/ppermute | solution.py:51
  286.4 19.1 %collective-permute-start.4 = (f32[273]{0:T(512)S(1)}, f32[273]{0:T(512)S(1)}, u32[]{:S(2)}, u32[]{:S(2)}) collective-permute-start(f32[273]{0:T(512)S(1)} %pad_maximum_fusion.3), channel_id=1, source_target_pairs={{0,4},{1,20},{2,5},{3,21},{4,6},{5,22},{6,7},{7,23},{8,0},{9,16},{... | collective-permute-start | bytes 3284 | tf_op jit(solution)/shard_map/ppermute | solution.py:51
  287.2 18.4 %collective-permute-start.3 = (f32[273]{0:T(512)S(1)}, f32[273]{0:T(512)S(1)}, u32[]{:S(2)}, u32[]{:S(2)}) collective-permute-start(f32[273]{0:T(512)S(1)} %pad_maximum_fusion.4), channel_id=1, source_target_pairs={{0,3},{1,19},{2,4},{3,20},{4,5},{5,21},{6,6},{7,22},{8,7},{9,23},{... | collective-permute-start | bytes 3284 | tf_op jit(solution)/shard_map/ppermute | solution.py:51
  294.2 11.4 %collective-permute-start.2 = (f32[273]{0:T(512)S(1)}, f32[273]{0:T(512)S(1)}, u32[]{:S(2)}, u32[]{:S(2)}) collective-permute-start(f32[273]{0:T(512)S(1)} %pad_maximum_fusion.5), channel_id=1, source_target_pairs={{0,2},{1,18},{2,3},{3,19},{4,4},{5,20},{6,5},{7,21},{8,6},{9,22},{... | collective-permute-start | bytes 3284 | tf_op jit(solution)/shard_map/ppermute | solution.py:51
  297.7 9.4 %collective-permute-start = (f32[273]{0:T(512)S(1)}, f32[273]{0:T(512)S(1)}, u32[]{:S(2)}, u32[]{:S(2)}) collective-permute-start(f32[273]{0:T(512)S(1)} %pad_maximum_fusion.7), channel_id=1, source_target_pairs={{0,0},{1,16},{2,1},{3,17},{4,2},{5,18},{6,3},{7,19},{8,4},{9,20},{... | collective-permute-start | bytes 3284 | tf_op jit(solution)/shard_map/ppermute | solution.py:51
  302.0 7.9 %collective-permute-start.1 = (f32[273]{0:T(512)S(1)}, f32[273]{0:T(512)S(1)}, u32[]{:S(2)}, u32[]{:S(2)}) collective-permute-start(f32[273]{0:T(512)S(1)} %pad_maximum_fusion.6), channel_id=1, source_target_pairs={{0,1},{1,17},{2,2},{3,18},{4,3},{5,19},{6,4},{7,20},{8,5},{9,21},{... | collective-permute-start | bytes 3284 | tf_op jit(solution)/shard_map/ppermute | solution.py:51
Sparse Core Ops, SparseCore 0:
  17.0 108.3 all-gather.2
  147.9 29.1 reduce-scatter.2
  179.6 89.4 reduce-scatter.4

commit v6 on v4

--- a/solution.py
+++ b/solution.py
@@ -4,6 +4,7 @@
 from jax.sharding import Mesh, PartitionSpec as P
 
 GROUP = ("z", "xh", "xl")
+CHUNKS = 2
 
 
 def per_device(integrals, owner_order, occ_energy, vir_energy):
@@ -19,17 +20,26 @@
     column = lax.dynamic_index_in_dim(integrals, owner, 1, keepdims=False)
     panel = lax.all_gather(column, GROUP, axis=0, tiled=True)
 
-    partial_sum = lax.dot_general(
-        left, panel, (((0,), (0,)), ((), ())), preferred_element_type=jnp.float32
-    )
-    summed = lax.psum_scatter(partial_sum, "core", scatter_dimension=1, tiled=True)
-    summed = lax.psum_scatter(summed, "y", scatter_dimension=1, tiled=True)
-
     near_energy = lax.dynamic_slice_in_dim(vir_energy, block * blk, blk)
     own_energy = lax.dynamic_index_in_dim(occ_energy, orbital, 0, keepdims=False)
     owner_energy = lax.dynamic_index_in_dim(occ_energy, owner, 0, keepdims=False)
-    denominator = own_energy + owner_energy - vir_energy[:, None] - near_energy[None, :]
-    part_rows = jnp.sum(summed * summed / denominator, axis=1)
+    half = nvir // nc
+    flip = [(k, k ^ 1) for k in range(nc)]
+
+    lanes = nvir // 128
+    cuts = [0] + [lanes * k // CHUNKS * 128 for k in range(1, CHUNKS)] + [nvir]
+    part_rows = []
+    for lo, hi in zip(cuts[:-1], cuts[1:]):
+        partial_sum = lax.dot_general(
+            left[:, lo:hi], panel, (((0,), (0,)), ((), ())), preferred_element_type=jnp.float32
+        )
+        keep = lax.dynamic_slice_in_dim(partial_sum, c * half, half, axis=1)
+        give = lax.dynamic_slice_in_dim(partial_sum, (1 - c) * half, half, axis=1)
+        summed = keep + lax.ppermute(give, "core", flip)
+        summed = lax.psum_scatter(summed, "y", scatter_dimension=1, tiled=True)
+        denominator = own_energy + owner_energy - vir_energy[lo:hi, None] - near_energy[None, :]
+        part_rows.append(jnp.sum(summed * summed / denominator, axis=1))
+    part_rows = jnp.concatenate(part_rows)
 
     total = jnp.sum(part_rows)
     pieces = part_rows.reshape(nc, ny // 2, 2, blk)

time: 305 us -> 316 us (1.036)
  blocking collectives: 83.5 us -> 0 us
  waiting for transfers between devices: 156 us -> 221 us
  other arithmetic: 4.28 us -> 15.1 us
  starting transfers between devices: 7.73 us -> 16.4 us
  local copies, waits for them, and re-layouts: 12.3 us -> 19.4 us
    all_to_all x0 -> x1, waiting for transfers between devices: none -> 103 us  [per_device(): left = lax.all_to_all(integrals, GROUP, 1, 0, tiled=True)[:, 0, :]]
    all_to_all x1 -> x0, blocking collectives: 83.5 us -> none  [per_device(): left = lax.all_to_all(integrals, GROUP, 1, 0, tiled=True)[:, 0, :]]
    reduce_scatter x1 -> x0, waiting for transfers between devices: 29.3 us -> none  [per_device(): lax.psum_scatter(partial_sum, 'core', scatter_dimension=1, tiled=True)]
    ppermute x0 -> x2, waiting for transfers between devices: none -> 16.1 us  [per_device(): summed = keep + lax.ppermute(give, 'core', flip)]
    reduce_scatter x1 -> x2, waiting for transfers between devices: 90 us -> 76.7 us  [per_device(): summed = lax.psum_scatter(summed, 'y', scatter_dimension=1, tiled=True)]
    all_gather x1, waiting for transfers between devices: 25 us -> 13.8 us  [per_device(): panel = lax.all_gather(column, GROUP, axis=0, tiled=True)]
    add x0 -> x2, other arithmetic: none -> 9.91 us  [per_device(): summed = keep + lax.ppermute(give, 'core', flip)]
    all_to_all x0 -> x1, starting transfers between devices: none -> 8.3 us  [per_device(): left = lax.all_to_all(integrals, GROUP, 1, 0, tiled=True)[:, 0, :]]
  transfers between devices with their start and end apart: 7 -> 10, of which waited for: 7 -> 10; matrix products, arithmetic and copies ran while one was open for 0% -> 6% of each run, Pallas kernels for 0% -> 0%
where the time goes in v6:
time: 316 us; the launch traced here: 315 us
  waiting for transfers between devices  221 us (70%)
  matrix products  23.3 us (7%)
  between operations  19.8 us (6%)
  local copies, waits for them, and re-layouts  19.4 us (6%)
  starting transfers between devices  16.4 us (5%)
  other arithmetic  15.1 us (5%)
    all_to_all x1, waiting for transfers between devices, per_device(): left = lax.all_to_all(integrals, GROUP, 1, 0, tiled=True)[:, 0, :]  103 us
    reduce_scatter x2, waiting for transfers between devices, per_device(): summed = lax.psum_scatter(summed, 'y', scatter_dimension=1, tiled=True)  76.7 us
    dot_general x2, matrix products, per_device(): lax.dot_general(left[:, lo:hi], panel, (((0,), (0,)), ((), ())), preferre...  23.3 us
    ppermute x2, waiting for transfers between devices, per_device(): summed = keep + lax.ppermute(give, 'core', flip)  16.1 us
    all_gather x1, waiting for transfers between devices, per_device(): panel = lax.all_gather(column, GROUP, axis=0, tiled=True)  13.8 us
    unnamed x9, local copies, waits for them, and re-layouts  10.6 us
    add x2, other arithmetic, per_device(): summed = keep + lax.ppermute(give, 'core', flip)  9.91 us
    all_to_all x1, starting transfers between devices, per_device(): left = lax.all_to_all(integrals, GROUP, 1, 0, tiled=True)[:, 0, :]  8.3 us
  transfers between devices with their start and end apart: 10, of which 10 were waited for; matrix products, arithmetic and copies ran while one was open for 6% of the time, Pallas kernels for 0%

profile of v6, /device:TPU:12, one launch (start us, length us, event | category | flops | bytes accessed | tf_op | source)
XLA Modules:
  0.0 315.5 jit_solution(4790278846636391092)
XLA Ops:
  7.2 0.0 all-gather.3.cloned.1.call-start
  8.5 6.5 %copy.6 = bf16[88,16,2176]{2,0,1:T(8,128)(2,1)} copy(bf16[88,16,2176]{2,1,0:T(8,128)(2,1)} %param.4) | data formatting | bytes 12255232 | tf_op args[0]
  15.1 1.8 constant_dynamic-slice_fusion.4
  16.8 0.0 all-gather.3.cloned.1.call-update
  16.9 8.3 %all-to-all-start = ((bf16[88,16,2176]{2,0,1:T(8,128)(2,1)}), bf16[88,16,2176]{2,0,1:T(8,128)(2,1)}, u32[]{:S(2)}, u32[]{:S(2)}) async-start(bf16[88,16,2176]{2,0,1:T(8,128)(2,1)} %copy.6), calls=%async_computation | async-start | bytes 12255232 | tf_op jit(solution)/shard_map/all_to_all | solution.py:18
  25.2 0.0 reduce-scatter.3.cloned.1.call-start
  25.2 103.2 %all-to-all-done = bf16[88,16,2176]{2,0,1:T(8,128)(2,1)} async-done(((bf16[88,16,2176]{2,0,1:T(8,128)(2,1)}), bf16[88,16,2176]{2,0,1:T(8,128)(2,1)}, u32[]{:S(2)}, u32[]{:S(2)}) %all-to-all-start) | async-done | bytes 6127648 | tf_op jit(solution)/shard_map/all_to_all | solution.py:18
  128.4 13.8 %all-gather.3.cloned.1.call-done = bf16[1408,1,2176]{2,0,1:T(8,128)(2,1)} async-done(((bf16[88,1,2176]{2,0,1:T(8,128)(2,1)}), bf16[1408,1,2176]{2,0,1:T(8,128)(2,1)}) %all-gather.3.cloned.1.call-update) | async-done | bytes 6127632 | tf_op jit(solution)/shard_map/all_gather | solution.py:21
  142.2 10.9 %fusion.2 = f32[2176,1024]{1,0:T(8,128)S(1)} fusion(bf16[1408,1,2176]{2,0,1:T(8,128)(2,1)} %all-gather.3.cloned.1.call-done, bf16[1408,2176]{1,0:T(8,128)(2,1)} %bitcast.4), kind=kOutput, calls=%fused_computation.2 | convolution fusion | flops 6274678784 | bytes 17924096 | tf_op jit(solution)/shard_map/dot_general | solution.py:33
  153.1 3.4 %copy-done = f32[2176,1024]{1,0:T(8,128)} copy-done((f32[2176,1024]{1,0:T(8,128)}, f32[2176,1024]{1,0:T(8,128)S(1)}, u32[]{:S(2)}) %copy-start) | copy-done | bytes 8912920
  156.5 2.7 dynamic-slice_bitcast_fusion.1
  159.2 7.9 %collective-permute-done = f32[1024,1088]{0,1:T(8,128)} collective-permute-done((f32[1024,1088]{0,1:T(8,128)}, f32[1024,1088]{0,1:T(8,128)}, u32[]{:S(2)}, u32[]{:S(2)}) %collective-permute-start) | collective-permute-done | bytes 4456480 | tf_op jit(solution)/shard_map/ppermute | solution.py:38
  167.1 7.2 %bitcast_add_fusion.1 = f32[1024,1088]{0,1:T(8,128)} fusion(f32[1024,1088]{0,1:T(8,128)} %collective-permute-done, f32[2176,1024]{1,0:T(8,128)} %copy-done, s32[]{:T(128)S(6)} %select_n.53), kind=kLoop, calls=%fused_computation.6 | loop fusion | flops 1114112 | bytes 13369348 | tf_op jit(solution)/shard_map/add | solution.py:38
  174.3 0.2 reduce-scatter.5.cloned.1.call-start
  174.5 12.5 %fusion = f32[2176,1152]{1,0:T(8,128)S(1)} fusion(bf16[1408,1,2176]{2,0,1:T(8,128)(2,1)} %all-gather.3.cloned.1.call-done, bf16[1408,2176]{1,0:T(8,128)(2,1)} %bitcast.4), kind=kOutput, calls=%fused_computation | convolution fusion | flops 7059013632 | bytes 19398656 | tf_op jit(solution)/shard_map/dot_general | solution.py:33
  187.0 0.3 dynamic-slice_bitcast_fusion
  187.3 0.2 collective-permute-start.1
  187.6 8.2 %collective-permute-done.1 = f32[1152,1088]{0,1:T(8,128)S(1)} collective-permute-done((f32[1152,1088]{0,1:T(8,128)S(1)}, f32[1152,1088]{0,1:T(8,128)S(1)}, u32[]{:S(2)}, u32[]{:S(2)}) %collective-permute-start.1) | collective-permute-done | bytes 5013536 | tf_op jit(solution)/shard_map/ppermute | solution.py:38
  195.8 2.7 bitcast_add_fusion
  198.5 0.7 copy-done.1
  199.2 0.1 dynamic_slice.52
  199.3 0.6 fusion.12
  201.2 23.3 %reduce-scatter.3.cloned.1.call-done = f32[1024,272]{0,1:T(8,128)} async-done(((f32[1024,1088]{0,1:T(8,128)}), f32[1024,272]{0,1:T(8,128)}) %reduce-scatter.3.cloned.1.call-update) | async-done | bytes 1114128 | tf_op jit(solution)/shard_map/reduce_scatter | solution.py:39
  224.5 2.3 fusion.9
  226.8 53.4 %reduce-scatter.5.cloned.1.call-done = f32[1152,272]{0,1:T(8,128)} async-done(((f32[1152,1088]{0,1:T(8,128)}), f32[1152,272]{0,1:T(8,128)}) %reduce-scatter.5.cloned.1.call-update) | async-done | bytes 1253392 | tf_op jit(solution)/shard_map/reduce_scatter | solution.py:39
  280.2 2.5 fusion.7
  282.7 0.1 reshape.34
  282.8 0.1 reshape.35
  284.2 0.1 pad_maximum_fusion.1
  284.3 0.0 collective-permute-start.2
  284.3 1.1 collective-permute-done.2
  285.5 0.6 slice.55
  286.7 0.1 reshape.36
  286.8 0.1 reshape.37
  286.9 0.1 pad_maximum_fusion.2
  287.0 1.5 collective-permute-start.3
  288.4 3.6 %collective-permute-done.3 = f32[545]{0:T(1024)S(1)} collective-permute-done((f32[545]{0:T(1024)S(1)}, f32[545]{0:T(1024)S(1)}, u32[]{:S(2)}, u32[]{:S(2)}) %collective-permute-start.3) | collective-permute-done | bytes 2212 | tf_op jit(solution)/shard_map/ppermute | solution.py:50
  292.1 0.6 slice.47
  293.3 0.1 reshape.38
  293.4 0.1 pad_maximum_fusion.3
  293.5 1.8 collective-permute-start.4
  295.3 1.8 collective-permute-done.4
  297.1 0.6 slice.49
  298.4 0.1 pad_maximum_fusion.4
  298.4 4.3 %collective-permute-start.5 = (f32[273]{0:T(512)S(1)}, f32[273]{0:T(512)S(1)}, u32[]{:S(2)}, u32[]{:S(2)}) collective-permute-start(f32[273]{0:T(512)S(1)} %pad_maximum_fusion.4), channel_id=1, source_target_pairs={{0,0},{1,16},{2,1},{3,17},{4,2},{5,18},{6,3},{7,19},{8,4},{9,20},{... | collective-permute-start | bytes 3284 | tf_op jit(solution)/shard_map/ppermute | solution.py:66
  302.7 5.1 %collective-permute-done.5 = f32[273]{0:T(512)S(1)} collective-permute-done((f32[273]{0:T(512)S(1)}, f32[273]{0:T(512)S(1)}, u32[]{:S(2)}, u32[]{:S(2)}) %collective-permute-start.5) | collective-permute-done | bytes 1124 | tf_op jit(solution)/shard_map/ppermute | solution.py:66
  307.8 0.6 reshape.39
  308.4 0.6 slice.51
  (18 shorter events, 0.1 us)
Async XLA Ops:
  7.2 135.0 %all-gather.3.cloned.1.call-start = ((), (), s32[]{:S(2)}) async-start(), calls=%async_computation.5 | async-start | bytes 6510592 | tf_op jit(solution)/shard_map/all_gather | solution.py:21
  8.5 6.5 %copy-start.3 = (s32[16]{0:T(128)S(1)}, s32[16]{0:T(128)}, u32[]{:S(2)}) copy-start(s32[16]{0:T(128)} %param.5) | copy-start | bytes 196
  16.9 111.5 %all-to-all-start = ((bf16[88,16,2176]{2,0,1:T(8,128)(2,1)}), bf16[88,16,2176]{2,0,1:T(8,128)(2,1)}, u32[]{:S(2)}, u32[]{:S(2)}) async-start(bf16[88,16,2176]{2,0,1:T(8,128)(2,1)} %copy.6), calls=%async_computation | async-start | bytes 12255232 | tf_op jit(solution)/shard_map/all_to_all | solution.py:18
  25.2 199.3 %reduce-scatter.3.cloned.1.call-start = ((), (), s32[]{:S(2)}) async-start(), calls=%async_computation.3 | async-start | bytes 5570560 | tf_op jit(solution)/shard_map/reduce_scatter | solution.py:39
  153.1 3.4 %copy-start = (f32[2176,1024]{1,0:T(8,128)}, f32[2176,1024]{1,0:T(8,128)S(1)}, u32[]{:S(2)}) copy-start(f32[2176,1024]{1,0:T(8,128)S(1)} %fusion.2) | copy-start | bytes 26738692
  159.2 7.9 %collective-permute-start = (f32[1024,1088]{0,1:T(8,128)}, f32[1024,1088]{0,1:T(8,128)}, u32[]{:S(2)}, u32[]{:S(2)}) collective-permute-start(f32[1024,1088]{0,1:T(8,128)} %dynamic-slice_bitcast_fusion.1), channel_id=1, source_target_pairs={{0,8},{8,0},{1,9},{9,1},{2,10},{10,2},{3,11},{11,3},{4,12},{12,4},... | collective-permute-start | bytes 13369352 | tf_op jit(solution)/shard_map/ppermute | solution.py:38
  174.3 105.9 %reduce-scatter.5.cloned.1.call-start = ((), (), s32[]{:S(2)}) async-start(), calls=%async_computation.4 | async-start | bytes 6266880 | tf_op jit(solution)/shard_map/reduce_scatter | solution.py:39
  187.3 8.4 %collective-permute-start.1 = (f32[1152,1088]{0,1:T(8,128)S(1)}, f32[1152,1088]{0,1:T(8,128)S(1)}, u32[]{:S(2)}, u32[]{:S(2)}) collective-permute-start(f32[1152,1088]{0,1:T(8,128)S(1)} %dynamic-slice_bitcast_fusion), channel_id=1, source_target_pairs={{0,8},{8,0},{1,9},{9,1},{2,10},{10,2},{3,11},{11,3},{4,12},{12,4},... | collective-permute-start | bytes 15040520 | tf_op jit(solution)/shard_map/ppermute | solution.py:38
  198.5 0.7 copy-start.1
  198.5 0.8 copy-start.2
  284.3 1.2 collective-permute-start.2
  287.0 5.1 %collective-permute-start.3 = (f32[545]{0:T(1024)S(1)}, f32[545]{0:T(1024)S(1)}, u32[]{:S(2)}, u32[]{:S(2)}) collective-permute-start(f32[545]{0:T(1024)S(1)} %pad_maximum_fusion.2), channel_id=1, source_target_pairs={{0,4},{2,6},{4,0},{6,2},{1,5},{3,7},{5,1},{7,3},{8,12},{10,14},{12... | collective-permute-start | bytes 6548 | tf_op jit(solution)/shard_map/ppermute | solution.py:50
  293.5 3.6 %collective-permute-start.4 = (f32[273]{0:T(512)S(1)}, f32[273]{0:T(512)S(1)}, u32[]{:S(2)}, u32[]{:S(2)}) collective-permute-start(f32[273]{0:T(512)S(1)} %pad_maximum_fusion.3), channel_id=1, source_target_pairs={{0,2},{2,0},{4,6},{6,4},{1,3},{3,1},{5,7},{7,5},{8,10},{10,8},{12,... | collective-permute-start | bytes 3284 | tf_op jit(solution)/shard_map/ppermute | solution.py:50
  298.4 9.4 %collective-permute-start.5 = (f32[273]{0:T(512)S(1)}, f32[273]{0:T(512)S(1)}, u32[]{:S(2)}, u32[]{:S(2)}) collective-permute-start(f32[273]{0:T(512)S(1)} %pad_maximum_fusion.4), channel_id=1, source_target_pairs={{0,0},{1,16},{2,1},{3,17},{4,2},{5,18},{6,3},{7,19},{8,4},{9,20},{... | collective-permute-start | bytes 3284 | tf_op jit(solution)/shard_map/ppermute | solution.py:66
Sparse Core Ops, SparseCore 0:
  17.0 125.1 all-gather.2
  174.4 50.0 reduce-scatter.2
  226.9 53.2 reduce-scatter.4

commit v7 on v4

--- a/solution.py
+++ b/solution.py
@@ -14,10 +14,11 @@
     orbital = (z * nh + h) * nl + l
     block = c * ny + y
 
-    left = lax.all_to_all(integrals, GROUP, 1, 0, tiled=True)[:, 0, :]
     owner = owner_order[0]
     column = lax.dynamic_index_in_dim(integrals, owner, 1, keepdims=False)
+    column, integrals = lax.optimization_barrier((column, integrals))
     panel = lax.all_gather(column, GROUP, axis=0, tiled=True)
+    left = lax.all_to_all(integrals, GROUP, 1, 0, tiled=True)[:, 0, :]
 
     partial_sum = lax.dot_general(
         left, panel, (((0,), (0,)), ((), ())), preferred_element_type=jnp.float32

time: 305 us -> 305 us (level)
    unnamed x7 -> x5, local copies, waits for them, and re-layouts: 6.52 us -> 0.79 us
    optimization_barrier x0 -> x1, local copies, waits for them, and re-layouts: none -> 3.9 us  [per_device(): column, integrals = lax.optimization_barrier((column, integrals))]
    all_gather x1, waiting for transfers between devices: 25 us -> 21.9 us  [per_device(): panel = lax.all_gather(column, GROUP, axis=0, tiled=True)]
  transfers between devices with their start and end apart: 7 -> 7, of which waited for: 7 -> 7; matrix products, arithmetic and copies ran while one was open for 0% -> 2% of each run, Pallas kernels for 0% -> 0%
where the time goes in v7:
time: 305 us; the launch traced here: 304 us
  waiting for transfers between devices  153 us (50%)
  blocking collectives  86.1 us (28%)
  matrix products  22.2 us (7%)
  between operations  19.7 us (6%)
  local copies, waits for them, and re-layouts  11.4 us (4%)
  starting transfers between devices  7.8 us (3%)
  other arithmetic  4.28 us (1%)
    reduce_scatter x1, waiting for transfers between devices, per_device(): summed = lax.psum_scatter(summed, 'y', scatter_dimension=1, tiled=True)  89.9 us
    all_to_all x1, blocking collectives, per_device(): left = lax.all_to_all(integrals, GROUP, 1, 0, tiled=True)[:, 0, :]  86.1 us
    reduce_scatter x1, waiting for transfers between devices, per_device(): lax.psum_scatter(partial_sum, 'core', scatter_dimension=1, tiled=True)  29.3 us
    dot_general x1, matrix products, per_device(): lax.dot_general(left, panel, (((0,), (0,)), ((), ())), preferred_element_...  22.2 us
    all_gather x1, waiting for transfers between devices, per_device(): panel = lax.all_gather(column, GROUP, axis=0, tiled=True)  21.9 us
    ppermute x3, waiting for transfers between devices, per_device(): lax.ppermute(jnp.concatenate([give.reshape(-1), total[None]]), axis, flip)  6.54 us
  transfers between devices with their start and end apart: 7, of which 7 were waited for; matrix products, arithmetic and copies ran while one was open for 2% of the time, Pallas kernels for 0%

profile of v7, /device:TPU:12, one launch (start us, length us, event | category | flops | bytes accessed | tf_op | source)
XLA Modules:
  0.0 304.3 jit_solution(16062863201023858518)
XLA Ops:
  7.2 0.0 all-gather.2.cloned.1.call-start
  9.1 2.7 constant_dynamic-slice_fusion.4
  11.8 0.8 copy.10
  12.6 0.0 all-gather.2.cloned.1.call-update
  12.6 0.0 reduce-scatter.3.cloned.1.call-start
  12.7 3.9 %copy.7 = bf16[88,16,2176]{2,0,1:T(8,128)(2,1)S(1)} copy(bf16[88,16,2176]{2,1,0:T(8,128)(2,1)} %param.4) | data formatting | bytes 12255232 | tf_op jit(solution)/shard_map/optimization_barrier | solution.py:19
  16.6 86.1 %all_to_all.15 = bf16[88,16,2176]{2,0,1:T(8,128)(2,1)} all-to-all(bf16[88,16,2176]{2,0,1:T(8,128)(2,1)S(1)} %copy.7), channel_id=1, replica_groups=mesh['z'=4,'xl'=2,'core'=2,'y'=4,'xh'=2] {'z','xh','xl'}, dimensions={1} | all-to-all | bytes 12255232 | tf_op jit(solution)/shard_map/all_to_all | solution.py:21
  102.7 21.9 %all-gather.2.cloned.1.call-done = bf16[1408,2176]{1,0:T(8,128)(2,1)} async-done(((bf16[88,2176]{1,0:T(8,128)(2,1)}), bf16[1408,2176]{1,0:T(8,128)(2,1)}) %all-gather.2.cloned.1.call-update) | async-done | bytes 6127632 | tf_op jit(solution)/shard_map/all_gather | solution.py:20
  124.6 22.2 %fusion.5 = f32[2176,2176]{0,1:T(8,128)} fusion(bf16[1408,2176]{1,0:T(8,128)(2,1)} %bitcast.28, bf16[1408,2176]{1,0:T(8,128)(2,1)} %all-gather.2.cloned.1.call-done), kind=kOutput, calls=%fused_computation.20 | convolution fusion | flops 13333692416 | bytes 31195136 | tf_op jit(solution)/shard_map/dot_general | solution.py:23
  146.8 0.0 reduce-scatter.3.cloned.1.call-update
  146.8 0.0 copy-start.1
  146.8 0.0 copy-start
  146.8 0.0 reduce-scatter.5.cloned.1.call-start
  146.9 29.3 %reduce-scatter.3.cloned.1.call-done = f32[2176,1088]{0,1:T(8,128)} async-done(((f32[2176,2176]{0,1:T(8,128)}), f32[2176,1088]{0,1:T(8,128)}) %reduce-scatter.3.cloned.1.call-update) | async-done | bytes 9469968 | tf_op jit(solution)/shard_map/reduce_scatter | solution.py:26
  176.2 0.0 reduce-scatter.5.cloned.1.call-update
  176.2 0.0 copy-done.1
  176.3 0.6 fusion.4
  178.2 0.0 copy-done
  178.2 0.1 dynamic_slice.38
  178.2 89.9 %reduce-scatter.5.cloned.1.call-done = f32[2176,272]{0,1:T(8,128)} async-done(((f32[2176,1088]{0,1:T(8,128)}), f32[2176,272]{0,1:T(8,128)}) %reduce-scatter.5.cloned.1.call-update) | async-done | bytes 2367504 | tf_op jit(solution)/shard_map/reduce_scatter | solution.py:27
  268.2 3.3 %fusion.1 = (f32[2176]{0:T(1024)S(1)}, f32[]{:T(128)}) fusion(f32[272]{0:T(512)S(1)} %dynamic_slice.38, f32[2176]{0:T(1024)S(1)} %broadcast_subtract_fusion, f32[2176,272]{0,1:T(8,128)} %reduce-scatter.5.cloned.1.call-done), kind=kLoop, calls=%fused_computation.3 | loop fusion | flops 2957183 | bytes 2385988 | tf_op jit(solution)/shard_map/reduce_sum | solution.py:33
  271.5 0.1 reshape.32
  271.6 0.1 reshape.33
  271.7 0.7 pad_maximum_fusion
  272.4 0.0 collective-permute-start
  272.4 1.1 collective-permute-done
  273.6 0.1 reshape.34
  273.7 0.1 reshape.35
  273.8 0.6 slice.37
  275.7 0.1 pad_maximum_fusion.1
  275.7 1.5 collective-permute-start.1
  277.2 3.6 %collective-permute-done.1 = f32[545]{0:T(1024)S(1)} collective-permute-done((f32[545]{0:T(1024)S(1)}, f32[545]{0:T(1024)S(1)}, u32[]{:S(2)}, u32[]{:S(2)}) %collective-permute-start.1) | collective-permute-done | bytes 2212 | tf_op jit(solution)/shard_map/ppermute | solution.py:41
  280.9 0.1 reshape.36
  280.9 0.6 slice.31
  282.2 0.1 pad_maximum_fusion.2
  282.3 1.8 collective-permute-start.2
  284.2 1.8 collective-permute-done.2
  285.9 0.6 slice.33
  287.2 0.1 pad_maximum_fusion.3
  287.2 4.3 %collective-permute-start.3 = (f32[273]{0:T(512)S(1)}, f32[273]{0:T(512)S(1)}, u32[]{:S(2)}, u32[]{:S(2)}) collective-permute-start(f32[273]{0:T(512)S(1)} %pad_maximum_fusion.3), channel_id=1, source_target_pairs={{0,0},{1,16},{2,1},{3,17},{4,2},{5,18},{6,3},{7,19},{8,4},{9,20},{... | collective-permute-start | bytes 3284 | tf_op jit(solution)/shard_map/ppermute | solution.py:57
  291.6 5.0 %collective-permute-done.3 = f32[273]{0:T(512)S(1)} collective-permute-done((f32[273]{0:T(512)S(1)}, f32[273]{0:T(512)S(1)}, u32[]{:S(2)}, u32[]{:S(2)}) %collective-permute-start.3) | collective-permute-done | bytes 1124 | tf_op jit(solution)/shard_map/ppermute | solution.py:57
  296.6 0.6 reshape.37
  297.2 0.6 slice.35
  (7 shorter events, 0.1 us)
Async XLA Ops:
  7.2 117.4 %all-gather.2.cloned.1.call-start = ((), (), s32[]{:S(2)}) async-start(), calls=%async_computation.3 | async-start | bytes 6510592 | tf_op jit(solution)/shard_map/all_gather | solution.py:20
  12.6 163.6 %reduce-scatter.3.cloned.1.call-start = ((), (), s32[]{:S(2)}) async-start(), calls=%async_computation.4 | async-start | bytes 28409856 | tf_op jit(solution)/shard_map/reduce_scatter | solution.py:26
  146.8 29.5 %copy-start.1 = (f32[16]{0:T(128)S(1)}, f32[16]{0:T(128)}, u32[]{:S(2)}) copy-start(f32[16]{0:T(128)} %param.6) | copy-start | bytes 196
  146.8 31.3 %copy-start = (f32[2176]{0:T(1024)S(1)}, f32[2176]{0:T(1024)}, u32[]{:S(2)}) copy-start(f32[2176]{0:T(1024)} %param.7) | copy-start | bytes 26116
  146.8 121.4 %reduce-scatter.5.cloned.1.call-start = ((), (), s32[]{:S(2)}) async-start(), calls=%async_computation.5 | async-start | bytes 11837440 | tf_op jit(solution)/shard_map/reduce_scatter | solution.py:27
  272.4 1.2 collective-permute-start
  275.7 5.1 %collective-permute-start.1 = (f32[545]{0:T(1024)S(1)}, f32[545]{0:T(1024)S(1)}, u32[]{:S(2)}, u32[]{:S(2)}) collective-permute-start(f32[545]{0:T(1024)S(1)} %pad_maximum_fusion.1), channel_id=1, source_target_pairs={{0,4},{2,6},{4,0},{6,2},{1,5},{3,7},{5,1},{7,3},{8,12},{10,14},{12... | collective-permute-start | bytes 6548 | tf_op jit(solution)/shard_map/ppermute | solution.py:41
  282.3 3.6 %collective-permute-start.2 = (f32[273]{0:T(512)S(1)}, f32[273]{0:T(512)S(1)}, u32[]{:S(2)}, u32[]{:S(2)}) collective-permute-start(f32[273]{0:T(512)S(1)} %pad_maximum_fusion.2), channel_id=1, source_target_pairs={{0,2},{2,0},{4,6},{6,4},{1,3},{3,1},{5,7},{7,5},{8,10},{10,8},{12,... | collective-permute-start | bytes 3284 | tf_op jit(solution)/shard_map/ppermute | solution.py:41
  287.2 9.4 %collective-permute-start.3 = (f32[273]{0:T(512)S(1)}, f32[273]{0:T(512)S(1)}, u32[]{:S(2)}, u32[]{:S(2)}) collective-permute-start(f32[273]{0:T(512)S(1)} %pad_maximum_fusion.3), channel_id=1, source_target_pairs={{0,0},{1,16},{2,1},{3,17},{4,2},{5,18},{6,3},{7,19},{8,4},{9,20},{... | collective-permute-start | bytes 3284 | tf_op jit(solution)/shard_map/ppermute | solution.py:57
Sparse Core Ops, SparseCore 0:
  12.7 111.7 all-gather.1
  146.9 29.2 reduce-scatter.2
  178.7 89.4 reduce-scatter.4

commit v8 on v7

--- a/solution.py
+++ b/solution.py
@@ -15,16 +15,21 @@
     block = c * ny + y
 
     owner = owner_order[0]
+    half = nvir // nc
+    flip = [(k, k ^ 1) for k in range(nc)]
     column = lax.dynamic_index_in_dim(integrals, owner, 1, keepdims=False)
     column, integrals = lax.optimization_barrier((column, integrals))
-    panel = lax.all_gather(column, GROUP, axis=0, tiled=True)
+    chip_rows = jnp.stack([column, lax.ppermute(column, "core", flip)])
+    mine = lax.dynamic_slice_in_dim(chip_rows, c * half, half, axis=2)
+    panel = lax.all_gather(mine, GROUP, axis=1, tiled=True).reshape(-1, half)
+
     left = lax.all_to_all(integrals, GROUP, 1, 0, tiled=True)[:, 0, :]
+    left = jnp.concatenate([left, lax.ppermute(left, "core", flip)])
 
     partial_sum = lax.dot_general(
         left, panel, (((0,), (0,)), ((), ())), preferred_element_type=jnp.float32
     )
-    summed = lax.psum_scatter(partial_sum, "core", scatter_dimension=1, tiled=True)
-    summed = lax.psum_scatter(summed, "y", scatter_dimension=1, tiled=True)
+    summed = lax.psum_scatter(partial_sum, "y", scatter_dimension=1, tiled=True)
 
     near_energy = lax.dynamic_slice_in_dim(vir_energy, block * blk, blk)
     own_energy = lax.dynamic_index_in_dim(occ_energy, orbital, 0, keepdims=False)

time: 305 us -> 296 us (0.970)
  blocking collectives: 86.1 us -> 0 us
  waiting for transfers between devices: 153 us -> 219 us
  starting transfers between devices: 7.8 us -> 16 us
    all_to_all x0 -> x1, waiting for transfers between devices: none -> 103 us  [per_device(): left = lax.all_to_all(integrals, GROUP, 1, 0, tiled=True)[:, 0, :]]
    all_to_all x1 -> x0, blocking collectives: 86.1 us -> none  [per_device(): left = lax.all_to_all(integrals, GROUP, 1, 0, tiled=True)[:, 0, :]]
    reduce_scatter x2 -> x1, waiting for transfers between devices: 119 us -> 88.4 us  [per_device(): summed = lax.psum_scatter(partial_sum, 'y', scatter_dimension=1, tiled=True)]
    all_to_all x0 -> x1, starting transfers between devices: none -> 8.29 us  [per_device(): left = lax.all_to_all(integrals, GROUP, 1, 0, tiled=True)[:, 0, :]]
    all_gather x1, waiting for transfers between devices: 21.9 us -> 15.7 us  [per_device(): panel = lax.all_gather(mine, GROUP, axis=1, tiled=True).reshape(-1, half)]
  transfers between devices with their start and end apart: 7 -> 9, of which waited for: 7 -> 7; matrix products, arithmetic and copies ran while one was open for 2% -> 3% of each run, Pallas kernels for 0% -> 0%
where the time goes in v8:
time: 296 us; the launch traced here: 295 us
  waiting for transfers between devices  219 us (74%)
  matrix products  20.9 us (7%)
  between operations  20 us (7%)
  starting transfers between devices  16 us (5%)
  local copies, waits for them, and re-layouts  13.8 us (5%)
  other arithmetic  5.24 us (2%)
    all_to_all x1, waiting for transfers between devices, per_device(): left = lax.all_to_all(integrals, GROUP, 1, 0, tiled=True)[:, 0, :]  103 us
    reduce_scatter x1, waiting for transfers between devices, per_device(): summed = lax.psum_scatter(partial_sum, 'y', scatter_dimension=1, tiled=True)  88.4 us
    dot_general x1, matrix products, per_device(): lax.dot_general(left, panel, (((0,), (0,)), ((), ())), preferred_element_...  20.9 us
    all_gather x1, waiting for transfers between devices, per_device(): panel = lax.all_gather(mine, GROUP, axis=1, tiled=True).reshape(-1, half)  15.7 us
    all_to_all x1, starting transfers between devices, per_device(): left = lax.all_to_all(integrals, GROUP, 1, 0, tiled=True)[:, 0, :]  8.29 us
    ppermute x3, waiting for transfers between devices, per_device(): lax.ppermute(jnp.concatenate([give.reshape(-1), total[None]]), axis, flip)  6.6 us
    optimization_barrier x1, local copies, waits for them, and re-layouts, per_device(): column, integrals = lax.optimization_barrier((column, integrals))  6.5 us
  transfers between devices with their start and end apart: 9, of which 7 were waited for; matrix products, arithmetic and copies ran while one was open for 3% of the time, Pallas kernels for 0%

profile of v8, /device:TPU:12, one launch (start us, length us, event | category | flops | bytes accessed | tf_op | source)
XLA Modules:
  0.0 295.3 jit_solution(8121158242149694228)
XLA Ops:
  9.1 2.7 constant_dynamic-slice_fusion.4
  11.8 0.1 collective-permute-start.1
  11.9 6.5 %copy.7 = bf16[88,16,2176]{2,0,1:T(8,128)(2,1)} copy(bf16[88,16,2176]{2,1,0:T(8,128)(2,1)} %param.4) | data formatting | bytes 12255232 | tf_op jit(solution)/shard_map/optimization_barrier | solution.py:21
  18.4 8.3 %all-to-all-start = ((bf16[88,16,2176]{2,0,1:T(8,128)(2,1)}), bf16[88,16,2176]{2,0,1:T(8,128)(2,1)}, u32[]{:S(2)}, u32[]{:S(2)}) async-start(bf16[88,16,2176]{2,0,1:T(8,128)(2,1)} %copy.7), calls=%async_computation | async-start | bytes 12255232 | tf_op jit(solution)/shard_map/all_to_all | solution.py:26
  26.7 0.0 all-gather.2.cloned.1.call-start
  26.8 0.0 collective-permute-done.1
  26.8 1.0 fusion.4
  27.7 0.0 all-gather.2.cloned.1.call-update
  27.7 0.0 reduce-scatter.2.cloned.1.call-start
  27.8 103.5 %all-to-all-done = bf16[88,16,2176]{2,0,1:T(8,128)(2,1)} async-done(((bf16[88,16,2176]{2,0,1:T(8,128)(2,1)}), bf16[88,16,2176]{2,0,1:T(8,128)(2,1)}, u32[]{:S(2)}, u32[]{:S(2)}) %all-to-all-start) | async-done | bytes 6127648 | tf_op jit(solution)/shard_map/all_to_all | solution.py:26
  131.3 0.0 collective-permute-start
  131.3 15.7 %all-gather.2.cloned.1.call-done = bf16[2,1408,1088]{2,1,0:T(8,128)(2,1)} async-done(((bf16[2,88,1088]{2,1,0:T(8,128)(2,1)}), bf16[2,1408,1088]{2,1,0:T(8,128)(2,1)}) %all-gather.2.cloned.1.call-update) | async-done | bytes 6127632 | tf_op jit(solution)/shard_map/all_gather | solution.py:24
  147.0 0.0 collective-permute-done
  147.0 20.9 %fusion = f32[2176,1088]{0,1:T(8,128)} fusion(bf16[2816,1088]{1,0:T(8,128)(2,1)} %bitcast.39, bf16[1408,2176]{1,0:T(8,128)(2,1)} %collective-permute-done, bf16[1408,2176]{1,0:T(8,128)(2,1)} %bitcast.4), kind=kOutput, calls=%fused_computation | convolution fusion | flops 13358202880 | bytes 27852800 | tf_op jit(solution)/shard_map/dot_general | solution.py:29
  167.9 0.0 copy-start.1
  167.9 0.0 copy-start
  167.9 0.0 reduce-scatter.2.cloned.1.call-update
  167.9 0.6 copy-done.1
  168.5 0.6 fusion.10
  170.4 0.0 copy-done
  170.4 0.1 dynamic_slice.42
  170.5 88.4 %reduce-scatter.2.cloned.1.call-done = f32[2176,272]{0,1:T(8,128)} async-done(((f32[2176,1088]{0,1:T(8,128)}), f32[2176,272]{0,1:T(8,128)}) %reduce-scatter.2.cloned.1.call-update) | async-done | bytes 2367504 | tf_op jit(solution)/shard_map/reduce_scatter | solution.py:32
  258.9 3.3 %fusion.6 = (f32[2176]{0:T(1024)S(1)}, f32[]{:T(128)}) fusion(f32[272]{0:T(512)S(1)} %dynamic_slice.42, f32[2176]{0:T(1024)S(1)} %broadcast_subtract_fusion, f32[2176,272]{0,1:T(8,128)} %reduce-scatter.2.cloned.1.call-done), kind=kLoop, calls=%fused_computation.10 | loop fusion | flops 2957183 | bytes 2385988 | tf_op jit(solution)/shard_map/reduce_sum | solution.py:38
  262.2 0.1 reshape.36
  262.3 0.1 reshape.37
  262.4 0.7 pad_maximum_fusion
  263.1 0.0 collective-permute-start.2
  263.2 1.1 collective-permute-done.2
  264.3 0.1 reshape.38
  264.4 0.1 reshape.39
  264.5 0.6 slice.37
  266.4 0.1 pad_maximum_fusion.1
  266.5 1.5 collective-permute-start.3
  267.9 3.7 %collective-permute-done.3 = f32[545]{0:T(1024)S(1)} collective-permute-done((f32[545]{0:T(1024)S(1)}, f32[545]{0:T(1024)S(1)}, u32[]{:S(2)}, u32[]{:S(2)}) %collective-permute-start.3) | collective-permute-done | bytes 2212 | tf_op jit(solution)/shard_map/ppermute | solution.py:46
  271.6 0.1 reshape.40
  271.7 0.6 slice.31
  273.0 0.1 pad_maximum_fusion.2
  273.0 1.8 collective-permute-start.4
  274.8 1.8 collective-permute-done.4
  276.6 0.6 slice.33
  277.9 0.1 pad_maximum_fusion.3
  278.0 4.3 %collective-permute-start.5 = (f32[273]{0:T(512)S(1)}, f32[273]{0:T(512)S(1)}, u32[]{:S(2)}, u32[]{:S(2)}) collective-permute-start(f32[273]{0:T(512)S(1)} %pad_maximum_fusion.3), channel_id=1, source_target_pairs={{0,0},{1,16},{2,1},{3,17},{4,2},{5,18},{6,3},{7,19},{8,4},{9,20},{... | collective-permute-start | bytes 3284 | tf_op jit(solution)/shard_map/ppermute | solution.py:62
  282.3 5.1 %collective-permute-done.5 = f32[273]{0:T(512)S(1)} collective-permute-done((f32[273]{0:T(512)S(1)}, f32[273]{0:T(512)S(1)}, u32[]{:S(2)}, u32[]{:S(2)}) %collective-permute-start.5) | collective-permute-done | bytes 1124 | tf_op jit(solution)/shard_map/ppermute | solution.py:62
  287.3 0.6 reshape.41
  287.9 0.6 slice.35
  (8 shorter events, 0.1 us)
Async XLA Ops:
  11.8 14.9 %collective-permute-start.1 = (bf16[88,2176]{1,0:T(8,128)(2,1)S(1)}, bf16[88,2176]{1,0:T(8,128)(2,1)S(1)}, u32[]{:S(2)}, u32[]{:S(2)}) collective-permute-start(bf16[88,2176]{1,0:T(8,128)(2,1)S(1)} %bitcast.30), channel_id=1, source_target_pairs={{0,8},{8,0},{1,9},{9,1},{2,10},{10,2},{3,11},{11,3},{4,12},{12,4},... | collective-permute-start | bytes 1148936 | tf_op jit(solution)/shard_map/ppermute | solution.py:22
  18.4 112.8 %all-to-all-start = ((bf16[88,16,2176]{2,0,1:T(8,128)(2,1)}), bf16[88,16,2176]{2,0,1:T(8,128)(2,1)}, u32[]{:S(2)}, u32[]{:S(2)}) async-start(bf16[88,16,2176]{2,0,1:T(8,128)(2,1)} %copy.7), calls=%async_computation | async-start | bytes 12255232 | tf_op jit(solution)/shard_map/all_to_all | solution.py:26
  26.7 120.3 %all-gather.2.cloned.1.call-start = ((), (), s32[]{:S(2)}) async-start(), calls=%async_computation.2 | async-start | bytes 6893568 | tf_op jit(solution)/shard_map/all_gather | solution.py:24
  27.7 231.2 %reduce-scatter.2.cloned.1.call-start = ((), (), s32[]{:S(2)}) async-start(), calls=%async_computation.3 | async-start | bytes 11837440 | tf_op jit(solution)/shard_map/reduce_scatter | solution.py:32
  131.3 15.7 %collective-permute-start = (bf16[1408,2176]{1,0:T(8,128)(2,1)}, bf16[1408,2176]{1,0:T(8,128)(2,1)}, u32[]{:S(2)}, u32[]{:S(2)}) collective-permute-start(bf16[1408,2176]{1,0:T(8,128)(2,1)} %bitcast.4), channel_id=1, source_target_pairs={{0,8},{8,0},{1,9},{9,1},{2,10},{10,2},{3,11},{11,3},{4,12},{12,4},... | collective-permute-start | bytes 18382856 | tf_op jit(solution)/shard_map/ppermute | solution.py:27
  167.9 0.7 copy-start.1
  167.9 2.5 copy-start
  263.1 1.2 collective-permute-start.2
  266.5 5.1 %collective-permute-start.3 = (f32[545]{0:T(1024)S(1)}, f32[545]{0:T(1024)S(1)}, u32[]{:S(2)}, u32[]{:S(2)}) collective-permute-start(f32[545]{0:T(1024)S(1)} %pad_maximum_fusion.1), channel_id=1, source_target_pairs={{0,4},{2,6},{4,0},{6,2},{1,5},{3,7},{5,1},{7,3},{8,12},{10,14},{12... | collective-permute-start | bytes 6548 | tf_op jit(solution)/shard_map/ppermute | solution.py:46
  273.0 3.6 %collective-permute-start.4 = (f32[273]{0:T(512)S(1)}, f32[273]{0:T(512)S(1)}, u32[]{:S(2)}, u32[]{:S(2)}) collective-permute-start(f32[273]{0:T(512)S(1)} %pad_maximum_fusion.2), channel_id=1, source_target_pairs={{0,2},{2,0},{4,6},{6,4},{1,3},{3,1},{5,7},{7,5},{8,10},{10,8},{12,... | collective-permute-start | bytes 3284 | tf_op jit(solution)/shard_map/ppermute | solution.py:46
  278.0 9.4 %collective-permute-start.5 = (f32[273]{0:T(512)S(1)}, f32[273]{0:T(512)S(1)}, u32[]{:S(2)}, u32[]{:S(2)}) collective-permute-start(f32[273]{0:T(512)S(1)} %pad_maximum_fusion.3), channel_id=1, source_target_pairs={{0,0},{1,16},{2,1},{3,17},{4,2},{5,18},{6,3},{7,19},{8,4},{9,20},{... | collective-permute-start | bytes 3284 | tf_op jit(solution)/shard_map/ppermute | solution.py:62
Sparse Core Ops, SparseCore 0:
  29.7 117.2 all-gather.1
  168.0 90.8 reduce-scatter.1

commit v9 on v8

--- a/solution.py
+++ b/solution.py
@@ -6,8 +6,8 @@
 GROUP = ("z", "xh", "xl")
 
 
-def per_device(integrals, owner_order, occ_energy, vir_energy):
-    nq, nocc, nvir = integrals.shape
+def body(integrals, owner_order, occ_energy, vir_energy):
+    _, _, nvir = integrals.shape
     ny, nh, nc, nl = lax.axis_size("y"), lax.axis_size("xh"), lax.axis_size("core"), lax.axis_size("xl")
     blk = nvir // (ny * nh)
     z, l, y, h, c = (lax.axis_index(a) for a in ("z", "xl", "y", "xh", "core"))
@@ -18,12 +18,15 @@
     half = nvir // nc
     flip = [(k, k ^ 1) for k in range(nc)]
     column = lax.dynamic_index_in_dim(integrals, owner, 1, keepdims=False)
-    column, integrals = lax.optimization_barrier((column, integrals))
     chip_rows = jnp.stack([column, lax.ppermute(column, "core", flip)])
     mine = lax.dynamic_slice_in_dim(chip_rows, c * half, half, axis=2)
-    panel = lax.all_gather(mine, GROUP, axis=1, tiled=True).reshape(-1, half)
+    mine, integrals = lax.optimization_barrier((mine, integrals))
+    by_orbital = jnp.transpose(integrals, (1, 0, 2))
+    panel = lax.all_gather(mine, GROUP, axis=1, tiled=True)
+    panel = panel.reshape(-1, half)
 
-    left = lax.all_to_all(integrals, GROUP, 1, 0, tiled=True)[:, 0, :]
+    left = lax.all_to_all(by_orbital, GROUP, 0, 0, tiled=True)
+    left = left.reshape(-1, nvir)
     left = jnp.concatenate([left, lax.ppermute(left, "core", flip)])
 
     partial_sum = lax.dot_general(
@@ -70,6 +73,4 @@
     fine = Mesh(mesh.devices.reshape(shape), ("z", "xl", "core", "y", "xh"))
     in_specs = (P(("z", "xl", "core", "y", "xh"), None, None), P(), P(), P())
     out_specs = (P(("z", "xl", "core"), None, ("y", "xh")), P(("z", "xl", "core"), None))
-    return jax.shard_map(
-        per_device, mesh=fine, in_specs=in_specs, out_specs=out_specs, check_vma=False
-    )
+    return jax.shard_map(body, mesh=fine, in_specs=in_specs, out_specs=out_specs, check_vma=False)

time: 296 us -> 297 us (level)
  transfers between devices with their start and end apart: 9 -> 9, of which waited for: 7 -> 8; matrix products, arithmetic and copies ran while one was open for 3% -> 0% of each run, Pallas kernels for 0% -> 0%
where the time goes in v9:
time: 297 us
  waiting for transfers between devices  221 us (74%)
  matrix products  20.9 us (7%)
  between operations  20 us (7%)
  starting transfers between devices  16.1 us (5%)
  local copies, waits for them, and re-layouts  13.8 us (5%)
  other arithmetic  5.23 us (2%)
    all_to_all x1, waiting for transfers between devices, body(): left = lax.all_to_all(by_orbital, GROUP, 0, 0, tiled=True)  103 us
    reduce_scatter x1, waiting for transfers between devices, body(): summed = lax.psum_scatter(partial_sum, 'y', scatter_dimension=1, tiled=True)  88.3 us
    dot_general x1, matrix products, body(): lax.dot_general(left, panel, (((0,), (0,)), ((), ())), preferred_element_...  20.9 us
    all_gather x1, waiting for transfers between devices, body(): panel = lax.all_gather(mine, GROUP, axis=1, tiled=True)  15.6 us
    all_to_all x1, starting transfers between devices, body(): left = lax.all_to_all(by_orbital, GROUP, 0, 0, tiled=True)  8.29 us
    ppermute x3, waiting for transfers between devices, body(): lax.ppermute(jnp.concatenate([give.reshape(-1), total[None]]), axis, flip)  6.53 us
    optimization_barrier x1, local copies, waits for them, and re-layouts, body(): mine, integrals = lax.optimization_barrier((mine, integrals))  6.5 us
  transfers between devices with their start and end apart: 9, of which 8 were waited for; matrix products, arithmetic and copies ran while one was open for 0% of the time, Pallas kernels for 0%

profile of v9, /device:TPU:12, one launch (start us, length us, event | category | flops | bytes accessed | tf_op | source)
XLA Modules:
  0.0 297.0 jit_solution(4710964948644526921)
XLA Ops:
  9.1 2.7 constant_dynamic-slice_fusion.4
  11.8 0.1 collective-permute-start
  11.9 1.7 collective-permute-done
  13.6 0.9 fusion.4
  14.6 6.5 %copy.12 = bf16[88,16,2176]{2,0,1:T(8,128)(2,1)} copy(bf16[88,16,2176]{2,1,0:T(8,128)(2,1)} %param.4) | data formatting | bytes 12255232 | tf_op jit(solution)/shard_map/optimization_barrier | solution.py:23
  21.1 8.3 %all-to-all-start = ((bf16[16,88,2176]{2,1,0:T(8,128)(2,1)}), bf16[16,88,2176]{2,1,0:T(8,128)(2,1)}, u32[]{:S(2)}, u32[]{:S(2)}) async-start(bf16[16,88,2176]{2,1,0:T(8,128)(2,1)} %bitcast.30), calls=%async_computation | async-start | bytes 12255232 | tf_op jit(solution)/shard_map/all_to_all | solution.py:28
  29.4 0.0 all-gather.2.cloned.1.call-start
  29.4 0.7 all-gather.2.cloned.1.call-update
  30.1 0.0 reduce-scatter.2.cloned.1.call-start
  30.1 103.1 %all-to-all-done = bf16[16,88,2176]{2,1,0:T(8,128)(2,1)} async-done(((bf16[16,88,2176]{2,1,0:T(8,128)(2,1)}), bf16[16,88,2176]{2,1,0:T(8,128)(2,1)}, u32[]{:S(2)}, u32[]{:S(2)}) %all-to-all-start) | async-done | bytes 6127648 | tf_op jit(solution)/shard_map/all_to_all | solution.py:28
  133.2 0.0 collective-permute-start.1
  133.2 15.6 %all-gather.2.cloned.1.call-done = bf16[2,1408,1088]{2,1,0:T(8,128)(2,1)} async-done(((bf16[2,88,1088]{2,1,0:T(8,128)(2,1)}), bf16[2,1408,1088]{2,1,0:T(8,128)(2,1)}) %all-gather.2.cloned.1.call-update) | async-done | bytes 6127632 | tf_op jit(solution)/shard_map/all_gather | solution.py:25
  148.8 0.0 collective-permute-done.1
  148.8 20.9 %fusion = f32[2176,1088]{0,1:T(8,128)} fusion(bf16[2816,1088]{1,0:T(8,128)(2,1)} %bitcast.40, bf16[1408,2176]{1,0:T(8,128)(2,1)} %collective-permute-done.1, bf16[1408,2176]{1,0:T(8,128)(2,1)} %bitcast.5), kind=kOutput, calls=%fused_computation | convolution fusion | flops 13358202880 | bytes 27852800 | tf_op jit(solution)/shard_map/dot_general | solution.py:32
  169.7 0.0 copy-start.1
  169.7 0.0 copy-start
  169.7 0.0 reduce-scatter.2.cloned.1.call-update
  169.7 0.6 copy-done.1
  170.3 0.6 fusion.10
  172.2 0.0 copy-done
  172.2 0.1 dynamic_slice.42
  172.3 88.3 %reduce-scatter.2.cloned.1.call-done = f32[2176,272]{0,1:T(8,128)} async-done(((f32[2176,1088]{0,1:T(8,128)}), f32[2176,272]{0,1:T(8,128)}) %reduce-scatter.2.cloned.1.call-update) | async-done | bytes 2367504 | tf_op jit(solution)/shard_map/reduce_scatter | solution.py:35
  260.6 3.3 %fusion.6 = (f32[2176]{0:T(1024)S(1)}, f32[]{:T(128)}) fusion(f32[272]{0:T(512)S(1)} %dynamic_slice.42, f32[2176]{0:T(1024)S(1)} %broadcast_subtract_fusion, f32[2176,272]{0,1:T(8,128)} %reduce-scatter.2.cloned.1.call-done), kind=kLoop, calls=%fused_computation.12 | loop fusion | flops 2957183 | bytes 2385988 | tf_op jit(solution)/shard_map/reduce_sum | solution.py:41
  263.9 0.1 reshape.40
  264.0 0.1 reshape.41
  264.1 0.7 pad_maximum_fusion
  264.8 0.0 collective-permute-start.2
  264.8 1.1 collective-permute-done.2
  266.0 0.1 reshape.42
  266.1 0.1 reshape.43
  266.2 0.6 slice.37
  268.0 0.1 pad_maximum_fusion.1
  268.1 1.5 collective-permute-start.3
  269.6 3.6 %collective-permute-done.3 = f32[545]{0:T(1024)S(1)} collective-permute-done((f32[545]{0:T(1024)S(1)}, f32[545]{0:T(1024)S(1)}, u32[]{:S(2)}, u32[]{:S(2)}) %collective-permute-start.3) | collective-permute-done | bytes 2212 | tf_op jit(solution)/shard_map/ppermute | solution.py:49
  273.3 0.1 reshape.44
  273.3 0.6 slice.31
  274.6 0.1 pad_maximum_fusion.2
  274.7 1.8 collective-permute-start.4
  276.5 1.8 collective-permute-done.4
  278.3 0.6 slice.33
  279.5 0.1 pad_maximum_fusion.3
  279.6 4.3 %collective-permute-start.5 = (f32[273]{0:T(512)S(1)}, f32[273]{0:T(512)S(1)}, u32[]{:S(2)}, u32[]{:S(2)}) collective-permute-start(f32[273]{0:T(512)S(1)} %pad_maximum_fusion.3), channel_id=1, source_target_pairs={{0,0},{1,16},{2,1},{3,17},{4,2},{5,18},{6,3},{7,19},{8,4},{9,20},{... | collective-permute-start | bytes 3284 | tf_op jit(solution)/shard_map/ppermute | solution.py:65
  283.9 5.1 %collective-permute-done.5 = f32[273]{0:T(512)S(1)} collective-permute-done((f32[273]{0:T(512)S(1)}, f32[273]{0:T(512)S(1)}, u32[]{:S(2)}, u32[]{:S(2)}) %collective-permute-start.5) | collective-permute-done | bytes 1124 | tf_op jit(solution)/shard_map/ppermute | solution.py:65
  289.0 0.6 reshape.45
  289.6 0.6 slice.35
  (8 shorter events, 0.1 us)
Async XLA Ops:
  11.8 1.8 collective-permute-start
  21.1 112.2 %all-to-all-start = ((bf16[16,88,2176]{2,1,0:T(8,128)(2,1)}), bf16[16,88,2176]{2,1,0:T(8,128)(2,1)}, u32[]{:S(2)}, u32[]{:S(2)}) async-start(bf16[16,88,2176]{2,1,0:T(8,128)(2,1)} %bitcast.30), calls=%async_computation | async-start | bytes 12255232 | tf_op jit(solution)/shard_map/all_to_all | solution.py:28
  29.4 119.4 %all-gather.2.cloned.1.call-start = ((), (), s32[]{:S(2)}) async-start(), calls=%async_computation.2 | async-start | bytes 6893568 | tf_op jit(solution)/shard_map/all_gather | solution.py:25
  30.1 230.5 %reduce-scatter.2.cloned.1.call-start = ((), (), s32[]{:S(2)}) async-start(), calls=%async_computation.3 | async-start | bytes 11837440 | tf_op jit(solution)/shard_map/reduce_scatter | solution.py:35
  133.2 15.6 %collective-permute-start.1 = (bf16[1408,2176]{1,0:T(8,128)(2,1)}, bf16[1408,2176]{1,0:T(8,128)(2,1)}, u32[]{:S(2)}, u32[]{:S(2)}) collective-permute-start(bf16[1408,2176]{1,0:T(8,128)(2,1)} %bitcast.5), channel_id=1, source_target_pairs={{0,8},{8,0},{1,9},{9,1},{2,10},{10,2},{3,11},{11,3},{4,12},{12,4},... | collective-permute-start | bytes 18382856 | tf_op jit(solution)/shard_map/ppermute | solution.py:30
  169.7 0.7 copy-start.1
  169.7 2.5 copy-start
  264.8 1.2 collective-permute-start.2
  268.1 5.1 %collective-permute-start.3 = (f32[545]{0:T(1024)S(1)}, f32[545]{0:T(1024)S(1)}, u32[]{:S(2)}, u32[]{:S(2)}) collective-permute-start(f32[545]{0:T(1024)S(1)} %pad_maximum_fusion.1), channel_id=1, source_target_pairs={{0,4},{2,6},{4,0},{6,2},{1,5},{3,7},{5,1},{7,3},{8,12},{10,14},{12... | collective-permute-start | bytes 6548 | tf_op jit(solution)/shard_map/ppermute | solution.py:49
  274.7 3.6 %collective-permute-start.4 = (f32[273]{0:T(512)S(1)}, f32[273]{0:T(512)S(1)}, u32[]{:S(2)}, u32[]{:S(2)}) collective-permute-start(f32[273]{0:T(512)S(1)} %pad_maximum_fusion.2), channel_id=1, source_target_pairs={{0,2},{2,0},{4,6},{6,4},{1,3},{3,1},{5,7},{7,5},{8,10},{10,8},{12,... | collective-permute-start | bytes 3284 | tf_op jit(solution)/shard_map/ppermute | solution.py:49
  279.6 9.4 %collective-permute-start.5 = (f32[273]{0:T(512)S(1)}, f32[273]{0:T(512)S(1)}, u32[]{:S(2)}, u32[]{:S(2)}) collective-permute-start(f32[273]{0:T(512)S(1)} %pad_maximum_fusion.3), channel_id=1, source_target_pairs={{0,0},{1,16},{2,1},{3,17},{4,2},{5,18},{6,3},{7,19},{8,4},{9,20},{... | collective-permute-start | bytes 3284 | tf_op jit(solution)/shard_map/ppermute | solution.py:65
Sparse Core Ops, SparseCore 0:
  32.4 116.3 all-gather.1
  169.8 90.7 reduce-scatter.1

commit v10 on v9

--- a/solution.py
+++ b/solution.py
@@ -18,19 +18,22 @@
     half = nvir // nc
     flip = [(k, k ^ 1) for k in range(nc)]
     column = lax.dynamic_index_in_dim(integrals, owner, 1, keepdims=False)
-    chip_rows = jnp.stack([column, lax.ppermute(column, "core", flip)])
-    mine = lax.dynamic_slice_in_dim(chip_rows, c * half, half, axis=2)
-    mine, integrals = lax.optimization_barrier((mine, integrals))
+    own_half = lax.dynamic_slice_in_dim(column, c * half, half, axis=1)
+    panel_own = lax.all_gather(own_half, GROUP, axis=0, tiled=True)
+    other = lax.ppermute(column, "core", flip)
+    other_half = lax.dynamic_slice_in_dim(other, c * half, half, axis=1)
+    panel_other = lax.all_gather(other_half, GROUP, axis=0, tiled=True)
+    other_half, integrals = lax.optimization_barrier((other_half, integrals))
     by_orbital = jnp.transpose(integrals, (1, 0, 2))
-    panel = lax.all_gather(mine, GROUP, axis=1, tiled=True)
-    panel = panel.reshape(-1, half)
 
     left = lax.all_to_all(by_orbital, GROUP, 0, 0, tiled=True)
     left = left.reshape(-1, nvir)
-    left = jnp.concatenate([left, lax.ppermute(left, "core", flip)])
+    left_other = lax.ppermute(left, "core", flip)
 
-    partial_sum = lax.dot_general(
-        left, panel, (((0,), (0,)), ((), ())), preferred_element_type=jnp.float32
+    contract = (((0,), (0,)), ((), ()))
+    partial_sum = lax.dot_general(left, panel_own, contract, preferred_element_type=jnp.float32)
+    partial_sum = partial_sum + lax.dot_general(
+        left_other, panel_other, contract, preferred_element_type=jnp.float32
     )
     summed = lax.psum_scatter(partial_sum, "y", scatter_dimension=1, tiled=True)
 

time: 297 us -> 325 us (1.094)
  waiting for transfers between devices: 221 us -> 237 us
  matrix products: 20.9 us -> 29.4 us
  local copies, waits for them, and re-layouts: 13.8 us -> 17.6 us
    all_gather x1 -> x2, waiting for transfers between devices: 15.6 us -> 46 us  [the longest x1 36.3 us: body(): panel_other = lax.all_gather(other_half, GROUP, axis=0, tiled=True)]
    all_to_all x1, waiting for transfers between devices: 103 us -> 92.4 us  [body(): left = lax.all_to_all(by_orbital, GROUP, 0, 0, tiled=True)]
    dot_general x1 -> x2, matrix products: 20.9 us -> 29.4 us  [the longest x1 15.4 us: body(): lax.dot_general(left_other, panel_other, contract, preferred_element_type...]
  transfers between devices with their start and end apart: 9 -> 10, of which waited for: 8 -> 9; matrix products, arithmetic and copies ran while one was open for 0% -> 5% of each run, Pallas kernels for 0% -> 0%
where the time goes in v10:
time: 325 us
  waiting for transfers between devices  237 us (73%)
  matrix products  29.4 us (9%)
  between operations  19.7 us (6%)
  local copies, waits for them, and re-layouts  17.6 us (5%)
  starting transfers between devices  16.3 us (5%)
  other arithmetic  4.28 us (1%)
    all_to_all x1, waiting for transfers between devices, body(): left = lax.all_to_all(by_orbital, GROUP, 0, 0, tiled=True)  92.4 us
    reduce_scatter x1, waiting for transfers between devices, body(): summed = lax.psum_scatter(partial_sum, 'y', scatter_dimension=1, tiled=True)  85.5 us
    all_gather x1, waiting for transfers between devices, body(): panel_other = lax.all_gather(other_half, GROUP, axis=0, tiled=True)  36.3 us
    dot_general x1, matrix products, body(): lax.dot_general(left_other, panel_other, contract, preferred_element_type...  15.4 us
    dot_general x1, matrix products, body(): lax.dot_general(left, panel_own, contract, preferred_element_type=jnp.flo...  14 us
    all_gather x1, waiting for transfers between devices, body(): panel_own = lax.all_gather(own_half, GROUP, axis=0, tiled=True)  9.74 us
    all_to_all x1, starting transfers between devices, body(): left = lax.all_to_all(by_orbital, GROUP, 0, 0, tiled=True)  8.29 us
    ppermute x3, waiting for transfers between devices, body(): lax.ppermute(jnp.concatenate([give.reshape(-1), total[None]]), axis, flip)  6.57 us
  transfers between devices with their start and end apart: 10, of which 9 were waited for; matrix products, arithmetic and copies ran while one was open for 5% of the time, Pallas kernels for 0%

profile of v10, /device:TPU:12, one launch (start us, length us, event | category | flops | bytes accessed | tf_op | source)
XLA Modules:
  0.0 324.6 jit_solution(17770818905507237721)
XLA Ops:
  9.1 2.7 constant_dynamic-slice_fusion.6
  11.8 0.1 collective-permute-start
  11.9 1.7 collective-permute-done
  13.6 0.8 constant_dynamic-slice_fusion.5
  14.4 6.5 %copy.17 = bf16[88,16,2176]{2,0,1:T(8,128)(2,1)} copy(bf16[88,16,2176]{2,1,0:T(8,128)(2,1)} %param.4) | data formatting | bytes 12255232 | tf_op jit(solution)/shard_map/optimization_barrier | solution.py:26
  20.9 8.3 %all-to-all-start = ((bf16[16,88,2176]{2,1,0:T(8,128)(2,1)}), bf16[16,88,2176]{2,1,0:T(8,128)(2,1)}, u32[]{:S(2)}, u32[]{:S(2)}) async-start(bf16[16,88,2176]{2,1,0:T(8,128)(2,1)} %bitcast.32), calls=%async_computation | async-start | bytes 12255232 | tf_op jit(solution)/shard_map/all_to_all | solution.py:29
  29.2 0.0 all-gather.6.cloned.1.call-start
  29.3 2.3 constant_dynamic-slice_fusion.4
  31.6 0.7 copy.13
  32.3 0.0 all-gather.6.cloned.1.call-update
  32.3 0.0 all-gather.4.cloned.1.call-start
  32.3 92.4 %all-to-all-done = bf16[16,88,2176]{2,1,0:T(8,128)(2,1)} async-done(((bf16[16,88,2176]{2,1,0:T(8,128)(2,1)}), bf16[16,88,2176]{2,1,0:T(8,128)(2,1)}, u32[]{:S(2)}, u32[]{:S(2)}) %all-to-all-start) | async-done | bytes 6127648 | tf_op jit(solution)/shard_map/all_to_all | solution.py:29
  124.7 0.0 collective-permute-start.1
  124.7 0.0 all-gather.4.cloned.1.call-update
  124.7 0.2 reduce-scatter.2.cloned.1.call-start
  125.0 9.7 %all-gather.6.cloned.1.call-done = bf16[1408,1,1088]{2,0,1:T(8,128)(2,1)} async-done(((bf16[88,1,1088]{2,0,1:T(8,128)(2,1)}), bf16[1408,1,1088]{2,0,1:T(8,128)(2,1)}) %all-gather.6.cloned.1.call-update) | async-done | bytes 3063824 | tf_op jit(solution)/shard_map/all_gather | solution.py:22
  134.7 14.0 %fusion = f32[2176,1088]{0,1:T(8,128)} fusion(bf16[1408,2176]{1,0:T(8,128)(2,1)} %bitcast.3, bf16[1408,1,1088]{2,0,1:T(8,128)(2,1)} %all-gather.6.cloned.1.call-done), kind=kOutput, calls=%fused_computation.2 | convolution fusion | flops 6666846208 | bytes 18661376 | tf_op jit(solution)/shard_map/dot_general | solution.py:34
  148.7 36.3 %all-gather.4.cloned.1.call-done = bf16[1408,1088]{1,0:T(8,128)(2,1)} async-done(((bf16[88,1088]{1,0:T(8,128)(2,1)}), bf16[1408,1088]{1,0:T(8,128)(2,1)}) %all-gather.4.cloned.1.call-update) | async-done | bytes 3063824 | tf_op jit(solution)/shard_map/all_gather | solution.py:25
  185.0 0.0 collective-permute-done.1
  185.0 15.4 %convolution_add_fusion = f32[2176,1088]{0,1:T(8,128)} fusion(f32[2176,1088]{0,1:T(8,128)} %fusion, bf16[1408,2176]{1,0:T(8,128)(2,1)} %collective-permute-done.1, bf16[1408,1088]{1,0:T(8,128)(2,1)} %all-gather.4.cloned.1.call-done), kind=kOutput, calls=%fused_computation | convolution fusion | flops 6669213696 | bytes 28131328 | tf_op jit(solution)/shard_map/dot_general | solution.py:35
  200.4 0.0 reduce-scatter.2.cloned.1.call-update
  200.4 0.6 copy-done.1
  201.0 0.6 fusion.6
  202.9 0.1 dynamic_slice.49
  203.0 85.5 %reduce-scatter.2.cloned.1.call-done = f32[2176,272]{0,1:T(8,128)} async-done(((f32[2176,1088]{0,1:T(8,128)}), f32[2176,272]{0,1:T(8,128)}) %reduce-scatter.2.cloned.1.call-update) | async-done | bytes 2367504 | tf_op jit(solution)/shard_map/reduce_scatter | solution.py:38
  288.5 3.3 %fusion.3 = (f32[2176]{0:T(1024)S(1)}, f32[]{:T(128)}) fusion(f32[272]{0:T(512)S(1)} %dynamic_slice.49, f32[2176]{0:T(1024)S(1)} %broadcast_subtract_fusion, f32[2176,272]{0,1:T(8,128)} %reduce-scatter.2.cloned.1.call-done), kind=kLoop, calls=%fused_computation.7 | loop fusion | flops 2957183 | bytes 2385988 | tf_op jit(solution)/shard_map/reduce_sum | solution.py:44
  291.8 0.1 reshape.36
  291.9 0.1 reshape.37
  292.0 0.7 pad_maximum_fusion
  292.7 0.0 collective-permute-start.2
  292.8 1.1 collective-permute-done.2
  293.9 0.1 reshape.38
  294.0 0.1 reshape.39
  294.1 0.6 slice.37
  296.0 0.1 pad_maximum_fusion.1
  296.0 1.5 collective-permute-start.3
  297.5 3.6 %collective-permute-done.3 = f32[545]{0:T(1024)S(1)} collective-permute-done((f32[545]{0:T(1024)S(1)}, f32[545]{0:T(1024)S(1)}, u32[]{:S(2)}, u32[]{:S(2)}) %collective-permute-start.3) | collective-permute-done | bytes 2212 | tf_op jit(solution)/shard_map/ppermute | solution.py:52
  301.2 0.1 reshape.40
  301.3 0.6 slice.31
  302.5 0.1 pad_maximum_fusion.2
  302.6 1.8 collective-permute-start.4
  304.4 1.8 collective-permute-done.4
  306.2 0.6 slice.33
  307.5 0.1 pad_maximum_fusion.3
  307.5 4.3 %collective-permute-start.5 = (f32[273]{0:T(512)S(1)}, f32[273]{0:T(512)S(1)}, u32[]{:S(2)}, u32[]{:S(2)}) collective-permute-start(f32[273]{0:T(512)S(1)} %pad_maximum_fusion.3), channel_id=1, source_target_pairs={{0,0},{1,16},{2,1},{3,17},{4,2},{5,18},{6,3},{7,19},{8,4},{9,20},{... | collective-permute-start | bytes 3284 | tf_op jit(solution)/shard_map/ppermute | solution.py:68
  311.9 5.1 %collective-permute-done.5 = f32[273]{0:T(512)S(1)} collective-permute-done((f32[273]{0:T(512)S(1)}, f32[273]{0:T(512)S(1)}, u32[]{:S(2)}, u32[]{:S(2)}) %collective-permute-start.5) | collective-permute-done | bytes 1124 | tf_op jit(solution)/shard_map/ppermute | solution.py:68
  316.9 0.6 reshape.41
  317.5 0.6 slice.35
  (11 shorter events, 0.1 us)
Async XLA Ops:
  11.8 1.8 collective-permute-start
  20.9 103.8 %all-to-all-start = ((bf16[16,88,2176]{2,1,0:T(8,128)(2,1)}), bf16[16,88,2176]{2,1,0:T(8,128)(2,1)}, u32[]{:S(2)}, u32[]{:S(2)}) async-start(bf16[16,88,2176]{2,1,0:T(8,128)(2,1)} %bitcast.32), calls=%async_computation | async-start | bytes 12255232 | tf_op jit(solution)/shard_map/all_to_all | solution.py:29
  29.2 105.5 %all-gather.6.cloned.1.call-start = ((), (), s32[]{:S(2)}) async-start(), calls=%async_computation.4 | async-start | bytes 3446784 | tf_op jit(solution)/shard_map/all_gather | solution.py:22
  32.3 152.7 %all-gather.4.cloned.1.call-start = ((), (), s32[]{:S(2)}) async-start(), calls=%async_computation.2 | async-start | bytes 3446784 | tf_op jit(solution)/shard_map/all_gather | solution.py:25
  124.7 60.3 %collective-permute-start.1 = (bf16[1408,2176]{1,0:T(8,128)(2,1)}, bf16[1408,2176]{1,0:T(8,128)(2,1)}, u32[]{:S(2)}, u32[]{:S(2)}) collective-permute-start(bf16[1408,2176]{1,0:T(8,128)(2,1)} %bitcast.3), channel_id=1, source_target_pairs={{0,8},{8,0},{1,9},{9,1},{2,10},{10,2},{3,11},{11,3},{4,12},{12,4},... | collective-permute-start | bytes 18382856 | tf_op jit(solution)/shard_map/ppermute | solution.py:31
  124.7 163.8 %reduce-scatter.2.cloned.1.call-start = ((), (), s32[]{:S(2)}) async-start(), calls=%async_computation.3 | async-start | bytes 11837440 | tf_op jit(solution)/shard_map/reduce_scatter | solution.py:38
  200.4 0.7 copy-start.1
  200.4 2.5 copy-start
  292.7 1.2 collective-permute-start.2
  296.0 5.1 %collective-permute-start.3 = (f32[545]{0:T(1024)S(1)}, f32[545]{0:T(1024)S(1)}, u32[]{:S(2)}, u32[]{:S(2)}) collective-permute-start(f32[545]{0:T(1024)S(1)} %pad_maximum_fusion.1), channel_id=1, source_target_pairs={{0,4},{2,6},{4,0},{6,2},{1,5},{3,7},{5,1},{7,3},{8,12},{10,14},{12... | collective-permute-start | bytes 6548 | tf_op jit(solution)/shard_map/ppermute | solution.py:52
  302.6 3.6 %collective-permute-start.4 = (f32[273]{0:T(512)S(1)}, f32[273]{0:T(512)S(1)}, u32[]{:S(2)}, u32[]{:S(2)}) collective-permute-start(f32[273]{0:T(512)S(1)} %pad_maximum_fusion.2), channel_id=1, source_target_pairs={{0,2},{2,0},{4,6},{6,4},{1,3},{3,1},{5,7},{7,5},{8,10},{10,8},{12,... | collective-permute-start | bytes 3284 | tf_op jit(solution)/shard_map/ppermute | solution.py:52
  307.5 9.4 %collective-permute-start.5 = (f32[273]{0:T(512)S(1)}, f32[273]{0:T(512)S(1)}, u32[]{:S(2)}, u32[]{:S(2)}) collective-permute-start(f32[273]{0:T(512)S(1)} %pad_maximum_fusion.3), channel_id=1, source_target_pairs={{0,0},{1,16},{2,1},{3,17},{4,2},{5,18},{6,3},{7,19},{8,4},{9,20},{... | collective-permute-start | bytes 3284 | tf_op jit(solution)/shard_map/ppermute | solution.py:68
Sparse Core Ops, SparseCore 0:
  32.4 102.2 all-gather.5
  136.8 48.0 all-gather.3
  200.5 87.9 reduce-scatter.1

commit v11 on v9

--- a/solution.py
+++ b/solution.py
@@ -18,8 +18,9 @@
     half = nvir // nc
     flip = [(k, k ^ 1) for k in range(nc)]
     column = lax.dynamic_index_in_dim(integrals, owner, 1, keepdims=False)
-    chip_rows = jnp.stack([column, lax.ppermute(column, "core", flip)])
-    mine = lax.dynamic_slice_in_dim(chip_rows, c * half, half, axis=2)
+    own_half = lax.dynamic_slice_in_dim(column, c * half, half, axis=1)
+    give_half = lax.dynamic_slice_in_dim(column, (1 - c) * half, half, axis=1)
+    mine = jnp.stack([own_half, lax.ppermute(give_half, "core", flip)])
     mine, integrals = lax.optimization_barrier((mine, integrals))
     by_orbital = jnp.transpose(integrals, (1, 0, 2))
     panel = lax.all_gather(mine, GROUP, axis=1, tiled=True)
@@ -42,27 +43,30 @@
 
     total = jnp.sum(part_rows)
     pieces = part_rows.reshape(nc, ny // 2, 2, blk)
-    for axis, bit, step, size in (("core", c, 1, nc), ("y", y // 2, 2, ny), ("y", y % 2, 1, ny)):
-        keep = lax.dynamic_index_in_dim(pieces, bit, 0, keepdims=False)
-        give = lax.dynamic_index_in_dim(pieces, 1 - bit, 0, keepdims=False)
-        flip = [(k, k ^ step) for k in range(size)]
-        got = lax.ppermute(jnp.concatenate([give.reshape(-1), total[None]]), axis, flip)
+    for bit, step, dim in ((y // 2, 2, 1), (y % 2, 1, 1)):
+        keep = lax.dynamic_index_in_dim(pieces, bit, dim, keepdims=False)
+        give = lax.dynamic_index_in_dim(pieces, 1 - bit, dim, keepdims=False)
+        moved = [(k, k ^ step) for k in range(ny)]
+        got = lax.ppermute(jnp.concatenate([give.reshape(-1), total[None]]), "y", moved)
         pieces = keep + got[:-1].reshape(keep.shape)
         total = total + got[-1]
-    rows = pieces.reshape(blk)
 
     def index(ll, cc, yy, hh):
         return ((ll * nc + cc) * ny + yy) * nh + hh
 
-    moves = []
-    for ll in range(nl):
-        for cc in range(nc):
-            for yy in range(ny):
-                for hh in range(nh):
-                    b = cc * ny + yy
-                    moves.append((index(ll, cc, yy, hh), index(hh, ll, b // nh, b % nh)))
-    packed = jnp.concatenate([rows, total[None]])
-    packed = lax.ppermute(packed, ("xl", "core", "y", "xh"), moves)
+    arrived = []
+    for j in range(nc):
+        moves = []
+        for ll in range(nl):
+            for cc in range(nc):
+                for yy in range(ny):
+                    for hh in range(nh):
+                        x = (cc ^ j) * ny + yy
+                        moves.append((index(ll, cc, yy, hh), index(hh, ll, x // nh, x % nh)))
+        piece = lax.dynamic_index_in_dim(pieces, c ^ j, 0, keepdims=False)
+        packed = jnp.concatenate([piece, total[None]])
+        arrived.append(lax.ppermute(packed, ("xl", "core", "y", "xh"), moves))
+    packed = arrived[0] + arrived[1]
     return packed[:blk].reshape(1, 1, blk), packed[blk:].reshape(1, 1)
 
 

time: 297 us -> 297 us (level)
  no operation moved by 1% of the time
where the time goes in v11:
time: 297 us
  waiting for transfers between devices  221 us (74%)
  matrix products  20.9 us (7%)
  between operations  19.3 us (6%)
  starting transfers between devices  16.1 us (5%)
  local copies, waits for them, and re-layouts  14.2 us (5%)
  other arithmetic  5.08 us (2%)
    all_to_all x1, waiting for transfers between devices, body(): left = lax.all_to_all(by_orbital, GROUP, 0, 0, tiled=True)  103 us
    reduce_scatter x1, waiting for transfers between devices, body(): summed = lax.psum_scatter(partial_sum, 'y', scatter_dimension=1, tiled=True)  88.3 us
    dot_general x1, matrix products, body(): lax.dot_general(left, panel, (((0,), (0,)), ((), ())), preferred_element_...  20.9 us
    all_gather x1, waiting for transfers between devices, body(): panel = lax.all_gather(mine, GROUP, axis=1, tiled=True)  15.5 us
    all_to_all x1, starting transfers between devices, body(): left = lax.all_to_all(by_orbital, GROUP, 0, 0, tiled=True)  8.29 us
    ppermute x2, waiting for transfers between devices, body(): arrived.append(lax.ppermute(packed, ('xl', 'core', 'y', 'xh'), moves))  6.84 us
    optimization_barrier x1, local copies, waits for them, and re-layouts, body(): mine, integrals = lax.optimization_barrier((mine, integrals))  6.48 us
  transfers between devices with their start and end apart: 9, of which 8 were waited for; matrix products, arithmetic and copies ran while one was open for 0% of the time, Pallas kernels for 0%

profile of v11, /device:TPU:12, one launch (start us, length us, event | category | flops | bytes accessed | tf_op | source)
XLA Modules:
  0.0 296.9 jit_solution(5964640132555902552)
XLA Ops:
  9.1 3.6 %constant_dynamic-slice_fusion.5 = (bf16[88,1,1088]{2,1,0:T(2,128)(2,1)S(1)}, bf16[88,1,1088]{2,1,0:T(2,128)(2,1)S(1)}) fusion(bf16[88,16,2176]{2,1,0:T(8,128)(2,1)} %param.4, s32[]{:T(128)S(6)} %select_n.57, s32[]{:T(128)S(6)} %select_n.59, s32[]{:T(128)S(6)} %select_n.61), kind=kLoop, calls=%fused_computation.24 | loop fusion | bytes 765964 | tf_op jit(solution)/shard_map/dynamic_slice | solution.py:21
  12.7 0.1 collective-permute-start
  12.8 1.4 collective-permute-done
  14.3 0.8 pad_maximum_fusion
  15.1 6.5 %copy.16 = bf16[88,16,2176]{2,0,1:T(8,128)(2,1)} copy(bf16[88,16,2176]{2,1,0:T(8,128)(2,1)} %param.4) | data formatting | bytes 12255232 | tf_op jit(solution)/shard_map/optimization_barrier | solution.py:24
  21.5 8.3 %all-to-all-start = ((bf16[16,88,2176]{2,1,0:T(8,128)(2,1)}), bf16[16,88,2176]{2,1,0:T(8,128)(2,1)}, u32[]{:S(2)}, u32[]{:S(2)}) async-start(bf16[16,88,2176]{2,1,0:T(8,128)(2,1)} %bitcast.29), calls=%async_computation | async-start | bytes 12255232 | tf_op jit(solution)/shard_map/all_to_all | solution.py:29
  29.8 0.0 all-gather.2.cloned.1.call-start
  29.9 0.7 all-gather.2.cloned.1.call-update
  30.6 0.0 reduce-scatter.2.cloned.1.call-start
  30.6 103.1 %all-to-all-done = bf16[16,88,2176]{2,1,0:T(8,128)(2,1)} async-done(((bf16[16,88,2176]{2,1,0:T(8,128)(2,1)}), bf16[16,88,2176]{2,1,0:T(8,128)(2,1)}, u32[]{:S(2)}, u32[]{:S(2)}) %all-to-all-start) | async-done | bytes 6127648 | tf_op jit(solution)/shard_map/all_to_all | solution.py:29
  133.7 0.0 collective-permute-start.1
  133.7 15.5 %all-gather.2.cloned.1.call-done = bf16[2,1408,1088]{2,1,0:T(8,128)(2,1)} async-done(((bf16[2,88,1088]{2,1,0:T(8,128)(2,1)}), bf16[2,1408,1088]{2,1,0:T(8,128)(2,1)}) %all-gather.2.cloned.1.call-update) | async-done | bytes 6127632 | tf_op jit(solution)/shard_map/all_gather | solution.py:26
  149.3 0.0 collective-permute-done.1
  149.3 20.9 %fusion = f32[2176,1088]{0,1:T(8,128)} fusion(bf16[2816,1088]{1,0:T(8,128)(2,1)} %bitcast.39, bf16[1408,2176]{1,0:T(8,128)(2,1)} %collective-permute-done.1, bf16[1408,2176]{1,0:T(8,128)(2,1)} %bitcast.5), kind=kOutput, calls=%fused_computation | convolution fusion | flops 13358202880 | bytes 27852800 | tf_op jit(solution)/shard_map/dot_general | solution.py:33
  170.1 0.0 copy-start.1
  170.2 0.0 copy-start
  170.2 0.0 reduce-scatter.2.cloned.1.call-update
  170.2 0.6 copy-done.1
  170.8 0.6 fusion.9
  172.7 0.0 copy-done
  172.7 0.1 dynamic_slice.46
  172.8 88.3 %reduce-scatter.2.cloned.1.call-done = f32[2176,272]{0,1:T(8,128)} async-done(((f32[2176,1088]{0,1:T(8,128)}), f32[2176,272]{0,1:T(8,128)}) %reduce-scatter.2.cloned.1.call-update) | async-done | bytes 2367504 | tf_op jit(solution)/shard_map/reduce_scatter | solution.py:36
  261.1 3.3 %fusion.5 = (f32[2176]{0:T(1024)S(1)}, f32[]{:T(128)}) fusion(f32[272]{0:T(512)S(1)} %dynamic_slice.46, f32[2176]{0:T(1024)S(1)} %broadcast_subtract_fusion, f32[2176,272]{0,1:T(8,128)} %reduce-scatter.2.cloned.1.call-done), kind=kLoop, calls=%fused_computation.10 | loop fusion | flops 2957183 | bytes 2385988 | tf_op jit(solution)/shard_map/reduce_sum | solution.py:42
  264.4 0.1 reshape.42
  264.5 0.1 reshape.43
  264.6 0.7 pad_maximum_fusion.1
  265.3 1.5 collective-permute-start.2
  266.8 3.7 %collective-permute-done.2 = f32[1089]{0:T(1024)S(1)} collective-permute-done((f32[1089]{0:T(1024)S(1)}, f32[1089]{0:T(1024)S(1)}, u32[]{:S(2)}, u32[]{:S(2)}) %collective-permute-start.2) | collective-permute-done | bytes 4388 | tf_op jit(solution)/shard_map/ppermute | solution.py:50
  270.4 0.1 reshape.44
  270.6 0.1 reshape.45
  270.7 0.6 slice.29
  272.5 0.1 pad_maximum_fusion.2
  272.6 1.8 collective-permute-start.3
  274.4 1.8 collective-permute-done.3
  276.2 0.1 reshape.46
  276.3 0.6 slice.25
  277.6 0.1 pad_maximum_fusion.3
  277.7 1.8 collective-permute-start.5
  279.5 0.1 pad_maximum_fusion.4
  279.6 2.5 collective-permute-start.4
  282.1 2.5 collective-permute-done.5
  284.6 4.3 %collective-permute-done.4 = f32[273]{0:T(512)S(1)} collective-permute-done((f32[273]{0:T(512)S(1)}, f32[273]{0:T(512)S(1)}, u32[]{:S(2)}, u32[]{:S(2)}) %collective-permute-start.4) | collective-permute-done | bytes 1124 | tf_op jit(solution)/shard_map/ppermute | solution.py:68
  289.0 0.6 slice.27
  289.5 0.6 reshape.47
  (9 shorter events, 0.1 us)
Async XLA Ops:
  12.7 1.5 collective-permute-start
  21.5 112.2 %all-to-all-start = ((bf16[16,88,2176]{2,1,0:T(8,128)(2,1)}), bf16[16,88,2176]{2,1,0:T(8,128)(2,1)}, u32[]{:S(2)}, u32[]{:S(2)}) async-start(bf16[16,88,2176]{2,1,0:T(8,128)(2,1)} %bitcast.29), calls=%async_computation | async-start | bytes 12255232 | tf_op jit(solution)/shard_map/all_to_all | solution.py:29
  29.8 119.4 %all-gather.2.cloned.1.call-start = ((), (), s32[]{:S(2)}) async-start(), calls=%async_computation.2 | async-start | bytes 6893568 | tf_op jit(solution)/shard_map/all_gather | solution.py:26
  30.6 230.5 %reduce-scatter.2.cloned.1.call-start = ((), (), s32[]{:S(2)}) async-start(), calls=%async_computation.3 | async-start | bytes 11837440 | tf_op jit(solution)/shard_map/reduce_scatter | solution.py:36
  133.7 15.6 %collective-permute-start.1 = (bf16[1408,2176]{1,0:T(8,128)(2,1)}, bf16[1408,2176]{1,0:T(8,128)(2,1)}, u32[]{:S(2)}, u32[]{:S(2)}) collective-permute-start(bf16[1408,2176]{1,0:T(8,128)(2,1)} %bitcast.5), channel_id=1, source_target_pairs={{0,8},{8,0},{1,9},{9,1},{2,10},{10,2},{3,11},{11,3},{4,12},{12,4},... | collective-permute-start | bytes 18382856 | tf_op jit(solution)/shard_map/ppermute | solution.py:31
  170.1 0.7 copy-start.1
  170.2 2.5 copy-start
  265.3 5.2 %collective-permute-start.2 = (f32[1089]{0:T(1024)S(1)}, f32[1089]{0:T(1024)S(1)}, u32[]{:S(2)}, u32[]{:S(2)}) collective-permute-start(f32[1089]{0:T(1024)S(1)} %pad_maximum_fusion.1), channel_id=1, source_target_pairs={{0,4},{2,6},{4,0},{6,2},{1,5},{3,7},{5,1},{7,3},{8,12},{10,14},{12... | collective-permute-start | bytes 13076 | tf_op jit(solution)/shard_map/ppermute | solution.py:50
  272.6 3.6 %collective-permute-start.3 = (f32[545]{0:T(1024)S(1)}, f32[545]{0:T(1024)S(1)}, u32[]{:S(2)}, u32[]{:S(2)}) collective-permute-start(f32[545]{0:T(1024)S(1)} %pad_maximum_fusion.2), channel_id=1, source_target_pairs={{0,2},{2,0},{4,6},{6,4},{1,3},{3,1},{5,7},{7,5},{8,10},{10,8},{12,... | collective-permute-start | bytes 6548 | tf_op jit(solution)/shard_map/ppermute | solution.py:50
  277.7 6.9 %collective-permute-start.5 = (f32[273]{0:T(512)S(1)}, f32[273]{0:T(512)S(1)}, u32[]{:S(2)}, u32[]{:S(2)}) collective-permute-start(f32[273]{0:T(512)S(1)} %pad_maximum_fusion.3), channel_id=1, source_target_pairs={{0,4},{1,20},{2,5},{3,21},{4,6},{5,22},{6,7},{7,23},{8,0},{9,16},{... | collective-permute-start | bytes 3284 | tf_op jit(solution)/shard_map/ppermute | solution.py:68
  279.6 9.4 %collective-permute-start.4 = (f32[273]{0:T(512)S(1)}, f32[273]{0:T(512)S(1)}, u32[]{:S(2)}, u32[]{:S(2)}) collective-permute-start(f32[273]{0:T(512)S(1)} %pad_maximum_fusion.4), channel_id=1, source_target_pairs={{0,0},{1,16},{2,1},{3,17},{4,2},{5,18},{6,3},{7,19},{8,4},{9,20},{... | collective-permute-start | bytes 3284 | tf_op jit(solution)/shard_map/ppermute | solution.py:68
Sparse Core Ops, SparseCore 0:
  32.8 116.3 all-gather.1
  170.3 90.7 reduce-scatter.1

commit v12 on v11

--- a/solution.py
+++ b/solution.py
@@ -3,7 +3,7 @@
 from jax import lax
 from jax.sharding import Mesh, PartitionSpec as P
 
-GROUP = ("z", "xh", "xl")
+GROUP = ("xh", "xl", "z")
 
 
 def body(integrals, owner_order, occ_energy, vir_energy):
@@ -11,7 +11,8 @@
     ny, nh, nc, nl = lax.axis_size("y"), lax.axis_size("xh"), lax.axis_size("core"), lax.axis_size("xl")
     blk = nvir // (ny * nh)
     z, l, y, h, c = (lax.axis_index(a) for a in ("z", "xl", "y", "xh", "core"))
-    orbital = (z * nh + h) * nl + l
+    nz = lax.axis_size("z")
+    orbital = (h * nl + l) * nz + z
     block = c * ny + y
 
     owner = owner_order[0]
@@ -51,21 +52,24 @@
         pieces = keep + got[:-1].reshape(keep.shape)
         total = total + got[-1]
 
-    def index(ll, cc, yy, hh):
-        return ((ll * nc + cc) * ny + yy) * nh + hh
+    def index(zz, ll, cc, yy, hh):
+        return (((zz * nl + ll) * nc + cc) * ny + yy) * nh + hh
 
     arrived = []
     for j in range(nc):
         moves = []
-        for ll in range(nl):
-            for cc in range(nc):
-                for yy in range(ny):
-                    for hh in range(nh):
-                        x = (cc ^ j) * ny + yy
-                        moves.append((index(ll, cc, yy, hh), index(hh, ll, x // nh, x % nh)))
+        for zz in range(nz):
+            for ll in range(nl):
+                for cc in range(nc):
+                    for yy in range(ny):
+                        for hh in range(nh):
+                            o = (hh * nl + ll) * nz + zz
+                            x = (cc ^ j) * ny + yy
+                            dest = index(o // (nl * nc), (o // nc) % nl, o % nc, x // nh, x % nh)
+                            moves.append((index(zz, ll, cc, yy, hh), dest))
         piece = lax.dynamic_index_in_dim(pieces, c ^ j, 0, keepdims=False)
         packed = jnp.concatenate([piece, total[None]])
-        arrived.append(lax.ppermute(packed, ("xl", "core", "y", "xh"), moves))
+        arrived.append(lax.ppermute(packed, ("z", "xl", "core", "y", "xh"), moves))
     packed = arrived[0] + arrived[1]
     return packed[:blk].reshape(1, 1, blk), packed[blk:].reshape(1, 1)
 

time: 297 us -> 313 us (1.054)
  waiting for transfers between devices: 221 us -> 232 us
  starting transfers between devices: 16.1 us -> 19.5 us
    all_gather x1, waiting for transfers between devices: 15.5 us -> 28.2 us  [body(): panel = lax.all_gather(mine, GROUP, axis=1, tiled=True)]
    ppermute x2, starting transfers between devices: 4.35 us -> 7.74 us  [body(): arrived.append(lax.ppermute(packed, ('z', 'xl', 'core', 'y', 'xh'), moves))]
  transfers between devices with their start and end apart: 9 -> 9, of which waited for: 8 -> 7; matrix products, arithmetic and copies ran while one was open for 0% -> 0% of each run, Pallas kernels for 0% -> 0%
where the time goes in v12:
time: 313 us; the launch traced here: 311 us
  waiting for transfers between devices  232 us (74%)
  matrix products  20.9 us (7%)
  starting transfers between devices  19.5 us (6%)
  between operations  19.4 us (6%)
  local copies, waits for them, and re-layouts  14.2 us (5%)
  other arithmetic  5.08 us (2%)
    all_to_all x1, waiting for transfers between devices, body(): left = lax.all_to_all(by_orbital, GROUP, 0, 0, tiled=True)  103 us
    reduce_scatter x1, waiting for transfers between devices, body(): summed = lax.psum_scatter(partial_sum, 'y', scatter_dimension=1, tiled=True)  87.3 us
    all_gather x1, waiting for transfers between devices, body(): panel = lax.all_gather(mine, GROUP, axis=1, tiled=True)  28.2 us
    dot_general x1, matrix products, body(): lax.dot_general(left, panel, (((0,), (0,)), ((), ())), preferred_element_...  20.9 us
    all_to_all x1, starting transfers between devices, body(): left = lax.all_to_all(by_orbital, GROUP, 0, 0, tiled=True)  8.3 us
    ppermute x2, starting transfers between devices, body(): arrived.append(lax.ppermute(packed, ('z', 'xl', 'core', 'y', 'xh'), moves))  7.74 us
    optimization_barrier x1, local copies, waits for them, and re-layouts, body(): mine, integrals = lax.optimization_barrier((mine, integrals))  6.48 us
  transfers between devices with their start and end apart: 9, of which 7 were waited for; matrix products, arithmetic and copies ran while one was open for 0% of the time, Pallas kernels for 0%

profile of v12, /device:TPU:12, one launch (start us, length us, event | category | flops | bytes accessed | tf_op | source)
XLA Modules:
  0.0 310.6 jit_solution(8352102755774171732)
XLA Ops:
  9.1 3.6 %constant_dynamic-slice_fusion.5 = (bf16[88,1,1088]{2,1,0:T(2,128)(2,1)S(1)}, bf16[88,1,1088]{2,1,0:T(2,128)(2,1)S(1)}) fusion(bf16[88,16,2176]{2,1,0:T(8,128)(2,1)} %param.4, s32[]{:T(128)S(6)} %select_n.57, s32[]{:T(128)S(6)} %select_n.59, s32[]{:T(128)S(6)} %select_n.61), kind=kLoop, calls=%fused_computation.24 | loop fusion | bytes 765964 | tf_op jit(solution)/shard_map/dynamic_slice | solution.py:22
  12.7 0.1 collective-permute-start
  12.8 1.4 collective-permute-done
  14.3 0.8 pad_maximum_fusion
  15.1 6.5 %copy.16 = bf16[88,16,2176]{2,0,1:T(8,128)(2,1)} copy(bf16[88,16,2176]{2,1,0:T(8,128)(2,1)} %param.4) | data formatting | bytes 12255232 | tf_op jit(solution)/shard_map/optimization_barrier | solution.py:25
  21.5 8.3 %all-to-all-start = ((bf16[16,88,2176]{2,1,0:T(8,128)(2,1)}), bf16[16,88,2176]{2,1,0:T(8,128)(2,1)}, u32[]{:S(2)}, u32[]{:S(2)}) async-start(bf16[16,88,2176]{2,1,0:T(8,128)(2,1)} %bitcast.29), calls=%async_computation | async-start | bytes 12255232 | tf_op jit(solution)/shard_map/all_to_all | solution.py:30
  29.8 0.0 all-gather.2.cloned.1.call-start
  29.9 0.7 all-gather.2.cloned.1.call-update
  30.6 0.0 reduce-scatter.2.cloned.1.call-start
  30.6 103.1 %all-to-all-done = bf16[16,88,2176]{2,1,0:T(8,128)(2,1)} async-done(((bf16[16,88,2176]{2,1,0:T(8,128)(2,1)}), bf16[16,88,2176]{2,1,0:T(8,128)(2,1)}, u32[]{:S(2)}, u32[]{:S(2)}) %all-to-all-start) | async-done | bytes 6127648 | tf_op jit(solution)/shard_map/all_to_all | solution.py:30
  133.7 0.0 collective-permute-start.1
  133.7 28.2 %all-gather.2.cloned.1.call-done = bf16[2,1408,1088]{2,1,0:T(8,128)(2,1)} async-done(((bf16[2,88,1088]{2,1,0:T(8,128)(2,1)}), bf16[2,1408,1088]{2,1,0:T(8,128)(2,1)}) %all-gather.2.cloned.1.call-update) | async-done | bytes 6127632 | tf_op jit(solution)/shard_map/all_gather | solution.py:27
  161.9 0.0 collective-permute-done.1
  161.9 20.9 %fusion = f32[2176,1088]{0,1:T(8,128)} fusion(bf16[2816,1088]{1,0:T(8,128)(2,1)} %bitcast.39, bf16[1408,2176]{1,0:T(8,128)(2,1)} %collective-permute-done.1, bf16[1408,2176]{1,0:T(8,128)(2,1)} %bitcast.5), kind=kOutput, calls=%fused_computation | convolution fusion | flops 13358202880 | bytes 27852800 | tf_op jit(solution)/shard_map/dot_general | solution.py:34
  182.8 0.0 copy-start.1
  182.8 0.0 copy-start
  182.8 0.0 reduce-scatter.2.cloned.1.call-update
  182.9 0.6 copy-done.1
  183.5 0.6 fusion.9
  185.4 0.0 copy-done
  185.4 0.1 dynamic_slice.46
  185.5 87.3 %reduce-scatter.2.cloned.1.call-done = f32[2176,272]{0,1:T(8,128)} async-done(((f32[2176,1088]{0,1:T(8,128)}), f32[2176,272]{0,1:T(8,128)}) %reduce-scatter.2.cloned.1.call-update) | async-done | bytes 2367504 | tf_op jit(solution)/shard_map/reduce_scatter | solution.py:37
  272.8 3.3 %fusion.5 = (f32[2176]{0:T(1024)S(1)}, f32[]{:T(128)}) fusion(f32[272]{0:T(512)S(1)} %dynamic_slice.46, f32[2176]{0:T(1024)S(1)} %broadcast_subtract_fusion, f32[2176,272]{0,1:T(8,128)} %reduce-scatter.2.cloned.1.call-done), kind=kLoop, calls=%fused_computation.10 | loop fusion | flops 2957183 | bytes 2385988 | tf_op jit(solution)/shard_map/reduce_sum | solution.py:43
  276.1 0.1 reshape.42
  276.2 0.1 reshape.43
  276.3 0.7 pad_maximum_fusion.1
  277.0 1.5 collective-permute-start.2
  278.5 3.7 %collective-permute-done.2 = f32[1089]{0:T(1024)S(1)} collective-permute-done((f32[1089]{0:T(1024)S(1)}, f32[1089]{0:T(1024)S(1)}, u32[]{:S(2)}, u32[]{:S(2)}) %collective-permute-start.2) | collective-permute-done | bytes 4388 | tf_op jit(solution)/shard_map/ppermute | solution.py:51
  282.2 0.1 reshape.44
  282.3 0.1 reshape.45
  282.4 0.6 slice.29
  284.2 0.1 pad_maximum_fusion.2
  284.3 1.8 collective-permute-start.3
  286.1 1.8 collective-permute-done.3
  287.9 0.1 reshape.46
  288.0 0.6 slice.25
  289.3 0.1 pad_maximum_fusion.3
  289.4 3.8 %collective-permute-start.5 = (f32[273]{0:T(512)S(1)}, f32[273]{0:T(512)S(1)}, u32[]{:S(2)}, u32[]{:S(2)}) collective-permute-start(f32[273]{0:T(512)S(1)} %pad_maximum_fusion.3), channel_id=1, source_target_pairs={{0,4},{1,68},{2,5},{3,69},{4,6},{5,70},{6,7},{7,71},{8,0},{9,64},{... | collective-permute-start | bytes 3284 | tf_op jit(solution)/shard_map/ppermute | solution.py:72
  293.2 0.1 pad_maximum_fusion.4
  293.3 3.9 %collective-permute-start.4 = (f32[273]{0:T(512)S(1)}, f32[273]{0:T(512)S(1)}, u32[]{:S(2)}, u32[]{:S(2)}) collective-permute-start(f32[273]{0:T(512)S(1)} %pad_maximum_fusion.4), channel_id=1, source_target_pairs={{0,0},{1,64},{2,1},{3,65},{4,2},{5,66},{6,3},{7,67},{8,4},{9,68},{... | collective-permute-start | bytes 3284 | tf_op jit(solution)/shard_map/ppermute | solution.py:72
  297.2 0.0 collective-permute-done.5
  297.2 5.4 %collective-permute-done.4 = f32[273]{0:T(512)S(1)} collective-permute-done((f32[273]{0:T(512)S(1)}, f32[273]{0:T(512)S(1)}, u32[]{:S(2)}, u32[]{:S(2)}) %collective-permute-start.4) | collective-permute-done | bytes 1124 | tf_op jit(solution)/shard_map/ppermute | solution.py:72
  302.6 0.6 slice.27
  303.2 0.6 reshape.47
  (9 shorter events, 0.1 us)
Async XLA Ops:
  12.7 1.5 collective-permute-start
  21.5 112.2 %all-to-all-start = ((bf16[16,88,2176]{2,1,0:T(8,128)(2,1)}), bf16[16,88,2176]{2,1,0:T(8,128)(2,1)}, u32[]{:S(2)}, u32[]{:S(2)}) async-start(bf16[16,88,2176]{2,1,0:T(8,128)(2,1)} %bitcast.29), calls=%async_computation | async-start | bytes 12255232 | tf_op jit(solution)/shard_map/all_to_all | solution.py:30
  29.8 132.1 %all-gather.2.cloned.1.call-start = ((), (), s32[]{:S(2)}) async-start(), calls=%async_computation.2 | async-start | bytes 6893568 | tf_op jit(solution)/shard_map/all_gather | solution.py:27
  30.6 242.2 %reduce-scatter.2.cloned.1.call-start = ((), (), s32[]{:S(2)}) async-start(), calls=%async_computation.3 | async-start | bytes 11837440 | tf_op jit(solution)/shard_map/reduce_scatter | solution.py:37
  133.7 28.2 %collective-permute-start.1 = (bf16[1408,2176]{1,0:T(8,128)(2,1)}, bf16[1408,2176]{1,0:T(8,128)(2,1)}, u32[]{:S(2)}, u32[]{:S(2)}) collective-permute-start(bf16[1408,2176]{1,0:T(8,128)(2,1)} %bitcast.5), channel_id=1, source_target_pairs={{0,8},{8,0},{1,9},{9,1},{2,10},{10,2},{3,11},{11,3},{4,12},{12,4},... | collective-permute-start | bytes 18382856 | tf_op jit(solution)/shard_map/ppermute | solution.py:32
  182.8 0.7 copy-start.1
  182.8 2.5 copy-start
  277.0 5.2 %collective-permute-start.2 = (f32[1089]{0:T(1024)S(1)}, f32[1089]{0:T(1024)S(1)}, u32[]{:S(2)}, u32[]{:S(2)}) collective-permute-start(f32[1089]{0:T(1024)S(1)} %pad_maximum_fusion.1), channel_id=1, source_target_pairs={{0,4},{2,6},{4,0},{6,2},{1,5},{3,7},{5,1},{7,3},{8,12},{10,14},{12... | collective-permute-start | bytes 13076 | tf_op jit(solution)/shard_map/ppermute | solution.py:51
  284.3 3.6 %collective-permute-start.3 = (f32[545]{0:T(1024)S(1)}, f32[545]{0:T(1024)S(1)}, u32[]{:S(2)}, u32[]{:S(2)}) collective-permute-start(f32[545]{0:T(1024)S(1)} %pad_maximum_fusion.2), channel_id=1, source_target_pairs={{0,2},{2,0},{4,6},{6,4},{1,3},{3,1},{5,7},{7,5},{8,10},{10,8},{12,... | collective-permute-start | bytes 6548 | tf_op jit(solution)/shard_map/ppermute | solution.py:51
  289.4 7.8 %collective-permute-start.5 = (f32[273]{0:T(512)S(1)}, f32[273]{0:T(512)S(1)}, u32[]{:S(2)}, u32[]{:S(2)}) collective-permute-start(f32[273]{0:T(512)S(1)} %pad_maximum_fusion.3), channel_id=1, source_target_pairs={{0,4},{1,68},{2,5},{3,69},{4,6},{5,70},{6,7},{7,71},{8,0},{9,64},{... | collective-permute-start | bytes 3284 | tf_op jit(solution)/shard_map/ppermute | solution.py:72
  293.3 9.4 %collective-permute-start.4 = (f32[273]{0:T(512)S(1)}, f32[273]{0:T(512)S(1)}, u32[]{:S(2)}, u32[]{:S(2)}) collective-permute-start(f32[273]{0:T(512)S(1)} %pad_maximum_fusion.4), channel_id=1, source_target_pairs={{0,0},{1,64},{2,1},{3,65},{4,2},{5,66},{6,3},{7,67},{8,4},{9,68},{... | collective-permute-start | bytes 3284 | tf_op jit(solution)/shard_map/ppermute | solution.py:72
Sparse Core Ops, SparseCore 0:
  32.8 129.0 all-gather.1
  183.0 89.7 reduce-scatter.1

commit v13 on v11

--- a/solution.py
+++ b/solution.py
@@ -42,13 +42,14 @@
     part_rows = jnp.sum(summed * summed / denominator, axis=1)
 
     total = jnp.sum(part_rows)
-    pieces = part_rows.reshape(nc, ny // 2, 2, blk)
-    for bit, step, dim in ((y // 2, 2, 1), (y % 2, 1, 1)):
-        keep = lax.dynamic_index_in_dim(pieces, bit, dim, keepdims=False)
-        give = lax.dynamic_index_in_dim(pieces, 1 - bit, dim, keepdims=False)
-        moved = [(k, k ^ step) for k in range(ny)]
-        got = lax.ppermute(jnp.concatenate([give.reshape(-1), total[None]]), "y", moved)
-        pieces = keep + got[:-1].reshape(keep.shape)
+    by_y = part_rows.reshape(nc, ny, blk)
+    pieces = lax.dynamic_index_in_dim(by_y, y, 1, keepdims=False)
+    sent_total = total
+    for shift in range(1, ny):
+        give = lax.dynamic_index_in_dim(by_y, (y + shift) % ny, 1, keepdims=False)
+        moved = [(k, (k + shift) % ny) for k in range(ny)]
+        got = lax.ppermute(jnp.concatenate([give.reshape(-1), sent_total[None]]), "y", moved)
+        pieces = pieces + got[:-1].reshape(pieces.shape)
         total = total + got[-1]
 
     def index(ll, cc, yy, hh):

time: 297 us -> 298 us (level)
  waiting for transfers between devices: 221 us -> 217 us
    ppermute x2 -> x3, waiting for transfers between devices: 5.51 us -> 2.01 us  [body(): lax.ppermute(jnp.concatenate([give.reshape(-1), sent_total[None]]), 'y',...]
  transfers between devices with their start and end apart: 9 -> 10, of which waited for: 8 -> 8; matrix products, arithmetic and copies ran while one was open for 0% -> 1% of each run, Pallas kernels for 0% -> 0%
where the time goes in v13:
time: 298 us; the launch traced here: 297 us
  waiting for transfers between devices  217 us (73%)
  matrix products  21 us (7%)
  between operations  20 us (7%)
  starting transfers between devices  17.8 us (6%)
  local copies, waits for them, and re-layouts  14.9 us (5%)
  other arithmetic  6.44 us (2%)
    all_to_all x1, waiting for transfers between devices, body(): left = lax.all_to_all(by_orbital, GROUP, 0, 0, tiled=True)  103 us
    reduce_scatter x1, waiting for transfers between devices, body(): summed = lax.psum_scatter(partial_sum, 'y', scatter_dimension=1, tiled=True)  88.3 us
    dot_general x1, matrix products, body(): lax.dot_general(left, panel, (((0,), (0,)), ((), ())), preferred_element_...  21 us
    all_gather x1, waiting for transfers between devices, body(): panel = lax.all_gather(mine, GROUP, axis=1, tiled=True)  15.5 us
    all_to_all x1, starting transfers between devices, body(): left = lax.all_to_all(by_orbital, GROUP, 0, 0, tiled=True)  8.29 us
    optimization_barrier x1, local copies, waits for them, and re-layouts, body(): mine, integrals = lax.optimization_barrier((mine, integrals))  6.5 us
    ppermute x2, waiting for transfers between devices, body(): arrived.append(lax.ppermute(packed, ('xl', 'core', 'y', 'xh'), moves))  6.26 us
  transfers between devices with their start and end apart: 10, of which 8 were waited for; matrix products, arithmetic and copies ran while one was open for 1% of the time, Pallas kernels for 0%

profile of v13, /device:TPU:12, one launch (start us, length us, event | category | flops | bytes accessed | tf_op | source)
XLA Modules:
  0.0 297.4 jit_solution(13899239676093003810)
XLA Ops:
  9.1 3.6 %constant_dynamic-slice_fusion.4 = (bf16[88,1,1088]{2,1,0:T(2,128)(2,1)S(1)}, bf16[88,1,1088]{2,1,0:T(2,128)(2,1)S(1)}) fusion(bf16[88,16,2176]{2,1,0:T(8,128)(2,1)} %param.4, s32[]{:T(128)S(6)} %select_n.60, s32[]{:T(128)S(6)} %select_n.62, s32[]{:T(128)S(6)} %select_n.64), kind=kLoop, calls=%fused_computation.27 | loop fusion | bytes 765964 | tf_op jit(solution)/shard_map/dynamic_slice | solution.py:21
  12.7 0.1 collective-permute-start
  12.8 1.4 collective-permute-done
  14.3 0.8 pad_maximum_fusion
  15.1 6.5 %copy.16 = bf16[88,16,2176]{2,0,1:T(8,128)(2,1)} copy(bf16[88,16,2176]{2,1,0:T(8,128)(2,1)} %param.4) | data formatting | bytes 12255232 | tf_op jit(solution)/shard_map/optimization_barrier | solution.py:24
  21.6 8.3 %all-to-all-start = ((bf16[16,88,2176]{2,1,0:T(8,128)(2,1)}), bf16[16,88,2176]{2,1,0:T(8,128)(2,1)}, u32[]{:S(2)}, u32[]{:S(2)}) async-start(bf16[16,88,2176]{2,1,0:T(8,128)(2,1)} %bitcast.32), calls=%async_computation | async-start | bytes 12255232 | tf_op jit(solution)/shard_map/all_to_all | solution.py:29
  29.9 0.0 all-gather.2.cloned.1.call-start
  29.9 0.7 all-gather.2.cloned.1.call-update
  30.6 0.0 reduce-scatter.2.cloned.1.call-start
  30.6 103.1 %all-to-all-done = bf16[16,88,2176]{2,1,0:T(8,128)(2,1)} async-done(((bf16[16,88,2176]{2,1,0:T(8,128)(2,1)}), bf16[16,88,2176]{2,1,0:T(8,128)(2,1)}, u32[]{:S(2)}, u32[]{:S(2)}) %all-to-all-start) | async-done | bytes 6127648 | tf_op jit(solution)/shard_map/all_to_all | solution.py:29
  133.7 0.0 collective-permute-start.1
  133.7 15.5 %all-gather.2.cloned.1.call-done = bf16[2,1408,1088]{2,1,0:T(8,128)(2,1)} async-done(((bf16[2,88,1088]{2,1,0:T(8,128)(2,1)}), bf16[2,1408,1088]{2,1,0:T(8,128)(2,1)}) %all-gather.2.cloned.1.call-update) | async-done | bytes 6127632 | tf_op jit(solution)/shard_map/all_gather | solution.py:26
  149.3 0.0 collective-permute-done.1
  149.3 21.0 %fusion = f32[2176,1088]{0,1:T(8,128)} fusion(bf16[2816,1088]{1,0:T(8,128)(2,1)} %bitcast.43, bf16[1408,2176]{1,0:T(8,128)(2,1)} %collective-permute-done.1, bf16[1408,2176]{1,0:T(8,128)(2,1)} %bitcast.5), kind=kOutput, calls=%fused_computation | convolution fusion | flops 13358202880 | bytes 27852800 | tf_op jit(solution)/shard_map/dot_general | solution.py:33
  170.3 0.0 reduce-scatter.2.cloned.1.call-update
  170.4 0.6 copy-done.1
  171.0 0.6 fusion.11
  172.9 0.1 dynamic_slice.45
  173.0 88.3 %reduce-scatter.2.cloned.1.call-done = f32[2176,272]{0,1:T(8,128)} async-done(((f32[2176,1088]{0,1:T(8,128)}), f32[2176,272]{0,1:T(8,128)}) %reduce-scatter.2.cloned.1.call-update) | async-done | bytes 2367504 | tf_op jit(solution)/shard_map/reduce_scatter | solution.py:36
  261.2 3.3 %fusion.5 = (f32[2176]{0:T(1024)S(1)}, f32[]{:T(128)}) fusion(f32[272]{0:T(512)S(1)} %dynamic_slice.45, f32[2176]{0:T(1024)S(1)} %broadcast_subtract_fusion, f32[2176,272]{0,1:T(8,128)} %reduce-scatter.2.cloned.1.call-done), kind=kLoop, calls=%fused_computation.10 | loop fusion | flops 2957183 | bytes 2385988 | tf_op jit(solution)/shard_map/reduce_sum | solution.py:42
  264.5 0.1 reshape.49
  264.6 0.1 dynamic-slice_reduce_fusion
  264.7 0.1 reshape.54
  264.8 0.7 pad_maximum_fusion.1
  265.5 1.8 collective-permute-start.4
  267.3 0.1 reshape.52
  267.4 0.7 pad_maximum_fusion.2
  268.1 0.9 collective-permute-start.3
  269.0 0.1 reshape.50
  269.0 0.7 pad_maximum_fusion.3
  269.7 1.4 collective-permute-start.2
  271.2 0.0 collective-permute-done.4
  271.2 0.1 reshape.55
  271.3 1.9 collective-permute-done.3
  273.2 0.1 reshape.53
  273.3 0.1 collective-permute-done.2
  273.4 0.1 reshape.51
  273.4 0.6 slice.31
  275.3 0.6 slice.32
  276.6 0.6 slice.33
  277.8 0.1 pad_maximum_fusion.4
  277.9 2.1 collective-permute-start.6
  280.0 0.1 pad_maximum_fusion.5
  280.1 3.1 %collective-permute-start.5 = (f32[273]{0:T(512)S(1)}, f32[273]{0:T(512)S(1)}, u32[]{:S(2)}, u32[]{:S(2)}) collective-permute-start(f32[273]{0:T(512)S(1)} %pad_maximum_fusion.5), channel_id=1, source_target_pairs={{0,0},{1,16},{2,1},{3,17},{4,2},{5,18},{6,3},{7,19},{8,4},{9,20},{... | collective-permute-start | bytes 3284 | tf_op jit(solution)/shard_map/ppermute | solution.py:69
  283.2 1.7 collective-permute-done.6
  284.9 4.6 %collective-permute-done.5 = f32[273]{0:T(512)S(1)} collective-permute-done((f32[273]{0:T(512)S(1)}, f32[273]{0:T(512)S(1)}, u32[]{:S(2)}, u32[]{:S(2)}) %collective-permute-start.5) | collective-permute-done | bytes 1124 | tf_op jit(solution)/shard_map/ppermute | solution.py:69
  289.5 0.6 slice.35
  290.0 0.6 reshape.56
  (9 shorter events, 0.1 us)
Async XLA Ops:
  12.7 1.5 collective-permute-start
  21.6 112.2 %all-to-all-start = ((bf16[16,88,2176]{2,1,0:T(8,128)(2,1)}), bf16[16,88,2176]{2,1,0:T(8,128)(2,1)}, u32[]{:S(2)}, u32[]{:S(2)}) async-start(bf16[16,88,2176]{2,1,0:T(8,128)(2,1)} %bitcast.32), calls=%async_computation | async-start | bytes 12255232 | tf_op jit(solution)/shard_map/all_to_all | solution.py:29
  29.9 119.4 %all-gather.2.cloned.1.call-start = ((), (), s32[]{:S(2)}) async-start(), calls=%async_computation.2 | async-start | bytes 6893568 | tf_op jit(solution)/shard_map/all_gather | solution.py:26
  30.6 230.6 %reduce-scatter.2.cloned.1.call-start = ((), (), s32[]{:S(2)}) async-start(), calls=%async_computation.3 | async-start | bytes 11837440 | tf_op jit(solution)/shard_map/reduce_scatter | solution.py:36
  133.7 15.6 %collective-permute-start.1 = (bf16[1408,2176]{1,0:T(8,128)(2,1)}, bf16[1408,2176]{1,0:T(8,128)(2,1)}, u32[]{:S(2)}, u32[]{:S(2)}) collective-permute-start(bf16[1408,2176]{1,0:T(8,128)(2,1)} %bitcast.5), channel_id=1, source_target_pairs={{0,8},{8,0},{1,9},{9,1},{2,10},{10,2},{3,11},{11,3},{4,12},{12,4},... | collective-permute-start | bytes 18382856 | tf_op jit(solution)/shard_map/ppermute | solution.py:31
  170.3 0.7 copy-start.1
  170.3 2.5 copy-start
  265.5 5.7 %collective-permute-start.4 = (f32[545]{0:T(1024)S(1)}, f32[545]{0:T(1024)S(1)}, u32[]{:S(2)}, u32[]{:S(2)}) collective-permute-start(f32[545]{0:T(1024)S(1)} %pad_maximum_fusion.1), channel_id=1, source_target_pairs={{0,6},{2,0},{4,2},{6,4},{1,7},{3,1},{5,3},{7,5},{8,14},{10,8},{12,... | collective-permute-start | bytes 6548 | tf_op jit(solution)/shard_map/ppermute | solution.py:51
  268.1 5.1 %collective-permute-start.3 = (f32[545]{0:T(1024)S(1)}, f32[545]{0:T(1024)S(1)}, u32[]{:S(2)}, u32[]{:S(2)}) collective-permute-start(f32[545]{0:T(1024)S(1)} %pad_maximum_fusion.2), channel_id=1, source_target_pairs={{0,4},{2,6},{4,0},{6,2},{1,5},{3,7},{5,1},{7,3},{8,12},{10,14},{12... | collective-permute-start | bytes 6548 | tf_op jit(solution)/shard_map/ppermute | solution.py:51
  269.7 3.6 %collective-permute-start.2 = (f32[545]{0:T(1024)S(1)}, f32[545]{0:T(1024)S(1)}, u32[]{:S(2)}, u32[]{:S(2)}) collective-permute-start(f32[545]{0:T(1024)S(1)} %pad_maximum_fusion.3), channel_id=1, source_target_pairs={{0,2},{2,4},{4,6},{6,0},{1,3},{3,5},{5,7},{7,1},{8,10},{10,12},{12... | collective-permute-start | bytes 6548 | tf_op jit(solution)/shard_map/ppermute | solution.py:51
  277.9 6.9 %collective-permute-start.6 = (f32[273]{0:T(512)S(1)}, f32[273]{0:T(512)S(1)}, u32[]{:S(2)}, u32[]{:S(2)}) collective-permute-start(f32[273]{0:T(512)S(1)} %pad_maximum_fusion.4), channel_id=1, source_target_pairs={{0,4},{1,20},{2,5},{3,21},{4,6},{5,22},{6,7},{7,23},{8,0},{9,16},{... | collective-permute-start | bytes 3284 | tf_op jit(solution)/shard_map/ppermute | solution.py:69
  280.1 9.4 %collective-permute-start.5 = (f32[273]{0:T(512)S(1)}, f32[273]{0:T(512)S(1)}, u32[]{:S(2)}, u32[]{:S(2)}) collective-permute-start(f32[273]{0:T(512)S(1)} %pad_maximum_fusion.5), channel_id=1, source_target_pairs={{0,0},{1,16},{2,1},{3,17},{4,2},{5,18},{6,3},{7,19},{8,4},{9,20},{... | collective-permute-start | bytes 3284 | tf_op jit(solution)/shard_map/ppermute | solution.py:69
Sparse Core Ops, SparseCore 0:
  32.9 116.3 all-gather.1
  170.5 90.7 reduce-scatter.1

commit v14 on v11

--- a/solution.py
+++ b/solution.py
@@ -42,8 +42,8 @@
     part_rows = jnp.sum(summed * summed / denominator, axis=1)
 
     total = jnp.sum(part_rows)
-    pieces = part_rows.reshape(nc, ny // 2, 2, blk)
-    for bit, step, dim in ((y // 2, 2, 1), (y % 2, 1, 1)):
+    pieces = part_rows.reshape(ny // 2, 2, nh, blk)
+    for bit, step, dim in ((y % 2, 1, 1), (y // 2, 2, 0)):
         keep = lax.dynamic_index_in_dim(pieces, bit, dim, keepdims=False)
         give = lax.dynamic_index_in_dim(pieces, 1 - bit, dim, keepdims=False)
         moved = [(k, k ^ step) for k in range(ny)]
@@ -61,7 +61,7 @@
             for cc in range(nc):
                 for yy in range(ny):
                     for hh in range(nh):
-                        x = (cc ^ j) * ny + yy
+                        x = yy * nh + (cc ^ j)
                         moves.append((index(ll, cc, yy, hh), index(hh, ll, x // nh, x % nh)))
         piece = lax.dynamic_index_in_dim(pieces, c ^ j, 0, keepdims=False)
         packed = jnp.concatenate([piece, total[None]])

time: 297 us -> 296 us (level)
  no operation moved by 1% of the time
where the time goes in v14:
time: 296 us; the launch traced here: 293 us
  waiting for transfers between devices  219 us (74%)
  matrix products  21 us (7%)
  between operations  19.3 us (7%)
  starting transfers between devices  14.8 us (5%)
  local copies, waits for them, and re-layouts  14.2 us (5%)
  other arithmetic  5.09 us (2%)
    all_to_all x1, waiting for transfers between devices, body(): left = lax.all_to_all(by_orbital, GROUP, 0, 0, tiled=True)  103 us
    reduce_scatter x1, waiting for transfers between devices, body(): summed = lax.psum_scatter(partial_sum, 'y', scatter_dimension=1, tiled=True)  88.3 us
    dot_general x1, matrix products, body(): lax.dot_general(left, panel, (((0,), (0,)), ((), ())), preferred_element_...  21 us
    all_gather x1, waiting for transfers between devices, body(): panel = lax.all_gather(mine, GROUP, axis=1, tiled=True)  15.5 us
    all_to_all x1, starting transfers between devices, body(): left = lax.all_to_all(by_orbital, GROUP, 0, 0, tiled=True)  8.29 us
    optimization_barrier x1, local copies, waits for them, and re-layouts, body(): mine, integrals = lax.optimization_barrier((mine, integrals))  6.49 us
  transfers between devices with their start and end apart: 9, of which 8 were waited for; matrix products, arithmetic and copies ran while one was open for 0% of the time, Pallas kernels for 0%

profile of v14, /device:TPU:12, one launch (start us, length us, event | category | flops | bytes accessed | tf_op | source)
XLA Modules:
  0.0 293.4 jit_solution(17195594642392491881)
XLA Ops:
  9.1 3.6 %constant_dynamic-slice_fusion.5 = (bf16[88,1,1088]{2,1,0:T(2,128)(2,1)S(1)}, bf16[88,1,1088]{2,1,0:T(2,128)(2,1)S(1)}) fusion(bf16[88,16,2176]{2,1,0:T(8,128)(2,1)} %param.4, s32[]{:T(128)S(6)} %select_n.57, s32[]{:T(128)S(6)} %select_n.59, s32[]{:T(128)S(6)} %select_n.61), kind=kLoop, calls=%fused_computation.23 | loop fusion | bytes 765964 | tf_op jit(solution)/shard_map/dynamic_slice | solution.py:21
  12.7 0.1 collective-permute-start
  12.8 1.4 collective-permute-done
  14.3 0.8 pad_maximum_fusion
  15.1 6.5 %copy.14 = bf16[88,16,2176]{2,0,1:T(8,128)(2,1)} copy(bf16[88,16,2176]{2,1,0:T(8,128)(2,1)} %param.4) | data formatting | bytes 12255232 | tf_op jit(solution)/shard_map/optimization_barrier | solution.py:24
  21.6 8.3 %all-to-all-start = ((bf16[16,88,2176]{2,1,0:T(8,128)(2,1)}), bf16[16,88,2176]{2,1,0:T(8,128)(2,1)}, u32[]{:S(2)}, u32[]{:S(2)}) async-start(bf16[16,88,2176]{2,1,0:T(8,128)(2,1)} %bitcast.29), calls=%async_computation | async-start | bytes 12255232 | tf_op jit(solution)/shard_map/all_to_all | solution.py:29
  29.9 0.0 all-gather.2.cloned.1.call-start
  29.9 0.7 all-gather.2.cloned.1.call-update
  30.6 0.0 reduce-scatter.2.cloned.1.call-start
  30.6 103.1 %all-to-all-done = bf16[16,88,2176]{2,1,0:T(8,128)(2,1)} async-done(((bf16[16,88,2176]{2,1,0:T(8,128)(2,1)}), bf16[16,88,2176]{2,1,0:T(8,128)(2,1)}, u32[]{:S(2)}, u32[]{:S(2)}) %all-to-all-start) | async-done | bytes 6127648 | tf_op jit(solution)/shard_map/all_to_all | solution.py:29
  133.7 0.0 collective-permute-start.1
  133.7 15.5 %all-gather.2.cloned.1.call-done = bf16[2,1408,1088]{2,1,0:T(8,128)(2,1)} async-done(((bf16[2,88,1088]{2,1,0:T(8,128)(2,1)}), bf16[2,1408,1088]{2,1,0:T(8,128)(2,1)}) %all-gather.2.cloned.1.call-update) | async-done | bytes 6127632 | tf_op jit(solution)/shard_map/all_gather | solution.py:26
  149.3 0.0 collective-permute-done.1
  149.3 21.0 %fusion = f32[2176,1088]{0,1:T(8,128)} fusion(bf16[2816,1088]{1,0:T(8,128)(2,1)} %bitcast.39, bf16[1408,2176]{1,0:T(8,128)(2,1)} %collective-permute-done.1, bf16[1408,2176]{1,0:T(8,128)(2,1)} %bitcast.5), kind=kOutput, calls=%fused_computation | convolution fusion | flops 13358202880 | bytes 27852800 | tf_op jit(solution)/shard_map/dot_general | solution.py:33
  170.2 0.0 copy-start.1
  170.2 0.0 copy-start
  170.2 0.0 reduce-scatter.2.cloned.1.call-update
  170.3 0.6 copy-done.1
  170.9 0.6 fusion.9
  172.8 0.0 copy-done
  172.8 0.1 dynamic_slice.46
  172.9 88.3 %reduce-scatter.2.cloned.1.call-done = f32[2176,272]{0,1:T(8,128)} async-done(((f32[2176,1088]{0,1:T(8,128)}), f32[2176,272]{0,1:T(8,128)}) %reduce-scatter.2.cloned.1.call-update) | async-done | bytes 2367504 | tf_op jit(solution)/shard_map/reduce_scatter | solution.py:36
  261.2 3.3 %fusion.5 = (f32[2176]{0:T(1024)S(1)}, f32[]{:T(128)}) fusion(f32[272]{0:T(512)S(1)} %dynamic_slice.46, f32[2176]{0:T(1024)S(1)} %broadcast_subtract_fusion, f32[2176,272]{0,1:T(8,128)} %reduce-scatter.2.cloned.1.call-done), kind=kLoop, calls=%fused_computation.10 | loop fusion | flops 2957183 | bytes 2385988 | tf_op jit(solution)/shard_map/reduce_sum | solution.py:42
  264.5 0.1 reshape.42
  264.6 0.1 reshape.43
  264.6 0.7 pad_maximum_fusion.1
  265.4 1.8 collective-permute-start.2
  267.2 1.9 collective-permute-done.2
  269.0 0.1 reshape.44
  269.2 0.1 reshape.45
  269.2 0.6 slice.29
  271.1 0.1 pad_maximum_fusion.2
  271.2 1.5 collective-permute-start.3
  272.7 3.7 %collective-permute-done.3 = f32[545]{0:T(1024)S(1)} collective-permute-done((f32[545]{0:T(1024)S(1)}, f32[545]{0:T(1024)S(1)}, u32[]{:S(2)}, u32[]{:S(2)}) %collective-permute-start.3) | collective-permute-done | bytes 2212 | tf_op jit(solution)/shard_map/ppermute | solution.py:50
  276.3 0.1 reshape.46
  276.4 0.6 slice.25
  277.7 0.1 pad_maximum_fusion.3
  277.8 1.2 collective-permute-start.5
  278.9 0.1 pad_maximum_fusion.4
  279.0 1.9 collective-permute-start.4
  280.9 1.9 collective-permute-done.5
  282.9 2.5 collective-permute-done.4
  285.4 0.6 slice.27
  286.0 0.6 reshape.47
  (9 shorter events, 0.1 us)
Async XLA Ops:
  12.7 1.5 collective-permute-start
  21.6 112.2 %all-to-all-start = ((bf16[16,88,2176]{2,1,0:T(8,128)(2,1)}), bf16[16,88,2176]{2,1,0:T(8,128)(2,1)}, u32[]{:S(2)}, u32[]{:S(2)}) async-start(bf16[16,88,2176]{2,1,0:T(8,128)(2,1)} %bitcast.29), calls=%async_computation | async-start | bytes 12255232 | tf_op jit(solution)/shard_map/all_to_all | solution.py:29
  29.9 119.4 %all-gather.2.cloned.1.call-start = ((), (), s32[]{:S(2)}) async-start(), calls=%async_computation.2 | async-start | bytes 6893568 | tf_op jit(solution)/shard_map/all_gather | solution.py:26
  30.6 230.6 %reduce-scatter.2.cloned.1.call-start = ((), (), s32[]{:S(2)}) async-start(), calls=%async_computation.3 | async-start | bytes 11837440 | tf_op jit(solution)/shard_map/reduce_scatter | solution.py:36
  133.7 15.6 %collective-permute-start.1 = (bf16[1408,2176]{1,0:T(8,128)(2,1)}, bf16[1408,2176]{1,0:T(8,128)(2,1)}, u32[]{:S(2)}, u32[]{:S(2)}) collective-permute-start(bf16[1408,2176]{1,0:T(8,128)(2,1)} %bitcast.5), channel_id=1, source_target_pairs={{0,8},{8,0},{1,9},{9,1},{2,10},{10,2},{3,11},{11,3},{4,12},{12,4},... | collective-permute-start | bytes 18382856 | tf_op jit(solution)/shard_map/ppermute | solution.py:31
  170.2 0.7 copy-start.1
  170.2 2.5 copy-start
  265.4 3.7 %collective-permute-start.2 = (f32[1089]{0:T(1024)S(1)}, f32[1089]{0:T(1024)S(1)}, u32[]{:S(2)}, u32[]{:S(2)}) collective-permute-start(f32[1089]{0:T(1024)S(1)} %pad_maximum_fusion.1), channel_id=1, source_target_pairs={{0,2},{2,0},{4,6},{6,4},{1,3},{3,1},{5,7},{7,5},{8,10},{10,8},{12,... | collective-permute-start | bytes 13076 | tf_op jit(solution)/shard_map/ppermute | solution.py:50
  271.2 5.1 %collective-permute-start.3 = (f32[545]{0:T(1024)S(1)}, f32[545]{0:T(1024)S(1)}, u32[]{:S(2)}, u32[]{:S(2)}) collective-permute-start(f32[545]{0:T(1024)S(1)} %pad_maximum_fusion.2), channel_id=1, source_target_pairs={{0,4},{2,6},{4,0},{6,2},{1,5},{3,7},{5,1},{7,3},{8,12},{10,14},{12... | collective-permute-start | bytes 6548 | tf_op jit(solution)/shard_map/ppermute | solution.py:50
  277.8 5.1 %collective-permute-start.5 = (f32[273]{0:T(512)S(1)}, f32[273]{0:T(512)S(1)}, u32[]{:S(2)}, u32[]{:S(2)}) collective-permute-start(f32[273]{0:T(512)S(1)} %pad_maximum_fusion.3), channel_id=1, source_target_pairs={{0,1},{1,17},{2,3},{3,19},{4,5},{5,21},{6,7},{7,23},{8,0},{9,16},{... | collective-permute-start | bytes 3284 | tf_op jit(solution)/shard_map/ppermute | solution.py:68
  279.0 6.4 %collective-permute-start.4 = (f32[273]{0:T(512)S(1)}, f32[273]{0:T(512)S(1)}, u32[]{:S(2)}, u32[]{:S(2)}) collective-permute-start(f32[273]{0:T(512)S(1)} %pad_maximum_fusion.4), channel_id=1, source_target_pairs={{0,0},{1,16},{2,2},{3,18},{4,4},{5,20},{6,6},{7,22},{8,1},{9,17},{... | collective-permute-start | bytes 3284 | tf_op jit(solution)/shard_map/ppermute | solution.py:68
Sparse Core Ops, SparseCore 0:
  32.8 116.3 all-gather.1
  170.4 90.7 reduce-scatter.1
